TPU v7x, 128 devices: a whole 4x4x4 slice. The times are simulated.
128 devices in a mesh: grp: 2 (over core), fsdp: 64 (over x, y, z).
Axes of the slice: x: 4, y: 4, z: 4, core: 2. Of those that a mesh axis runs over, the one named last changes fastest.
Arguments:
- item_states: bfloat16 [512, 256, 2048], P(('grp', 'fsdp')), may hold values from -6 to 6
- w_query: bfloat16 [2048, 2048], P('fsdp'), may hold values from -0.125 to 0.125
- w_key: bfloat16 [2048, 256], P('fsdp'), may hold values from -0.125 to 0.125
- w_value: bfloat16 [2048, 256], P('fsdp'), may hold values from -0.125 to 0.125
- item_gain: float32 [2048], replicated, may hold values from 0.25 to 1.75
- w_adapt: bfloat16 [2048, 4096], P('fsdp'), may hold values from -0.125 to 0.125
- user_gain: float32 [4096], replicated, may hold values from 0.25 to 1.75
- user_query: bfloat16 [4096, 128], P('fsdp'), may hold values from -0.5 to 0.5
- hist_owner: int32 [128, 128, 1], P(('grp', 'fsdp')), may hold values from 0 to 127; in each aligned block of 128 rows (0 to 127, 128 to 255, ..., all dimensions but the last counted through in order) at most 2 rows name the same one
- history_position_index: int32 [128, 128], P(('grp', 'fsdp')), may hold values from 0 to 3
- cotangent: bfloat16 [128, 128, 4096], P(('grp', 'fsdp')), may hold values from -6 to 6
Outputs:
- item_embed: bfloat16 [512, 2048], P(('grp', 'fsdp'))
- user_attention_output: bfloat16 [128, 128, 4096], P(('grp', 'fsdp'))
- item_grad: float32 [512, 2048], P(('grp', 'fsdp'))
Inputs may be any that keep to these rules, and one draw needn't show every extreme that they name: `hist_owner`: within one history no device is named by more than 2 positions, and some device is named by exactly 2 positions.
All inputs are finite; a program needn't handle non-finite values.
Results may differ from a plain program's by a relative error of at most 0.011.
Values may be sent and summed in bfloat16 or wider, within the bound.
No kernel may reach another device: no remote copies, remote signals or barrier semaphores. Data moves between devices by JAX's collectives and lax.ppermute only.
A program may use at most 128 MiB of HBM per device.

v0:
```python
import jax
import jax.numpy as jnp
from jax import lax
from jax.sharding import PartitionSpec as P

DI = 2048
IHEADS = 32
IHD = 64
IKV = 4
UHEADS = 32
UHD = 128
ILEN = 256


def stored(values):
    return lax.optimization_barrier(values.astype(jnp.bfloat16))


def rms_scale(values, gain):
    mean_sq = jnp.mean(values * values, axis=-1, keepdims=True)
    return values * lax.rsqrt(mean_sq + 1e-05) * gain


def item_pool(states, key_rows, value_rows, query_rows, item_gain):
    count = states.shape[0]
    group = IHEADS // IKV
    query_heads = query_rows.reshape(count, IKV, group, IHD).astype(jnp.float32)
    key_heads = key_rows.reshape(count, ILEN, IKV, IHD).astype(jnp.float32)
    value_heads = value_rows.reshape(count, ILEN, IKV, IHD).astype(jnp.float32)
    scores = jnp.einsum("igrd,itgd->igrt", query_heads, key_heads) * IHD ** (-0.5)
    weights = stored(jax.nn.softmax(scores, axis=-1)).astype(jnp.float32)
    mixed = jnp.einsum("igrt,itgd->igrd", weights, value_heads).reshape(count, IHEADS * IHD)
    last_row = states[:, ILEN - 1, :].astype(jnp.float32)
    return rms_scale(last_row + mixed, item_gain).astype(jnp.bfloat16)


def user_layer(hidden, user_gain, user_query):
    length_total = hidden.shape[0]
    normed = stored(rms_scale(hidden.astype(jnp.float32), user_gain)).astype(jnp.float32)
    heads = normed.reshape(length_total, UHEADS, UHD)
    query_map = user_query.reshape(UHEADS, UHD, UHD).astype(jnp.float32)
    queries = stored(jnp.einsum("thd,hde->the", heads, query_map)).astype(jnp.float32)
    scores = jnp.einsum("the,she->hts", queries, heads) * UHD ** (-0.5)
    target = jnp.arange(length_total, dtype=jnp.int32)
    causal = target[None, :, None] >= target[None, None, :]
    scores = jnp.where(causal, scores, -1e30)
    weights = stored(jax.nn.softmax(scores, axis=-1)).astype(jnp.float32)
    mixed = jnp.einsum("hts,shd->thd", weights, heads).reshape(length_total, UHEADS * UHD)
    return (hidden.astype(jnp.float32) + mixed).astype(jnp.bfloat16)


def serve_rows(requests, lookup_matrix):
    chosen_items = (
        requests[..., None] == jnp.arange(lookup_matrix.shape[0], dtype=jnp.int32)
    ).astype(lookup_matrix.dtype)
    return jnp.einsum(
        "ltj,jy->lty", chosen_items, lookup_matrix, preferred_element_type=jnp.float32
    ).astype(lookup_matrix.dtype)


def per_device(
    item_states,
    w_query,
    w_key,
    w_value,
    item_gain,
    w_adapt,
    user_gain,
    user_query,
    hist_owner,
    history_position_index,
    cotangent,
):
    groups = lax.axis_size("grp")
    shards = lax.axis_size("fsdp")
    devices = groups * shards
    count = item_states.shape[0]
    flat = item_states.reshape(count * ILEN, DI)
    last_row = item_states[:, ILEN - 1, :]
    columns = flat
    key_sum = jnp.dot(
        columns,
        lax.all_gather(w_key, "fsdp", axis=0, tiled=True),
        preferred_element_type=jnp.float32,
    )
    summed_value = jnp.dot(
        columns,
        lax.all_gather(w_value, "fsdp", axis=0, tiled=True),
        preferred_element_type=jnp.float32,
    )
    columns = last_row
    query_sum = jnp.dot(
        columns,
        lax.all_gather(w_query, "fsdp", axis=0, tiled=True),
        preferred_element_type=jnp.float32,
    )
    adapter, query_map = (
        lax.all_gather(w_adapt, "fsdp", axis=0, tiled=True),
        lax.all_gather(user_query, "fsdp", axis=0, tiled=True),
    )
    item_embed = item_pool(
        item_states, stored(key_sum), stored(summed_value), stored(query_sum), item_gain
    )
    length_total = history_position_index.shape[1]
    cap_slots = max(2, 2 * length_total // devices)
    owner_users = hist_owner[0, :, 0]
    owner_hot = (owner_users[:, None] == jnp.arange(devices, dtype=jnp.int32)[None, :]).astype(
        jnp.int32
    )
    earlier = jnp.cumsum(owner_hot, axis=0) - owner_hot
    rank_in = jnp.sum(owner_hot * earlier, axis=1)
    position = owner_users * cap_slots + rank_in
    request = (
        jnp.full((devices * cap_slots,), count, jnp.int32)
        .at[position]
        .set(history_position_index[0])
    )
    request = request.reshape(devices, cap_slots)
    width = item_embed.shape[1]
    incoming = lax.all_to_all(request, ("grp", "fsdp"), split_axis=0, concat_axis=0, tiled=True)
    found = serve_rows(incoming, item_embed)
    returned = lax.all_to_all(found, ("grp", "fsdp"), split_axis=0, concat_axis=0, tiled=True)
    fetched = jnp.take(returned.reshape(devices * cap_slots, width), position, axis=0)
    hidden = stored(jnp.dot(fetched, adapter, preferred_element_type=jnp.float32))
    user_attention_output, pull = jax.vjp(
        lambda values: user_layer(values, user_gain, query_map), hidden
    )
    (grad_hidden,) = pull(cotangent[0])
    grad_rows = jnp.dot(grad_hidden, adapter.T, preferred_element_type=jnp.float32)
    outgoing = jnp.zeros((devices * cap_slots, DI), jnp.float32).at[position].set(grad_rows)
    arrived = lax.all_to_all(
        outgoing.reshape(devices, cap_slots, DI).astype(jnp.bfloat16),
        ("grp", "fsdp"),
        split_axis=0,
        concat_axis=0,
        tiled=True,
    ).astype(jnp.float32)
    terms = arrived.reshape(devices * cap_slots, DI)
    slot_hot = (
        incoming.reshape(-1)[:, None] == jnp.arange(count, dtype=jnp.int32)[None, :]
    ).astype(jnp.float32)
    item_grad = jnp.dot(slot_hot.T, terms, precision=lax.Precision.HIGHEST)
    return (item_embed, user_attention_output[None], item_grad)


def solution(mesh):
    placed = (
        P(("grp", "fsdp"), None, None),
        P("fsdp", None),
        P("fsdp", None),
        P("fsdp", None),
        P(),
        P("fsdp", None),
        P(),
        P("fsdp", None),
        P(("grp", "fsdp"), None, None),
        P(("grp", "fsdp"), None),
        P(("grp", "fsdp"), None, None),
    )
    return jax.shard_map(
        per_device,
        mesh=mesh,
        in_specs=placed,
        out_specs=(
            P(("grp", "fsdp"), None),
            P(("grp", "fsdp"), None, None),
            P(("grp", "fsdp"), None),
        ),
        check_vma=False,
    )
```

profile of v0, /device:TPU:1, one launch (start us, length us, event | category | flops | bytes accessed | tf_op | source)
XLA Modules:
  0.0 473.3 jit_solution(699172735839082642)
XLA Ops:
  7.2 0.7 all-gather.8.cloned.1.call-update
  7.9 0.7 all-gather.10.cloned.1.call-update
  8.7 0.7 all-gather.6.cloned.1.call-update
  9.4 0.5 all-gather.12.cloned.1.call-update
  10.0 0.7 fusion.54
  10.9 0.8 select_reduce_fusion
  11.7 0.7 fusion.58
  12.4 1.1 scatter_custom_fusion
  13.5 0.8 all_to_all.12
  14.3 11.5 %all-to-all-start = ((s32[128,1,2]{2,1,0:T(1,128)}), s32[128,1,2]{2,1,0:T(1,128)S(1)}, u32[]{:S(2)}, u32[]{:S(2)}) async-start(s32[128,1,2]{2,1,0:T(1,128)} %bitcast.7), calls=%async_computation | async-start | bytes 131072 | tf_op jit(solution)/shard_map/all_to_all | solution.py:120
  25.8 0.9 slice.4
  26.8 8.2 %all-to-all-done = s32[128,1,2]{2,1,0:T(1,128)S(1)} async-done(((s32[128,1,2]{2,1,0:T(1,128)}), s32[128,1,2]{2,1,0:T(1,128)S(1)}, u32[]{:S(2)}, u32[]{:S(2)}) %all-to-all-start) | async-done | bytes 1056 | tf_op jit(solution)/shard_map/all_to_all | solution.py:120
  35.1 41.2 %all-gather.8.cloned.1.call-done = bf16[2048,256]{1,0:T(8,128)(2,1)} async-done(((bf16[32,256]{1,0:T(8,128)(2,1)}), bf16[2048,256]{1,0:T(8,128)(2,1)}) %all-gather.8.cloned.1.call-update) | async-done | bytes 1048592 | tf_op jit(solution)/shard_map/all_gather | solution.py:83
  76.3 3.7 convolution_convert_fusion.7
  80.4 60.2 %all-gather.10.cloned.1.call-done = bf16[2048,256]{1,0:T(8,128)(2,1)} async-done(((bf16[32,256]{1,0:T(8,128)(2,1)}), bf16[2048,256]{1,0:T(8,128)(2,1)}) %all-gather.10.cloned.1.call-update) | async-done | bytes 1048592 | tf_op jit(solution)/shard_map/all_gather | solution.py:88
  140.7 3.7 convolution_convert_fusion.6
  144.8 76.3 %all-gather.6.cloned.1.call-done = bf16[2048,2048]{1,0:T(8,128)(2,1)} async-done(((bf16[32,2048]{1,0:T(8,128)(2,1)}), bf16[2048,2048]{1,0:T(8,128)(2,1)}) %all-gather.6.cloned.1.call-update) | async-done | bytes 8388624 | tf_op jit(solution)/shard_map/all_gather | solution.py:94
  221.1 4.6 convolution_convert_fusion.2
  225.8 0.6 fusion.75
  227.0 0.5 convolution_convert_fusion.1
  227.5 2.0 copy.53
  229.5 8.0 %all-to-all-start.1 = ((bf16[128,2,2048]{2,1,0:T(2,128)(2,1)}), bf16[128,2,2048]{2,1,0:T(2,128)(2,1)S(1)}, u32[]{:S(2)}, u32[]{:S(2)}) async-start(bf16[128,2,2048]{2,1,0:T(2,128)(2,1)} %copy.53), calls=%async_computation.1 | async-start | bytes 2097152 | tf_op jit(solution)/shard_map/all_to_all | solution.py:122
  238.2 0.7 copy.79
  238.9 17.7 %all-to-all-done.1 = bf16[128,2,2048]{2,1,0:T(2,128)(2,1)S(1)} async-done(((bf16[128,2,2048]{2,1,0:T(2,128)(2,1)}), bf16[128,2,2048]{2,1,0:T(2,128)(2,1)S(1)}, u32[]{:S(2)}, u32[]{:S(2)}) %all-to-all-start.1) | async-done | bytes 1048608 | tf_op jit(solution)/shard_map/all_to_all | solution.py:122
  257.1 0.9 gather_fusion
  258.0 78.2 %all-gather.12.cloned.1.call-done = bf16[2048,4096]{1,0:T(8,128)(2,1)} async-done(((bf16[32,4096]{1,0:T(8,128)(2,1)}), bf16[2048,4096]{1,0:T(8,128)(2,1)}) %all-gather.12.cloned.1.call-update) | async-done | bytes 16777232 | tf_op jit(solution)/shard_map/all_gather | solution.py:98
  336.2 8.2 %convolution_convert_fusion = bf16[128,4096]{1,0:T(8,128)(2,1)S(1)} fusion(bf16[2048,4096]{1,0:T(8,128)(2,1)} %all-gather.12.cloned.1.call-done, bf16[128,2048]{1,0:T(8,128)(2,1)S(1)} %gather_fusion, pred[128]{0:T(512)(128)(4,1)S(1)} %compare_and_fusion), kind=kOutput, calls=%fused_computation.5 | convolution fusion | flops 2148270080 | bytes 18350208 | tf_op jit(solution)/shard_map/dot_general | solution.py:124
  345.0 55.9 %all-gather.14.cloned.1.call-done = bf16[4096,128]{1,0:T(8,128)(2,1)} async-done(((bf16[64,128]{1,0:T(8,128)(2,1)}), bf16[4096,128]{1,0:T(8,128)(2,1)}) %all-gather.14.cloned.1.call-update) | async-done | bytes 1048592 | tf_op jit(solution)/shard_map/all_gather | solution.py:99
  400.9 2.6 fusion.15
  403.5 1.4 fusion.16
  404.9 3.5 fusion.76
  408.5 2.6 fusion.7
  411.6 0.8 fusion.73
  412.4 0.8 fusion.17
  413.2 0.9 fusion.81
  414.1 1.9 fusion.29
  416.0 0.9 add_convert_fusion
  416.9 0.5 copy.80
  417.4 2.9 copy.78
  420.3 3.1 fusion.13
  423.4 12.5 %fusion.22 = f32[128,2048]{1,0:T(8,128)} fusion(bf16[2048,4096]{1,0:T(8,128)(2,1)} %all-gather.12.cloned.1.call-done, bf16[128,4096]{1,0:T(8,128)(2,1)S(1)} %convolution_convert_fusion, bf16[128,4096]{1,0:T(8,128)(2,1)S(1)} %copy.80, bf16[1,128,4096]{2,1,0:T(8,128)(2,1)S(1)} %copy-done.2, f32[128]{0:T(128)S(1)} %multiply_multiply_fusion, ...), kind=kOutput, calls=%fused_computation.47 | convolution fusion | flops 2152202240 | bytes 20988928 | tf_op jit(solution)/shard_map/dot_general | solution.py:129
  435.9 2.4 scatter_custom_fusion.1
  438.5 1.5 convert_element_type.130
  440.0 7.6 %all-to-all-start.2 = ((bf16[128,2,2048]{2,1,0:T(2,128)(2,1)}), bf16[128,2,2048]{2,1,0:T(2,128)(2,1)S(1)}, u32[]{:S(2)}, u32[]{:S(2)}) async-start(bf16[128,2,2048]{2,1,0:T(2,128)(2,1)} %convert_element_type.130), calls=%async_computation.2 | async-start | bytes 2097152 | tf_op jit(solution)/shard_map/all_to_all | solution.py:131
  447.6 0.5 broadcast.136
  448.1 0.8 reduce.4
  449.0 16.4 %all-to-all-done.2 = bf16[128,2,2048]{2,1,0:T(2,128)(2,1)S(1)} async-done(((bf16[128,2,2048]{2,1,0:T(2,128)(2,1)}), bf16[128,2,2048]{2,1,0:T(2,128)(2,1)S(1)}, u32[]{:S(2)}, u32[]{:S(2)}) %all-to-all-start.2) | async-done | bytes 1048608 | tf_op jit(solution)/shard_map/all_to_all | solution.py:131
  465.8 1.0 fusion.52
  (51 shorter events, 4.9 us)
Async XLA Ops:
  7.2 69.1 %all-gather.8.cloned.1.call-start = ((), (), s32[]{:S(2)}) async-start(), calls=%async_computation.4 | async-start | bytes 1064960 | tf_op jit(solution)/shard_map/all_gather | solution.py:83
  7.9 132.8 %all-gather.10.cloned.1.call-start = ((), (), s32[]{:S(2)}) async-start(), calls=%async_computation.5 | async-start | bytes 1064960 | tf_op jit(solution)/shard_map/all_gather | solution.py:88
  8.6 212.4 %all-gather.6.cloned.1.call-start = ((), (), s32[]{:S(2)}) async-start(), calls=%async_computation.3 | async-start | bytes 8519680 | tf_op jit(solution)/shard_map/all_gather | solution.py:94
  9.4 326.8 %all-gather.12.cloned.1.call-start = ((), (), s32[]{:S(2)}) async-start(), calls=%async_computation.6 | async-start | bytes 17039360 | tf_op jit(solution)/shard_map/all_gather | solution.py:98
  14.3 20.8 %all-to-all-start = ((s32[128,1,2]{2,1,0:T(1,128)}), s32[128,1,2]{2,1,0:T(1,128)S(1)}, u32[]{:S(2)}, u32[]{:S(2)}) async-start(s32[128,1,2]{2,1,0:T(1,128)} %bitcast.7), calls=%async_computation | async-start | bytes 131072 | tf_op jit(solution)/shard_map/all_to_all | solution.py:120
  225.7 1.2 copy-start.8
  227.0 2.6 copy-start.7
  227.5 10.7 %copy-start.1 = (bf16[1,128,4096]{2,1,0:T(8,128)(2,1)S(1)}, bf16[1,128,4096]{2,1,0:T(8,128)(2,1)}, u32[]{:S(2)}) copy-start(bf16[1,128,4096]{2,1,0:T(8,128)(2,1)} %param.21) | copy-start | bytes 3145732
  229.5 9.3 %copy-start.9 = (s32[1,128,1]{1,2,0:T(1,128)S(1)}, s32[1,128,1]{1,2,0:T(1,128)}, u32[]{:S(2)}) copy-start(s32[1,128,1]{1,2,0:T(1,128)} %param.19) | copy-start | bytes 1540
  229.5 27.1 %all-to-all-start.1 = ((bf16[128,2,2048]{2,1,0:T(2,128)(2,1)}), bf16[128,2,2048]{2,1,0:T(2,128)(2,1)S(1)}, u32[]{:S(2)}, u32[]{:S(2)}) async-start(bf16[128,2,2048]{2,1,0:T(2,128)(2,1)} %copy.53), calls=%async_computation.1 | async-start | bytes 2097152 | tf_op jit(solution)/shard_map/all_to_all | solution.py:122
  237.6 163.3 %all-gather.14.cloned.1.call-start = ((), (), s32[]{:S(2)}) async-start(), calls=%async_computation.7 | async-start | bytes 1064960 | tf_op jit(solution)/shard_map/all_gather | solution.py:99
  258.0 86.7 %copy-start.6 = (f32[4096]{0:T(1024)S(1)}, f32[4096]{0:T(1024)}, u32[]{:S(2)}) copy-start(f32[4096]{0:T(1024)} %param.17) | copy-start | bytes 49156
  408.5 2.6 copy-start.3
  408.5 2.9 copy-start.4
  408.5 3.1 copy-start.5
  414.1 1.9 copy-start
  420.3 3.1 copy-start.2
  440.0 25.4 %all-to-all-start.2 = ((bf16[128,2,2048]{2,1,0:T(2,128)(2,1)}), bf16[128,2,2048]{2,1,0:T(2,128)(2,1)S(1)}, u32[]{:S(2)}, u32[]{:S(2)}) async-start(bf16[128,2,2048]{2,1,0:T(2,128)(2,1)} %convert_element_type.130), calls=%async_computation.2 | async-start | bytes 2097152 | tf_op jit(solution)/shard_map/all_to_all | solution.py:131
Sparse Core Ops, SparseCore 0:
  10.9 65.3 all-gather.7
  79.2 61.4 all-gather.9
  143.6 77.4 all-gather.5
  223.8 112.3 all-gather.11
  339.0 61.9 all-gather.13
where the time goes:
time: 474 us; the launch traced here: 473 us
  waiting for transfers between devices  357 us (75%)
  matrix products  47.8 us (10%)
  starting transfers between devices  27.4 us (6%)
  local copies, waits for them, and re-layouts  17 us (4%)
  between operations  14.1 us (3%)
  other arithmetic  9.93 us (2%)
    all_gather x1, waiting for transfers between devices, per_device(): lax.all_gather(w_adapt, 'fsdp', axis=0, tiled=True)  78.2 us
    all_gather x1, waiting for transfers between devices, per_device(): lax.all_gather(w_query, 'fsdp', axis=0, tiled=True)  76.3 us
    all_gather x1, waiting for transfers between devices, per_device(): lax.all_gather(w_value, 'fsdp', axis=0, tiled=True)  60.2 us
    all_gather x1, waiting for transfers between devices, per_device(): lax.all_gather(user_query, 'fsdp', axis=0, tiled=True)  55.9 us
    all_gather x1, waiting for transfers between devices, per_device(): lax.all_gather(w_key, 'fsdp', axis=0, tiled=True)  41.2 us
    all_to_all x1, waiting for transfers between devices, per_device(): lax.all_to_all(found, ('grp', 'fsdp'), split_axis=0, concat_axis=0, tiled...  17.7 us
    all_to_all x1, waiting for transfers between devices, per_device(): lax.all_to_all(outgoing.reshape(devices, cap_slots, DI).astype(jnp.bfloat...  16.4 us
    dot_general x1, matrix products, per_device(): jnp.dot(grad_hidden, adapter.T, preferred_element_type=jnp.float32)  12.5 us
  transfers between devices with their start and end apart: 8, of which 8 were waited for; matrix products, arithmetic and copies ran while one was open for 7% of the time, Pallas kernels for 0%

commit v1 on v0

--- a/solution.py
+++ b/solution.py
@@ -77,27 +77,21 @@
     count = item_states.shape[0]
     flat = item_states.reshape(count * ILEN, DI)
     last_row = item_states[:, ILEN - 1, :]
-    columns = flat
-    key_sum = jnp.dot(
-        columns,
-        lax.all_gather(w_key, "fsdp", axis=0, tiled=True),
-        preferred_element_type=jnp.float32,
+    packed = jnp.concatenate(
+        [w_key, w_value, w_query, w_adapt, user_query.reshape(w_key.shape[0], -1)], axis=1
     )
-    summed_value = jnp.dot(
-        columns,
-        lax.all_gather(w_value, "fsdp", axis=0, tiled=True),
-        preferred_element_type=jnp.float32,
+    gathered = lax.all_gather(packed, "fsdp", axis=0, tiled=True)
+    kv_cols = w_key.shape[1] + w_value.shape[1]
+    q_end = kv_cols + w_query.shape[1]
+    a_end = q_end + w_adapt.shape[1]
+    kv_sum = jnp.dot(flat, gathered[:, :kv_cols], preferred_element_type=jnp.float32)
+    key_sum = kv_sum[:, : w_key.shape[1]]
+    summed_value = kv_sum[:, w_key.shape[1] :]
+    query_sum = jnp.dot(
+        last_row, gathered[:, kv_cols:q_end], preferred_element_type=jnp.float32
     )
-    columns = last_row
-    query_sum = jnp.dot(
-        columns,
-        lax.all_gather(w_query, "fsdp", axis=0, tiled=True),
-        preferred_element_type=jnp.float32,
-    )
-    adapter, query_map = (
-        lax.all_gather(w_adapt, "fsdp", axis=0, tiled=True),
-        lax.all_gather(user_query, "fsdp", axis=0, tiled=True),
-    )
+    adapter = gathered[:, q_end:a_end]
+    query_map = gathered[:, a_end:].reshape(-1, user_query.shape[1])
     item_embed = item_pool(
         item_states, stored(key_sum), stored(summed_value), stored(query_sum), item_gain
     )

time: 474 us -> 280 us (0.59)
  waiting for transfers between devices: 357 us -> 161 us
  local copies, waits for them, and re-layouts: 17 us -> 25 us
  matrix products: 47.8 us -> 42.8 us
    all_gather x5 -> x1, waiting for transfers between devices: 312 us -> 120 us  [per_device(): gathered = lax.all_gather(packed, 'fsdp', axis=0, tiled=True)]
    dot_general x3 -> x2, matrix products: 12 us -> 9.79 us  [the longest x1 5.22 us: per_device(): jnp.dot(flat, gathered[:, :kv_cols], preferred_element_type=jnp.float32)]
  transfers between devices with their start and end apart: 8 -> 4, of which waited for: 8 -> 4; matrix products, arithmetic and copies ran while one was open for 7% -> 3% of each run, Pallas kernels for 0% -> 0%
where the time goes in v1:
time: 280 us; the launch traced here: 279 us
  waiting for transfers between devices  161 us (58%)
  matrix products  42.8 us (15%)
  starting transfers between devices  25.5 us (9%)
  local copies, waits for them, and re-layouts  25 us (9%)
  between operations  14.4 us (5%)
  other arithmetic  10.3 us (4%)
    all_gather x1, waiting for transfers between devices, per_device(): gathered = lax.all_gather(packed, 'fsdp', axis=0, tiled=True)  120 us
    all_to_all x1, waiting for transfers between devices, per_device(): lax.all_to_all(outgoing.reshape(devices, cap_slots, DI).astype(jnp.bfloat...  16.4 us
    all_to_all x1, waiting for transfers between devices, per_device(): lax.all_to_all(found, ('grp', 'fsdp'), split_axis=0, concat_axis=0, tiled...  15.8 us
    all_to_all x1, starting transfers between devices, per_device(): lax.all_to_all(request, ('grp', 'fsdp'), split_axis=0, concat_axis=0, til...  11.5 us
    dot_general x1, matrix products, per_device(): jnp.dot(grad_hidden, adapter.T, preferred_element_type=jnp.float32)  10.4 us
    all_to_all x1, waiting for transfers between devices, per_device(): lax.all_to_all(request, ('grp', 'fsdp'), split_axis=0, concat_axis=0, til...  8.54 us
    all_to_all x1, starting transfers between devices, per_device(): lax.all_to_all(found, ('grp', 'fsdp'), split_axis=0, concat_axis=0, tiled...  8.49 us
    dot_general x1, matrix products, per_device(): jnp.dot(fetched, adapter, preferred_element_type=jnp.float32)  8.37 us
  transfers between devices with their start and end apart: 4, of which 4 were waited for; matrix products, arithmetic and copies ran while one was open for 3% of the time, Pallas kernels for 0%

profile of v1, /device:TPU:1, one launch (start us, length us, event | category | flops | bytes accessed | tf_op | source)
XLA Modules:
  0.0 279.0 jit_solution(11355290367567312266)
XLA Ops:
  7.2 0.7 constant_dynamic-update-slice_fusion.4
  7.9 0.7 reshape.146
  8.7 0.7 constant_dynamic-update-slice_fusion.3
  9.4 0.9 constant_dynamic-update-slice_fusion.2
  10.3 1.0 constant_dynamic-update-slice_fusion.1
  11.3 0.8 copy-done.9
  12.1 0.7 fusion.76
  13.0 0.8 select_reduce_fusion
  13.8 0.7 fusion.80
  14.5 1.1 scatter_custom_fusion
  15.6 0.8 all_to_all.12
  16.4 11.5 %all-to-all-start = ((s32[128,1,2]{2,1,0:T(1,128)}), s32[128,1,2]{2,1,0:T(1,128)S(1)}, u32[]{:S(2)}, u32[]{:S(2)}) async-start(s32[128,1,2]{2,1,0:T(1,128)} %bitcast.9), calls=%async_computation | async-start | bytes 131072 | tf_op jit(solution)/shard_map/all_to_all | solution.py:114
  27.9 0.9 slice.24
  28.9 8.5 %all-to-all-done = s32[128,1,2]{2,1,0:T(1,128)S(1)} async-done(((s32[128,1,2]{2,1,0:T(1,128)}), s32[128,1,2]{2,1,0:T(1,128)S(1)}, u32[]{:S(2)}, u32[]{:S(2)}) %all-to-all-start) | async-done | bytes 1056 | tf_op jit(solution)/shard_map/all_to_all | solution.py:114
  37.5 120.2 %all-gather.2.cloned.1.call-done = bf16[2048,6912]{1,0:T(8,128)(2,1)} async-done(((bf16[32,6912]{1,0:T(8,128)(2,1)}), bf16[2048,6912]{1,0:T(8,128)(2,1)}) %all-gather.2.cloned.1.call-update) | async-done | bytes 28311568 | tf_op jit(solution)/shard_map/all_gather | solution.py:83
  157.8 4.6 %fusion.14 = bf16[4,2048]{1,0:T(4,128)(2,1)S(1)} fusion(bf16[2048,6912]{1,0:T(8,128)(2,1)} %all-gather.2.cloned.1.call-done, bf16[4,1,2048]{2,1,0:T(2,128)(2,1)S(1)} %slice.24), kind=kOutput, calls=%fused_computation.22 | convolution fusion | flops 33562624 | bytes 8421376 | tf_op jit(solution)/shard_map/dot_general | solution.py:90
  162.4 5.2 %fusion.35 = bf16[1024,512]{0,1:T(8,128)(2,1)S(1)} fusion(bf16[1024,2048]{1,0:T(8,128)(2,1)} %bitcast.113, bf16[2048,6912]{1,0:T(8,128)(2,1)} %all-gather.2.cloned.1.call-done), kind=kOutput, calls=%fused_computation.47 | convolution fusion | flops 2148007936 | bytes 7340032 | tf_op jit(solution)/shard_map/dot_general | solution.py:87
  169.5 0.5 convolution_convert_fusion
  170.0 2.0 copy.51
  172.1 8.5 %all-to-all-start.1 = ((bf16[128,2,2048]{2,1,0:T(2,128)(2,1)}), bf16[128,2,2048]{2,1,0:T(2,128)(2,1)}, u32[]{:S(2)}, u32[]{:S(2)}) async-start(bf16[128,2,2048]{2,1,0:T(2,128)(2,1)} %copy.51), calls=%async_computation.1 | async-start | bytes 2097152 | tf_op jit(solution)/shard_map/all_to_all | solution.py:116
  180.6 0.7 copy.75
  181.3 0.5 slice-done
  182.2 15.8 %all-to-all-done.1 = bf16[128,2,2048]{2,1,0:T(2,128)(2,1)} async-done(((bf16[128,2,2048]{2,1,0:T(2,128)(2,1)}), bf16[128,2,2048]{2,1,0:T(2,128)(2,1)}, u32[]{:S(2)}, u32[]{:S(2)}) %all-to-all-start.1) | async-done | bytes 1048608 | tf_op jit(solution)/shard_map/all_to_all | solution.py:116
  198.1 1.5 reshape.152
  199.5 1.7 gather_fusion
  201.3 8.4 %fusion.8 = bf16[128,4096]{1,0:T(8,128)(2,1)S(1)} fusion(bf16[2048,6912]{1,0:T(8,128)(2,1)} %all-gather.2.cloned.1.call-done, bf16[128,2048]{1,0:T(8,128)(2,1)} %gather_fusion, pred[128]{0:T(512)(128)(4,1)S(1)} %compare_and_fusion), kind=kOutput, calls=%fused_computation.11 | convolution fusion | flops 2148270080 | bytes 18350208 | tf_op jit(solution)/shard_map/dot_general | solution.py:118
  210.3 1.9 fusion.38
  212.1 1.4 fusion.39
  213.6 3.5 %fusion.99 = (f32[32,128]{1,0:T(8,128)S(1)}, f32[32,128,128]{1,2,0:T(8,128)}) fusion(pred[128,128]{0,1:T(8,128)(4,1)S(1)} %iota_compare_fusion.2, bf16[128,32,128]{0,2,1:T(8,128)(2,1)} %fusion.38, bf16[128,4096]{1,0:T(8,128)(2,1)S(1)} %fusion.26), kind=kOutput, calls=%fused_computation.124 | convolution fusion | flops 136315008 | bytes 4227072 | tf_op jit(solution)/shard_map/jvp()/sub | solution.py:47
  217.1 2.6 fusion.22
  220.2 0.9 fusion.95
  221.0 0.8 fusion.40
  221.8 0.9 fusion.104
  222.7 2.0 fusion.51
  224.6 0.9 add_convert_fusion
  225.5 1.3 copy.76
  226.8 0.6 copy-done.2
  227.5 1.9 copy.74
  229.4 3.5 %fusion.28 = (f32[128]{0:T(128)S(1)}, bf16[1,128,4096]{2,1,0:T(8,128)(2,1)}) fusion(bf16[128,4096]{1,0:T(8,128)(2,1)S(1)} %copy-done.1, bf16[128,4096]{1,0:T(8,128)(2,1)} %copy.76, f32[4096]{0:T(1024)S(1)} %copy-done.10, f32[128,4096]{1,0:T(8,128)} %copy.74), kind=kLoop, calls=%fused_computation.34 | loop fusion | flops 3669888 | bytes 5259776 | tf_op jit(solution)/shard_map/transpose(jvp())/reduce_sum | solution.py:21
  232.9 10.4 %fusion.2 = f32[128,2048]{1,0:T(8,128)} fusion(bf16[2048,6912]{1,0:T(8,128)(2,1)} %all-gather.2.cloned.1.call-done, bf16[128,4096]{1,0:T(8,128)(2,1)S(1)} %copy-done.1, bf16[128,4096]{1,0:T(8,128)(2,1)S(1)} %copy-done.4, bf16[1,128,4096]{2,1,0:T(8,128)(2,1)S(1)} %copy-done.8, f32[128]{0:T(128)S(1)} %multiply_multiply_fusion, f32[4096]{0:T(1024)S(1)} %copy-done.10, ...), kind=kOutput, calls=%fused_computation.5 | convolution fusion | flops 2152202240 | bytes 20988928 | tf_op jit(solution)/shard_map/dot_general | solution.py:123
  243.3 2.4 scatter_custom_fusion.1
  245.9 1.5 convert_element_type.128
  247.4 5.5 %all-to-all-start.2 = ((bf16[128,2,2048]{2,1,0:T(2,128)(2,1)}), bf16[128,2,2048]{2,1,0:T(2,128)(2,1)S(1)}, u32[]{:S(2)}, u32[]{:S(2)}) async-start(bf16[128,2,2048]{2,1,0:T(2,128)(2,1)} %convert_element_type.128), calls=%async_computation.2 | async-start | bytes 2097152 | tf_op jit(solution)/shard_map/all_to_all | solution.py:125
  252.9 0.5 broadcast.136
  253.4 0.8 reduce.4
  254.4 16.4 %all-to-all-done.2 = bf16[128,2,2048]{2,1,0:T(2,128)(2,1)S(1)} async-done(((bf16[128,2,2048]{2,1,0:T(2,128)(2,1)}), bf16[128,2,2048]{2,1,0:T(2,128)(2,1)S(1)}, u32[]{:S(2)}, u32[]{:S(2)}) %all-to-all-start.2) | async-done | bytes 1048608 | tf_op jit(solution)/shard_map/all_to_all | solution.py:125
  270.7 0.4 reshape.156
  271.2 1.0 fusion.74
  (56 shorter events, 4.2 us)
Async XLA Ops:
  7.2 150.6 %all-gather.2.cloned.1.call-start = ((), (), s32[]{:S(2)}) async-start(), calls=%async_computation.3 | async-start | bytes 28753920 | tf_op jit(solution)/shard_map/all_gather | solution.py:83
  11.3 0.8 copy-start.9
  16.4 21.1 %all-to-all-start = ((s32[128,1,2]{2,1,0:T(1,128)}), s32[128,1,2]{2,1,0:T(1,128)S(1)}, u32[]{:S(2)}, u32[]{:S(2)}) async-start(s32[128,1,2]{2,1,0:T(1,128)} %bitcast.9), calls=%async_computation | async-start | bytes 131072 | tf_op jit(solution)/shard_map/all_to_all | solution.py:114
  167.7 1.7 copy-start.12
  169.5 2.6 copy-start.11
  170.0 10.6 %copy-start.7 = (bf16[1,128,4096]{2,1,0:T(8,128)(2,1)S(1)}, bf16[1,128,4096]{2,1,0:T(8,128)(2,1)}, u32[]{:S(2)}) copy-start(bf16[1,128,4096]{2,1,0:T(8,128)(2,1)} %param.21) | copy-start | bytes 3145732
  172.1 9.2 %copy-start.13 = (s32[1,128,1]{1,2,0:T(1,128)S(1)}, s32[1,128,1]{1,2,0:T(1,128)}, u32[]{:S(2)}) copy-start(s32[1,128,1]{1,2,0:T(1,128)} %param.19) | copy-start | bytes 1540
  172.1 26.0 %all-to-all-start.1 = ((bf16[128,2,2048]{2,1,0:T(2,128)(2,1)}), bf16[128,2,2048]{2,1,0:T(2,128)(2,1)}, u32[]{:S(2)}, u32[]{:S(2)}) async-start(bf16[128,2,2048]{2,1,0:T(2,128)(2,1)} %copy.51), calls=%async_computation.1 | async-start | bytes 2097152 | tf_op jit(solution)/shard_map/all_to_all | solution.py:116
  180.6 1.2 slice-start
  201.3 8.7 %copy-start.10 = (f32[4096]{0:T(1024)S(1)}, f32[4096]{0:T(1024)}, u32[]{:S(2)}) copy-start(f32[4096]{0:T(1024)} %param.17) | copy-start | bytes 49156
  209.6 2.5 copy-start
  217.0 2.6 copy-start.3
  217.0 2.9 %copy-start.5 = (f32[32,128,128]{1,2,0:T(8,128)S(1)}, f32[32,128,128]{1,2,0:T(8,128)}, u32[]{:S(2)}) copy-start(f32[32,128,128]{1,2,0:T(8,128)} %get-tuple-element.14) | copy-start | bytes 6291460
  217.0 3.1 %copy-start.6 = (bf16[128,32,128]{0,2,1:T(8,128)(2,1)S(1)}, bf16[128,32,128]{0,2,1:T(8,128)(2,1)}, u32[]{:S(2)}) copy-start(bf16[128,32,128]{0,2,1:T(8,128)(2,1)} %fusion.38) | copy-start | bytes 3145732
  225.5 2.0 copy-start.2
  227.5 1.9 copy-start.1
  229.4 3.5 %copy-start.4 = (bf16[128,4096]{1,0:T(8,128)(2,1)S(1)}, bf16[128,4096]{1,0:T(8,128)(2,1)}, u32[]{:S(2)}) copy-start(bf16[128,4096]{1,0:T(8,128)(2,1)} %copy.76) | copy-start | bytes 3145732
  229.4 3.5 %copy-start.8 = (bf16[1,128,4096]{2,1,0:T(8,128)(2,1)S(1)}, bf16[1,128,4096]{2,1,0:T(8,128)(2,1)}, u32[]{:S(2)}) copy-start(bf16[1,128,4096]{2,1,0:T(8,128)(2,1)} %param.21) | copy-start | bytes 3145732
  247.4 23.3 %all-to-all-start.2 = ((bf16[128,2,2048]{2,1,0:T(2,128)(2,1)}), bf16[128,2,2048]{2,1,0:T(2,128)(2,1)S(1)}, u32[]{:S(2)}, u32[]{:S(2)}) async-start(bf16[128,2,2048]{2,1,0:T(2,128)(2,1)} %convert_element_type.128), calls=%async_computation.2 | async-start | bytes 2097152 | tf_op jit(solution)/shard_map/all_to_all | solution.py:125
Sparse Core Ops, SparseCore 0:
  12.2 145.5 all-gather.1

commit v2 on v1

--- a/solution.py
+++ b/solution.py
@@ -77,21 +77,33 @@
     count = item_states.shape[0]
     flat = item_states.reshape(count * ILEN, DI)
     last_row = item_states[:, ILEN - 1, :]
-    packed = jnp.concatenate(
-        [w_key, w_value, w_query, w_adapt, user_query.reshape(w_key.shape[0], -1)], axis=1
+    side = lax.axis_index("grp")
+
+    def half(w, rows=None):
+        w = w if rows is None else w.reshape(rows, -1)
+        return lax.dynamic_slice_in_dim(w, side * (w.shape[1] // 2), w.shape[1] // 2, axis=1)
+
+    pieces = [half(w_key), half(w_value), half(w_query), half(w_adapt), half(user_query, w_key.shape[0])]
+    widths = [p.shape[1] for p in pieces]
+    ends = [sum(widths[: i + 1]) for i in range(len(widths))]
+    gathered = lax.all_gather(
+        jnp.concatenate(pieces, axis=1), ("grp", "fsdp"), axis=0, tiled=True
+    ).reshape(groups, DI, ends[-1])
+    kv_sum = jnp.einsum(
+        "td,gdc->tgc", flat, gathered[:, :, : ends[1]], preferred_element_type=jnp.float32
     )
-    gathered = lax.all_gather(packed, "fsdp", axis=0, tiled=True)
-    kv_cols = w_key.shape[1] + w_value.shape[1]
-    q_end = kv_cols + w_query.shape[1]
-    a_end = q_end + w_adapt.shape[1]
-    kv_sum = jnp.dot(flat, gathered[:, :kv_cols], preferred_element_type=jnp.float32)
-    key_sum = kv_sum[:, : w_key.shape[1]]
-    summed_value = kv_sum[:, w_key.shape[1] :]
-    query_sum = jnp.dot(
-        last_row, gathered[:, kv_cols:q_end], preferred_element_type=jnp.float32
+    key_sum = kv_sum[:, :, : widths[0]].reshape(flat.shape[0], -1)
+    summed_value = kv_sum[:, :, widths[0] :].reshape(flat.shape[0], -1)
+    query_sum = jnp.einsum(
+        "id,gdc->igc", last_row, gathered[:, :, ends[1] : ends[2]], preferred_element_type=jnp.float32
+    ).reshape(count, -1)
+    adapter_halves = gathered[:, :, ends[2] : ends[3]]
+    query_map = (
+        gathered[:, :, ends[3] :]
+        .reshape(groups, DI, -1, user_query.shape[1])
+        .transpose(1, 2, 0, 3)
+        .reshape(-1, user_query.shape[1])
     )
-    adapter = gathered[:, q_end:a_end]
-    query_map = gathered[:, a_end:].reshape(-1, user_query.shape[1])
     item_embed = item_pool(
         item_states, stored(key_sum), stored(summed_value), stored(query_sum), item_gain
     )
@@ -115,12 +127,21 @@
     found = serve_rows(incoming, item_embed)
     returned = lax.all_to_all(found, ("grp", "fsdp"), split_axis=0, concat_axis=0, tiled=True)
     fetched = jnp.take(returned.reshape(devices * cap_slots, width), position, axis=0)
-    hidden = stored(jnp.dot(fetched, adapter, preferred_element_type=jnp.float32))
+    hidden = stored(
+        jnp.einsum("td,gdc->tgc", fetched, adapter_halves, preferred_element_type=jnp.float32).reshape(
+            fetched.shape[0], -1
+        )
+    )
     user_attention_output, pull = jax.vjp(
         lambda values: user_layer(values, user_gain, query_map), hidden
     )
     (grad_hidden,) = pull(cotangent[0])
-    grad_rows = jnp.dot(grad_hidden, adapter.T, preferred_element_type=jnp.float32)
+    grad_rows = jnp.einsum(
+        "tgc,gdc->td",
+        grad_hidden.reshape(grad_hidden.shape[0], groups, -1),
+        adapter_halves,
+        preferred_element_type=jnp.float32,
+    )
     outgoing = jnp.zeros((devices * cap_slots, DI), jnp.float32).at[position].set(grad_rows)
     arrived = lax.all_to_all(
         outgoing.reshape(devices, cap_slots, DI).astype(jnp.bfloat16),

time: 280 us -> 228 us (0.81)
  waiting for transfers between devices: 161 us -> 106 us
  local copies, waits for them, and re-layouts: 25 us -> 31.5 us
    all_gather x1, waiting for transfers between devices: 120 us -> 76.3 us  [per_device(): lax.all_gather(jnp.concatenate(pieces, axis=1), ('grp', 'fsdp'), axis=0,...]
    transpose x0 -> x2, local copies, waits for them, and re-layouts: none -> 10.8 us  [per_device(): query_map = gathered[:, :, ends[3]:].reshape(groups, DI, -1, user_query.s...]
    all_to_all x1, waiting for transfers between devices: 15.8 us -> 6.32 us  [per_device(): lax.all_to_all(found, ('grp', 'fsdp'), split_axis=0, concat_axis=0, tiled...]
    unnamed x32 -> x30, local copies, waits for them, and re-layouts: 5.25 us -> 6.89 us
  transfers between devices with their start and end apart: 4 -> 4, of which waited for: 4 -> 4; matrix products, arithmetic and copies ran while one was open for 3% -> 8% of each run, Pallas kernels for 0% -> 0%
where the time goes in v2:
time: 228 us; the launch traced here: 227 us
  waiting for transfers between devices  106 us (46%)
  matrix products  40.8 us (18%)
  local copies, waits for them, and re-layouts  31.5 us (14%)
  starting transfers between devices  24.3 us (11%)
  between operations  14.4 us (6%)
  other arithmetic  10.2 us (4%)
    all_gather x1, waiting for transfers between devices, per_device(): lax.all_gather(jnp.concatenate(pieces, axis=1), ('grp', 'fsdp'), axis=0,...  76.3 us
    all_to_all x1, waiting for transfers between devices, per_device(): lax.all_to_all(outgoing.reshape(devices, cap_slots, DI).astype(jnp.bfloat...  15 us
    all_to_all x1, starting transfers between devices, per_device(): lax.all_to_all(request, ('grp', 'fsdp'), split_axis=0, concat_axis=0, til...  11.5 us
    transpose x2, local copies, waits for them, and re-layouts, per_device(): query_map = gathered[:, :, ends[3]:].reshape(groups, DI, -1, user_query.s...  10.8 us
    dot_general x1, matrix products, per_device(): jnp.einsum('tgc,gdc->td', grad_hidden.reshape(grad_hidden.shape[0], group...  10.3 us
    all_to_all x1, waiting for transfers between devices, per_device(): lax.all_to_all(request, ('grp', 'fsdp'), split_axis=0, concat_axis=0, til...  8.29 us
    dot_general x1, matrix products, per_device(): jnp.einsum('td,gdc->tgc', fetched, adapter_halves, preferred_element_type...  8.24 us
    all_to_all x1, starting transfers between devices, per_device(): lax.all_to_all(found, ('grp', 'fsdp'), split_axis=0, concat_axis=0, tiled...  7.26 us
  transfers between devices with their start and end apart: 4, of which 4 were waited for; matrix products, arithmetic and copies ran while one was open for 8% of the time, Pallas kernels for 0%

profile of v2, /device:TPU:1, one launch (start us, length us, event | category | flops | bytes accessed | tf_op | source)
XLA Modules:
  0.0 227.2 jit_solution(43007588154248595)
XLA Ops:
  7.2 0.7 reshape.163
  7.9 0.7 constant_dynamic-update-slice_fusion.2
  8.7 0.7 constant_dynamic-update-slice_fusion.1
  9.4 0.8 dynamic-slice_dynamic-update-slice_fusion.1
  10.2 0.9 dynamic-slice_dynamic-update-slice_fusion
  11.2 0.7 copy-done.7
  11.9 0.7 fusion.59
  12.8 0.8 select_reduce_fusion
  13.6 0.7 fusion.63
  14.3 1.1 scatter_custom_fusion
  15.4 0.8 all_to_all.12
  16.1 11.5 %all-to-all-start = ((s32[128,1,2]{2,1,0:T(1,128)}), s32[128,1,2]{2,1,0:T(1,128)S(1)}, u32[]{:S(2)}, u32[]{:S(2)}) async-start(s32[128,1,2]{2,1,0:T(1,128)} %bitcast.15), calls=%async_computation | async-start | bytes 131072 | tf_op jit(solution)/shard_map/all_to_all | solution.py:126
  27.6 0.9 slice.24
  28.7 8.3 %all-to-all-done = s32[128,1,2]{2,1,0:T(1,128)S(1)} async-done(((s32[128,1,2]{2,1,0:T(1,128)}), s32[128,1,2]{2,1,0:T(1,128)S(1)}, u32[]{:S(2)}, u32[]{:S(2)}) %all-to-all-start) | async-done | bytes 1056 | tf_op jit(solution)/shard_map/all_to_all | solution.py:126
  37.1 76.3 %all-gather.2.cloned.1.call-done = bf16[4096,3456]{1,0:T(8,128)(2,1)} async-done(((bf16[32,3456]{1,0:T(8,128)(2,1)}), bf16[4096,3456]{1,0:T(8,128)(2,1)}) %all-gather.2.cloned.1.call-update) | async-done | bytes 28311568 | tf_op jit(solution)/shard_map/all_gather | solution.py:89
  113.4 4.6 %fusion.40 = bf16[2,1024,4]{1,2,0:T(4,128)(2,1)S(1)} fusion(bf16[2,2048,3456]{2,1,0:T(8,128)(2,1)} %bitcast.115, bf16[4,1,2048]{2,1,0:T(2,128)(2,1)S(1)} %slice.24), kind=kOutput, calls=%fused_computation.53 | convolution fusion | flops 33562624 | bytes 8421376 | tf_op jit(solution)/shard_map/id,gdc->igc/dot_general | solution.py:97
  118.0 5.3 %fusion.32 = bf16[1024,2,256]{0,2,1:T(8,128)(2,1)S(1)} fusion(bf16[1024,2048,1]{1,0,2:T(8,128)(2,1)} %bitcast.123, bf16[2,2048,3456]{2,1,0:T(8,128)(2,1)} %bitcast.116), kind=kOutput, calls=%fused_computation.46 | convolution fusion | flops 2148007936 | bytes 7340032 | tf_op jit(solution)/shard_map/td,gdc->tgc/dot_general | solution.py:92
  125.2 0.5 convolution_convert_fusion
  125.7 2.0 copy.55
  127.8 7.3 %all-to-all-start.1 = ((bf16[128,2,2048]{2,1,0:T(2,128)(2,1)}), bf16[128,2,2048]{2,1,0:T(2,128)(2,1)S(1)}, u32[]{:S(2)}, u32[]{:S(2)}) async-start(bf16[128,2,2048]{2,1,0:T(2,128)(2,1)} %copy.55), calls=%async_computation.1 | async-start | bytes 2097152 | tf_op jit(solution)/shard_map/all_to_all | solution.py:128
  135.0 0.7 copy.63
  135.8 1.3 slice_bitcast_fusion
  137.1 9.5 %copy.57 = bf16[2048,1,2,128]{3,2,0,1:T(2,128)(2,1)} copy(bf16[2048,1,2,128]{3,0,2,1:T(8,128)(2,1)S(1)} %slice_bitcast_fusion) | data formatting | bytes 2097152 | tf_op jit(solution)/shard_map/transpose | solution.py:104
  146.5 6.3 %all-to-all-done.1 = bf16[128,2,2048]{2,1,0:T(2,128)(2,1)S(1)} async-done(((bf16[128,2,2048]{2,1,0:T(2,128)(2,1)}), bf16[128,2,2048]{2,1,0:T(2,128)(2,1)S(1)}, u32[]{:S(2)}, u32[]{:S(2)}) %all-to-all-start.1) | async-done | bytes 1048608 | tf_op jit(solution)/shard_map/all_to_all | solution.py:128
  153.3 0.9 gather_fusion
  154.2 8.2 %fusion.8 = bf16[128,2,2048]{2,0,1:T(8,128)(2,1)S(1)} fusion(bf16[2,2048,3456]{2,1,0:T(8,128)(2,1)} %bitcast.118, bf16[128,2048]{1,0:T(8,128)(2,1)S(1)} %gather_fusion, pred[128]{0:T(512)(128)(4,1)S(1)} %compare_and_fusion), kind=kOutput, calls=%fused_computation.19 | convolution fusion | flops 2148270080 | bytes 18350208 | tf_op jit(solution)/shard_map/td,gdc->tgc/dot_general | solution.py:131
  162.5 0.7 copy.56
  163.1 0.6 fusion.21
  163.7 0.9 fusion.23
  164.7 1.5 fusion.36
  166.2 1.5 fusion.35
  167.7 3.5 %fusion.78 = (f32[32,128]{1,0:T(8,128)S(1)}, f32[32,128,128]{1,2,0:T(8,128)}) fusion(pred[128,128]{0,1:T(8,128)(4,1)S(1)} %iota_compare_fusion.2, bf16[128,32,128]{0,2,1:T(8,128)(2,1)} %fusion.35, bf16[128,32,128]{0,2,1:T(8,128)(2,1)S(1)} %bitcast.101), kind=kOutput, calls=%fused_computation.110 | convolution fusion | flops 136315008 | bytes 4227072 | tf_op jit(solution)/shard_map/jvp()/sub | solution.py:47
  171.2 2.6 %fusion.19 = (f32[32,128]{1,0:T(8,128)S(1)}, bf16[32,128,128]{1,2,0:T(8,128)(2,1)S(1)}) fusion(f32[32,128,128]{1,2,0:T(8,128)} %get-tuple-element.20, bf16[32,128,128]{1,2,0:T(8,128)(2,1)} %fusion.36, f32[32,128]{1,0:T(8,128)S(1)} %multiply_divide_fusion, f32[32,128]{1,0:T(8,128)S(1)} %get-tuple-element.19), kind=kLoop, calls=%fused_computation.27 | loop fusion | flops 3141632 | bytes 4243456 | tf_op jit(solution)/shard_map/transpose(jvp())/reduce_sum | solution.py:47
  174.1 0.8 fusion.37
  175.3 0.9 fusion.74
  176.6 0.8 fusion.82
  177.8 0.8 add_convert_fusion
  178.7 1.6 fusion.25
  180.3 0.9 fusion.43
  181.2 10.3 %fusion.11 = f32[128,2048]{1,0:T(8,128)} fusion(bf16[128,2,2048]{0,2,1:T(8,128)(2,1)S(1)} %bitcast.113, bf16[2,2048,3456]{2,1,0:T(8,128)(2,1)} %bitcast.119), kind=kOutput, calls=%fused_computation.21 | convolution fusion | flops 2147483648 | bytes 18874368 | tf_op jit(solution)/shard_map/tgc,gdc->td/dot_general | solution.py:139
  191.5 2.4 %scatter_custom_fusion.1 = f32[256,2048]{1,0:T(8,128)S(1)} fusion(s32[128]{0:T(128)S(1)} %fusion.63, f32[128,2048]{1,0:T(8,128)} %fusion.11, f32[]{:T(128)} %constant.32.clone.1), kind=kCustom, calls=%fused_computation.57 | custom fusion | bytes 2097664 | tf_op jit(solution)/shard_map/scatter | solution.py:145
  194.1 1.5 convert_element_type.144
  195.6 5.5 %all-to-all-start.2 = ((bf16[128,2,2048]{2,1,0:T(2,128)(2,1)}), bf16[128,2,2048]{2,1,0:T(2,128)(2,1)S(1)}, u32[]{:S(2)}, u32[]{:S(2)}) async-start(bf16[128,2,2048]{2,1,0:T(2,128)(2,1)} %convert_element_type.144), calls=%async_computation.2 | async-start | bytes 2097152 | tf_op jit(solution)/shard_map/all_to_all | solution.py:146
  201.1 0.5 broadcast.136
  201.6 0.8 reduce.4
  202.6 1.3 copy.72
  203.9 15.0 %all-to-all-done.2 = bf16[128,2,2048]{2,1,0:T(2,128)(2,1)S(1)} async-done(((bf16[128,2,2048]{2,1,0:T(2,128)(2,1)}), bf16[128,2,2048]{2,1,0:T(2,128)(2,1)S(1)}, u32[]{:S(2)}, u32[]{:S(2)}) %all-to-all-start.2) | async-done | bytes 1048608 | tf_op jit(solution)/shard_map/all_to_all | solution.py:146
  219.4 1.0 fusion.57
  (52 shorter events, 5.0 us)
Async XLA Ops:
  7.2 106.2 %all-gather.2.cloned.1.call-start = ((), (), s32[]{:S(2)}) async-start(), calls=%async_computation.3 | async-start | bytes 28532736 | tf_op jit(solution)/shard_map/all_gather | solution.py:89
  11.1 0.7 copy-start.7
  16.1 20.9 %all-to-all-start = ((s32[128,1,2]{2,1,0:T(1,128)}), s32[128,1,2]{2,1,0:T(1,128)S(1)}, u32[]{:S(2)}, u32[]{:S(2)}) async-start(s32[128,1,2]{2,1,0:T(1,128)} %bitcast.15), calls=%async_computation | async-start | bytes 131072 | tf_op jit(solution)/shard_map/all_to_all | solution.py:126
  123.4 1.7 copy-start.10
  125.2 2.6 %copy-start.9 = (bf16[4,2048]{1,0:T(4,128)(2,1)}, bf16[4,2048]{1,0:T(4,128)(2,1)S(1)}, u32[]{:S(2)}) copy-start(bf16[4,2048]{1,0:T(4,128)(2,1)S(1)} %multiply_convert_fusion) | copy-start | bytes 49156
  125.7 9.3 %copy-start.6 = (bf16[1,128,4096]{2,1,0:T(8,128)(2,1)S(1)}, bf16[1,128,4096]{2,1,0:T(8,128)(2,1)}, u32[]{:S(2)}) copy-start(bf16[1,128,4096]{2,1,0:T(8,128)(2,1)} %param.21) | copy-start | bytes 3145732
  127.8 8.0 %copy-start.11 = (s32[1,128,1]{1,2,0:T(1,128)S(1)}, s32[1,128,1]{1,2,0:T(1,128)}, u32[]{:S(2)}) copy-start(s32[1,128,1]{1,2,0:T(1,128)} %param.19) | copy-start | bytes 1540
  127.8 25.1 %all-to-all-start.1 = ((bf16[128,2,2048]{2,1,0:T(2,128)(2,1)}), bf16[128,2,2048]{2,1,0:T(2,128)(2,1)S(1)}, u32[]{:S(2)}, u32[]{:S(2)}) async-start(bf16[128,2,2048]{2,1,0:T(2,128)(2,1)} %copy.55), calls=%async_computation.1 | async-start | bytes 2097152 | tf_op jit(solution)/shard_map/all_to_all | solution.py:128
  162.5 1.2 copy-start.8
  164.6 1.5 copy-start
  171.2 2.6 %copy-start.2 = (bf16[32,128,128]{1,2,0:T(8,128)(2,1)S(1)}, bf16[32,128,128]{1,2,0:T(8,128)(2,1)}, u32[]{:S(2)}) copy-start(bf16[32,128,128]{1,2,0:T(8,128)(2,1)} %fusion.36) | copy-start | bytes 3145732
  171.2 2.9 %copy-start.4 = (f32[32,128,128]{1,2,0:T(8,128)S(1)}, f32[32,128,128]{1,2,0:T(8,128)}, u32[]{:S(2)}) copy-start(f32[32,128,128]{1,2,0:T(8,128)} %get-tuple-element.20) | copy-start | bytes 6291460
  174.1 1.2 copy-start.5
  176.6 1.2 copy-start.1
  194.1 8.5 %copy-start.3 = (bf16[128,4096]{0,1:T(8,128)(2,1)S(1)}, bf16[128,4096]{0,1:T(8,128)(2,1)}, u32[]{:S(2)}) copy-start(bf16[128,4096]{0,1:T(8,128)(2,1)} %get-tuple-element.12) | copy-start | bytes 3145732
  195.6 23.3 %all-to-all-start.2 = ((bf16[128,2,2048]{2,1,0:T(2,128)(2,1)}), bf16[128,2,2048]{2,1,0:T(2,128)(2,1)S(1)}, u32[]{:S(2)}, u32[]{:S(2)}) async-start(bf16[128,2,2048]{2,1,0:T(2,128)(2,1)} %convert_element_type.144), calls=%async_computation.2 | async-start | bytes 2097152 | tf_op jit(solution)/shard_map/all_to_all | solution.py:146
Sparse Core Ops, SparseCore 0:
  12.0 101.3 all-gather.1

commit v3 on v2

--- a/solution.py
+++ b/solution.py
@@ -78,32 +78,33 @@
     flat = item_states.reshape(count * ILEN, DI)
     last_row = item_states[:, ILEN - 1, :]
     side = lax.axis_index("grp")
+    query_rows_of = user_query.reshape(w_key.shape[0], -1)
 
-    def half(w, rows=None):
-        w = w if rows is None else w.reshape(rows, -1)
-        return lax.dynamic_slice_in_dim(w, side * (w.shape[1] // 2), w.shape[1] // 2, axis=1)
+    def halves(w):
+        return [w[:, i * (w.shape[1] // groups) : (i + 1) * (w.shape[1] // groups)] for i in range(groups)]
 
-    pieces = [half(w_key), half(w_value), half(w_query), half(w_adapt), half(user_query, w_key.shape[0])]
-    widths = [p.shape[1] for p in pieces]
+    split = [halves(w) for w in (w_adapt, w_query, w_key, w_value)]
+    widths = [part[0].shape[1] for part in split] + [query_rows_of.shape[1]]
     ends = [sum(widths[: i + 1]) for i in range(len(widths))]
+    both = jnp.concatenate(
+        [piece for i in range(groups) for piece in [part[i] for part in split] + [query_rows_of]], axis=1
+    )
     gathered = lax.all_gather(
-        jnp.concatenate(pieces, axis=1), ("grp", "fsdp"), axis=0, tiled=True
+        lax.dynamic_slice_in_dim(both, side * ends[-1], ends[-1], axis=1),
+        ("grp", "fsdp"),
+        axis=0,
+        tiled=True,
     ).reshape(groups, DI, ends[-1])
     kv_sum = jnp.einsum(
-        "td,gdc->tgc", flat, gathered[:, :, : ends[1]], preferred_element_type=jnp.float32
+        "td,gdc->tgc", flat, gathered[:, :, ends[1] : ends[3]], preferred_element_type=jnp.float32
     )
-    key_sum = kv_sum[:, :, : widths[0]].reshape(flat.shape[0], -1)
-    summed_value = kv_sum[:, :, widths[0] :].reshape(flat.shape[0], -1)
+    key_sum = kv_sum[:, :, : widths[2]].reshape(flat.shape[0], -1)
+    summed_value = kv_sum[:, :, widths[2] :].reshape(flat.shape[0], -1)
     query_sum = jnp.einsum(
-        "id,gdc->igc", last_row, gathered[:, :, ends[1] : ends[2]], preferred_element_type=jnp.float32
+        "id,gdc->igc", last_row, gathered[:, :, ends[0] : ends[1]], preferred_element_type=jnp.float32
     ).reshape(count, -1)
-    adapter_halves = gathered[:, :, ends[2] : ends[3]]
-    query_map = (
-        gathered[:, :, ends[3] :]
-        .reshape(groups, DI, -1, user_query.shape[1])
-        .transpose(1, 2, 0, 3)
-        .reshape(-1, user_query.shape[1])
-    )
+    adapter_halves = gathered[:, :, : ends[0]]
+    query_map = gathered[0, :, ends[3] :].reshape(-1, user_query.shape[1])
     item_embed = item_pool(
         item_states, stored(key_sum), stored(summed_value), stored(query_sum), item_gain
     )

time: 228 us -> 233 us (1.022)
  waiting for transfers between devices: 106 us -> 116 us
  local copies, waits for them, and re-layouts: 31.5 us -> 26.4 us
    transpose x2 -> x0, local copies, waits for them, and re-layouts: 10.8 us -> none  [per_device(): query_map = gathered[:, :, ends[3]:].reshape(groups, DI, -1, user_query.s...]
    all_to_all x1, waiting for transfers between devices: 6.32 us -> 14.6 us  [per_device(): lax.all_to_all(found, ('grp', 'fsdp'), split_axis=0, concat_axis=0, tiled...]
    unnamed x30 -> x33, local copies, waits for them, and re-layouts: 6.89 us -> 9.38 us
  transfers between devices with their start and end apart: 4 -> 4, of which waited for: 4 -> 4; matrix products, arithmetic and copies ran while one was open for 8% -> 5% of each run, Pallas kernels for 0% -> 0%
where the time goes in v3:
time: 233 us; the launch traced here: 232 us
  waiting for transfers between devices  116 us (50%)
  matrix products  41.1 us (18%)
  local copies, waits for them, and re-layouts  26.4 us (11%)
  starting transfers between devices  24.3 us (10%)
  between operations  14.4 us (6%)
  other arithmetic  10 us (4%)
    all_gather x1, waiting for transfers between devices, per_device(): lax.all_gather(lax.dynamic_slice_in_dim(both, side * ends[-1], ends[-1],...  78.1 us
    all_to_all x1, waiting for transfers between devices, per_device(): lax.all_to_all(outgoing.reshape(devices, cap_slots, DI).astype(jnp.bfloat...  15 us
    all_to_all x1, waiting for transfers between devices, per_device(): lax.all_to_all(found, ('grp', 'fsdp'), split_axis=0, concat_axis=0, tiled...  14.6 us
    all_to_all x1, starting transfers between devices, per_device(): lax.all_to_all(request, ('grp', 'fsdp'), split_axis=0, concat_axis=0, til...  11.5 us
    dot_general x1, matrix products, per_device(): jnp.einsum('tgc,gdc->td', grad_hidden.reshape(grad_hidden.shape[0], group...  10.6 us
    unnamed x33, local copies, waits for them, and re-layouts  9.38 us
    all_to_all x1, waiting for transfers between devices, per_device(): lax.all_to_all(request, ('grp', 'fsdp'), split_axis=0, concat_axis=0, til...  8.3 us
    dot_general x1, matrix products, per_device(): jnp.einsum('td,gdc->tgc', fetched, adapter_halves, preferred_element_type...  8.24 us
  transfers between devices with their start and end apart: 4, of which 4 were waited for; matrix products, arithmetic and copies ran while one was open for 5% of the time, Pallas kernels for 0%

profile of v3, /device:TPU:1, one launch (start us, length us, event | category | flops | bytes accessed | tf_op | source)
XLA Modules:
  0.0 232.3 jit_solution(16296114219733206983)
XLA Ops:
  7.2 0.7 reshape.160
  7.9 0.9 slice_dynamic-update-slice_fusion.1
  8.9 0.8 slice_dynamic-update-slice_fusion.3
  9.7 0.7 constant_dynamic-update-slice_fusion.5
  10.4 0.7 constant_dynamic-update-slice_fusion.4
  11.1 0.9 slice_dynamic-update-slice_fusion
  12.0 0.8 slice_dynamic-update-slice_fusion.2
  12.9 0.7 constant_dynamic-update-slice_fusion.2
  13.6 0.7 constant_dynamic-update-slice_fusion.1
  14.3 0.7 constant_dynamic-slice_fusion
  15.0 0.7 fusion.59
  15.9 0.8 select_reduce_fusion
  16.8 0.7 fusion.63
  17.4 1.1 scatter_custom_fusion
  18.6 0.8 all_to_all.12
  19.3 11.5 %all-to-all-start = ((s32[128,1,2]{2,1,0:T(1,128)}), s32[128,1,2]{2,1,0:T(1,128)S(1)}, u32[]{:S(2)}, u32[]{:S(2)}) async-start(s32[128,1,2]{2,1,0:T(1,128)} %bitcast.15), calls=%async_computation | async-start | bytes 131072 | tf_op jit(solution)/shard_map/all_to_all | solution.py:127
  30.8 0.9 slice.48
  31.9 8.3 %all-to-all-done = s32[128,1,2]{2,1,0:T(1,128)S(1)} async-done(((s32[128,1,2]{2,1,0:T(1,128)}), s32[128,1,2]{2,1,0:T(1,128)S(1)}, u32[]{:S(2)}, u32[]{:S(2)}) %all-to-all-start) | async-done | bytes 1056 | tf_op jit(solution)/shard_map/all_to_all | solution.py:127
  40.2 78.1 %all-gather.2.cloned.1.call-done = bf16[4096,3584]{1,0:T(8,128)(2,1)} async-done(((bf16[32,3584]{1,0:T(8,128)(2,1)}), bf16[4096,3584]{1,0:T(8,128)(2,1)}) %all-gather.2.cloned.1.call-update) | async-done | bytes 29360144 | tf_op jit(solution)/shard_map/all_gather | solution.py:92
  118.4 4.6 %fusion.40 = bf16[2,1024,4]{1,2,0:T(4,128)(2,1)S(1)} fusion(bf16[2,2048,3584]{2,1,0:T(8,128)(2,1)} %bitcast.108, bf16[4,1,2048]{2,1,0:T(2,128)(2,1)S(1)} %slice.48), kind=kOutput, calls=%fused_computation.53 | convolution fusion | flops 33562624 | bytes 8421376 | tf_op jit(solution)/shard_map/id,gdc->igc/dot_general | solution.py:103
  123.1 5.2 %fusion.32 = bf16[1024,2,256]{0,2,1:T(8,128)(2,1)S(1)} fusion(bf16[1024,2048,1]{1,0,2:T(8,128)(2,1)} %bitcast.116, bf16[2,2048,3584]{2,1,0:T(8,128)(2,1)} %bitcast.109), kind=kOutput, calls=%fused_computation.46 | convolution fusion | flops 2148007936 | bytes 7340032 | tf_op jit(solution)/shard_map/td,gdc->tgc/dot_general | solution.py:98
  130.7 2.0 copy.54
  132.7 7.3 %all-to-all-start.1 = ((bf16[128,2,2048]{2,1,0:T(2,128)(2,1)}), bf16[128,2,2048]{2,1,0:T(2,128)(2,1)S(1)}, u32[]{:S(2)}, u32[]{:S(2)}) async-start(bf16[128,2,2048]{2,1,0:T(2,128)(2,1)} %copy.54), calls=%async_computation.1 | async-start | bytes 2097152 | tf_op jit(solution)/shard_map/all_to_all | solution.py:129
  140.0 0.7 copy.61
  140.7 1.3 slice.70
  142.0 1.2 reshape_reshape_squeeze.3
  143.2 14.6 %all-to-all-done.1 = bf16[128,2,2048]{2,1,0:T(2,128)(2,1)S(1)} async-done(((bf16[128,2,2048]{2,1,0:T(2,128)(2,1)}), bf16[128,2,2048]{2,1,0:T(2,128)(2,1)S(1)}, u32[]{:S(2)}, u32[]{:S(2)}) %all-to-all-start.1) | async-done | bytes 1048608 | tf_op jit(solution)/shard_map/all_to_all | solution.py:129
  158.3 0.9 gather_fusion
  159.2 8.2 %fusion.8 = bf16[128,2,2048]{2,0,1:T(8,128)(2,1)S(1)} fusion(bf16[2,2048,3584]{2,1,0:T(8,128)(2,1)} %bitcast.111, bf16[128,2048]{1,0:T(8,128)(2,1)S(1)} %gather_fusion, pred[128]{0:T(512)(128)(4,1)S(1)} %compare_and_fusion), kind=kOutput, calls=%fused_computation.19 | convolution fusion | flops 2148270080 | bytes 18350208 | tf_op jit(solution)/shard_map/td,gdc->tgc/dot_general | solution.py:132
  168.7 0.7 fusion.23
  169.4 1.5 fusion.36
  170.9 1.5 fusion.35
  172.4 3.5 %fusion.78 = (f32[32,128]{1,0:T(8,128)S(1)}, f32[32,128,128]{1,2,0:T(8,128)}) fusion(pred[128,128]{0,1:T(8,128)(4,1)S(1)} %iota_compare_fusion.2, bf16[128,32,128]{0,2,1:T(8,128)(2,1)} %fusion.35, bf16[128,32,128]{0,2,1:T(8,128)(2,1)S(1)} %bitcast.96), kind=kOutput, calls=%fused_computation.115 | convolution fusion | flops 136315008 | bytes 4227072 | tf_op jit(solution)/shard_map/jvp()/sub | solution.py:47
  175.9 2.6 %fusion.19 = (f32[32,128]{1,0:T(8,128)S(1)}, bf16[32,128,128]{1,2,0:T(8,128)(2,1)S(1)}) fusion(f32[32,128,128]{1,2,0:T(8,128)} %get-tuple-element.20, bf16[32,128,128]{1,2,0:T(8,128)(2,1)} %fusion.36, f32[32,128]{1,0:T(8,128)S(1)} %multiply_divide_fusion, f32[32,128]{1,0:T(8,128)S(1)} %get-tuple-element.19), kind=kLoop, calls=%fused_computation.27 | loop fusion | flops 3141632 | bytes 4243456 | tf_op jit(solution)/shard_map/transpose(jvp())/reduce_sum | solution.py:47
  178.8 0.8 fusion.37
  180.0 0.9 fusion.74
  181.3 0.9 fusion.82
  182.5 0.8 add_convert_fusion
  183.4 1.6 fusion.25
  185.0 0.9 fusion.43
  186.0 10.6 %fusion.11 = f32[128,2048]{1,0:T(8,128)} fusion(bf16[128,2,2048]{0,2,1:T(8,128)(2,1)S(1)} %bitcast.106, bf16[2,2048,3584]{2,1,0:T(8,128)(2,1)} %bitcast.112), kind=kOutput, calls=%fused_computation.21 | convolution fusion | flops 2147483648 | bytes 18874368 | tf_op jit(solution)/shard_map/tgc,gdc->td/dot_general | solution.py:140
  196.6 2.4 %scatter_custom_fusion.1 = f32[256,2048]{1,0:T(8,128)S(1)} fusion(s32[128]{0:T(128)S(1)} %fusion.63, f32[128,2048]{1,0:T(8,128)} %fusion.11, f32[]{:T(128)} %constant.27.clone.1), kind=kCustom, calls=%fused_computation.56 | custom fusion | bytes 2097664 | tf_op jit(solution)/shard_map/scatter | solution.py:146
  199.2 1.5 convert_element_type.144
  200.7 5.5 %all-to-all-start.2 = ((bf16[128,2,2048]{2,1,0:T(2,128)(2,1)}), bf16[128,2,2048]{2,1,0:T(2,128)(2,1)S(1)}, u32[]{:S(2)}, u32[]{:S(2)}) async-start(bf16[128,2,2048]{2,1,0:T(2,128)(2,1)} %convert_element_type.144), calls=%async_computation.2 | async-start | bytes 2097152 | tf_op jit(solution)/shard_map/all_to_all | solution.py:147
  206.7 0.8 reduce.4
  207.7 1.3 copy.70
  209.0 15.0 %all-to-all-done.2 = bf16[128,2,2048]{2,1,0:T(2,128)(2,1)S(1)} async-done(((bf16[128,2,2048]{2,1,0:T(2,128)(2,1)}), bf16[128,2,2048]{2,1,0:T(2,128)(2,1)S(1)}, u32[]{:S(2)}, u32[]{:S(2)}) %all-to-all-start.2) | async-done | bytes 1048608 | tf_op jit(solution)/shard_map/all_to_all | solution.py:147
  224.4 1.0 fusion.57
  (56 shorter events, 7.3 us)
Async XLA Ops:
  7.2 111.2 %all-gather.2.cloned.1.call-start = ((), (), s32[]{:S(2)}) async-start(), calls=%async_computation.3 | async-start | bytes 29589504 | tf_op jit(solution)/shard_map/all_gather | solution.py:92
  19.3 20.9 %all-to-all-start = ((s32[128,1,2]{2,1,0:T(1,128)}), s32[128,1,2]{2,1,0:T(1,128)S(1)}, u32[]{:S(2)}, u32[]{:S(2)}) async-start(s32[128,1,2]{2,1,0:T(1,128)} %bitcast.15), calls=%async_computation | async-start | bytes 131072 | tf_op jit(solution)/shard_map/all_to_all | solution.py:127
  128.4 1.7 copy-start.9
  130.1 2.6 %copy-start.8 = (bf16[4,2048]{1,0:T(4,128)(2,1)}, bf16[4,2048]{1,0:T(4,128)(2,1)S(1)}, u32[]{:S(2)}) copy-start(bf16[4,2048]{1,0:T(4,128)(2,1)S(1)} %multiply_convert_fusion) | copy-start | bytes 49156
  130.7 9.3 %copy-start.6 = (bf16[1,128,4096]{2,1,0:T(8,128)(2,1)S(1)}, bf16[1,128,4096]{2,1,0:T(8,128)(2,1)}, u32[]{:S(2)}) copy-start(bf16[1,128,4096]{2,1,0:T(8,128)(2,1)} %param.21) | copy-start | bytes 3145732
  132.7 8.0 %copy-start.10 = (s32[1,128,1]{1,2,0:T(1,128)S(1)}, s32[1,128,1]{1,2,0:T(1,128)}, u32[]{:S(2)}) copy-start(s32[1,128,1]{1,2,0:T(1,128)} %param.19) | copy-start | bytes 1540
  132.7 25.1 %all-to-all-start.1 = ((bf16[128,2,2048]{2,1,0:T(2,128)(2,1)}), bf16[128,2,2048]{2,1,0:T(2,128)(2,1)S(1)}, u32[]{:S(2)}, u32[]{:S(2)}) async-start(bf16[128,2,2048]{2,1,0:T(2,128)(2,1)} %copy.54), calls=%async_computation.1 | async-start | bytes 2097152 | tf_op jit(solution)/shard_map/all_to_all | solution.py:129
  167.4 1.2 copy-start.7
  169.4 1.5 copy-start
  175.9 2.6 %copy-start.2 = (bf16[32,128,128]{1,2,0:T(8,128)(2,1)S(1)}, bf16[32,128,128]{1,2,0:T(8,128)(2,1)}, u32[]{:S(2)}) copy-start(bf16[32,128,128]{1,2,0:T(8,128)(2,1)} %fusion.36) | copy-start | bytes 3145732
  175.9 2.9 %copy-start.4 = (f32[32,128,128]{1,2,0:T(8,128)S(1)}, f32[32,128,128]{1,2,0:T(8,128)}, u32[]{:S(2)}) copy-start(f32[32,128,128]{1,2,0:T(8,128)} %get-tuple-element.20) | copy-start | bytes 6291460
  178.8 1.2 copy-start.5
  181.3 1.2 copy-start.1
  199.2 8.5 %copy-start.3 = (bf16[128,4096]{0,1:T(8,128)(2,1)S(1)}, bf16[128,4096]{0,1:T(8,128)(2,1)}, u32[]{:S(2)}) copy-start(bf16[128,4096]{0,1:T(8,128)(2,1)} %get-tuple-element.12) | copy-start | bytes 3145732
  200.7 23.3 %all-to-all-start.2 = ((bf16[128,2,2048]{2,1,0:T(2,128)(2,1)}), bf16[128,2,2048]{2,1,0:T(2,128)(2,1)S(1)}, u32[]{:S(2)}, u32[]{:S(2)}) async-start(bf16[128,2,2048]{2,1,0:T(2,128)(2,1)} %convert_element_type.144), calls=%async_computation.2 | async-start | bytes 2097152 | tf_op jit(solution)/shard_map/all_to_all | solution.py:147
Sparse Core Ops, SparseCore 0:
  15.1 103.1 all-gather.1

commit v4 on v2

--- a/solution.py
+++ b/solution.py
@@ -136,15 +136,20 @@
         lambda values: user_layer(values, user_gain, query_map), hidden
     )
     (grad_hidden,) = pull(cotangent[0])
-    grad_rows = jnp.einsum(
+    slot_of = (
+        position[None, :] == jnp.arange(devices * cap_slots, dtype=jnp.int32)[:, None]
+    ).astype(grad_hidden.dtype)
+    slot_grads = jnp.dot(slot_of, grad_hidden, preferred_element_type=jnp.float32).astype(
+        grad_hidden.dtype
+    )
+    outgoing = jnp.einsum(
         "tgc,gdc->td",
-        grad_hidden.reshape(grad_hidden.shape[0], groups, -1),
+        slot_grads.reshape(slot_grads.shape[0], groups, -1),
         adapter_halves,
         preferred_element_type=jnp.float32,
-    )
-    outgoing = jnp.zeros((devices * cap_slots, DI), jnp.float32).at[position].set(grad_rows)
+    ).astype(jnp.bfloat16)
     arrived = lax.all_to_all(
-        outgoing.reshape(devices, cap_slots, DI).astype(jnp.bfloat16),
+        outgoing.reshape(devices, cap_slots, DI),
         ("grp", "fsdp"),
         split_axis=0,
         concat_axis=0,

time: 228 us -> 227 us (level)
  matrix products: 40.8 us -> 43.8 us
  local copies, waits for them, and re-layouts: 31.5 us -> 29 us
    dot_general x1 -> x2, matrix products: 10.3 us -> 13.2 us  [the longest x1 10.9 us: per_device(): jnp.einsum('tgc,gdc->td', slot_grads.reshape(slot_grads.shape[0], groups,...]
    scatter x1 -> x0, local copies, waits for them, and re-layouts: 2.42 us -> none  [per_device(): jnp.zeros((devices * cap_slots, DI), jnp.float32).at[position]]
    unnamed x30 -> x28, local copies, waits for them, and re-layouts: 6.89 us -> 6.88 us
where the time goes in v4:
time: 227 us; the launch traced here: 226 us
  waiting for transfers between devices  106 us (47%)
  matrix products  43.8 us (19%)
  local copies, waits for them, and re-layouts  29 us (13%)
  starting transfers between devices  24.3 us (11%)
  between operations  14.4 us (6%)
  other arithmetic  8.46 us (4%)
    all_gather x1, waiting for transfers between devices, per_device(): lax.all_gather(jnp.concatenate(pieces, axis=1), ('grp', 'fsdp'), axis=0,...  76.3 us
    all_to_all x1, waiting for transfers between devices, per_device(): lax.all_to_all(outgoing.reshape(devices, cap_slots, DI), ('grp', 'fsdp'),...  15.1 us
    all_to_all x1, starting transfers between devices, per_device(): lax.all_to_all(request, ('grp', 'fsdp'), split_axis=0, concat_axis=0, til...  11.5 us
    dot_general x1, matrix products, per_device(): jnp.einsum('tgc,gdc->td', slot_grads.reshape(slot_grads.shape[0], groups,...  10.9 us
    transpose x2, local copies, waits for them, and re-layouts, per_device(): query_map = gathered[:, :, ends[3]:].reshape(groups, DI, -1, user_query.s...  10.8 us
    all_to_all x1, waiting for transfers between devices, per_device(): lax.all_to_all(request, ('grp', 'fsdp'), split_axis=0, concat_axis=0, til...  8.29 us
    dot_general x1, matrix products, per_device(): jnp.einsum('td,gdc->tgc', fetched, adapter_halves, preferred_element_type...  8.24 us
    all_to_all x1, starting transfers between devices, per_device(): lax.all_to_all(found, ('grp', 'fsdp'), split_axis=0, concat_axis=0, tiled...  7.26 us
  transfers between devices with their start and end apart: 4, of which 4 were waited for; matrix products, arithmetic and copies ran while one was open for 8% of the time, Pallas kernels for 0%

profile of v4, /device:TPU:1, one launch (start us, length us, event | category | flops | bytes accessed | tf_op | source)
XLA Modules:
  0.0 225.9 jit_solution(6471771580719833024)
XLA Ops:
  7.2 0.7 reshape.172
  7.9 0.7 constant_dynamic-update-slice_fusion.2
  8.7 0.7 constant_dynamic-update-slice_fusion.1
  9.4 0.8 dynamic-slice_dynamic-update-slice_fusion.1
  10.2 0.9 dynamic-slice_dynamic-update-slice_fusion
  11.2 0.7 copy-done.6
  11.9 0.7 fusion.68
  12.8 0.8 select_reduce_fusion
  13.6 0.7 fusion.72
  14.3 1.1 scatter_custom_fusion
  15.4 0.8 all_to_all.12
  16.1 11.5 %all-to-all-start = ((s32[128,1,2]{2,1,0:T(1,128)}), s32[128,1,2]{2,1,0:T(1,128)S(1)}, u32[]{:S(2)}, u32[]{:S(2)}) async-start(s32[128,1,2]{2,1,0:T(1,128)} %bitcast.15), calls=%async_computation | async-start | bytes 131072 | tf_op jit(solution)/shard_map/all_to_all | solution.py:126
  27.6 0.9 slice.24
  28.7 8.3 %all-to-all-done = s32[128,1,2]{2,1,0:T(1,128)S(1)} async-done(((s32[128,1,2]{2,1,0:T(1,128)}), s32[128,1,2]{2,1,0:T(1,128)S(1)}, u32[]{:S(2)}, u32[]{:S(2)}) %all-to-all-start) | async-done | bytes 1056 | tf_op jit(solution)/shard_map/all_to_all | solution.py:126
  37.1 76.3 %all-gather.2.cloned.1.call-done = bf16[4096,3456]{1,0:T(8,128)(2,1)} async-done(((bf16[32,3456]{1,0:T(8,128)(2,1)}), bf16[4096,3456]{1,0:T(8,128)(2,1)}) %all-gather.2.cloned.1.call-update) | async-done | bytes 28311568 | tf_op jit(solution)/shard_map/all_gather | solution.py:89
  113.4 4.6 %fusion.45 = bf16[2,1024,4]{1,2,0:T(4,128)(2,1)S(1)} fusion(bf16[2,2048,3456]{2,1,0:T(8,128)(2,1)} %bitcast.122, bf16[4,1,2048]{2,1,0:T(2,128)(2,1)S(1)} %slice.24), kind=kOutput, calls=%fused_computation.56 | convolution fusion | flops 33562624 | bytes 8421376 | tf_op jit(solution)/shard_map/id,gdc->igc/dot_general | solution.py:97
  118.0 5.3 %fusion.37 = bf16[1024,2,256]{0,2,1:T(8,128)(2,1)S(1)} fusion(bf16[1024,2048,1]{1,0,2:T(8,128)(2,1)} %bitcast.130, bf16[2,2048,3456]{2,1,0:T(8,128)(2,1)} %bitcast.123), kind=kOutput, calls=%fused_computation.49 | convolution fusion | flops 2148007936 | bytes 7340032 | tf_op jit(solution)/shard_map/td,gdc->tgc/dot_general | solution.py:92
  125.2 0.5 convolution_convert_fusion.1
  125.7 2.0 copy.55
  127.8 7.3 %all-to-all-start.1 = ((bf16[128,2,2048]{2,1,0:T(2,128)(2,1)}), bf16[128,2,2048]{2,1,0:T(2,128)(2,1)S(1)}, u32[]{:S(2)}, u32[]{:S(2)}) async-start(bf16[128,2,2048]{2,1,0:T(2,128)(2,1)} %copy.55), calls=%async_computation.1 | async-start | bytes 2097152 | tf_op jit(solution)/shard_map/all_to_all | solution.py:128
  135.0 0.7 copy.63
  135.8 1.3 slice_bitcast_fusion
  137.1 9.5 %copy.57 = bf16[2048,1,2,128]{3,2,0,1:T(2,128)(2,1)} copy(bf16[2048,1,2,128]{3,0,2,1:T(8,128)(2,1)S(1)} %slice_bitcast_fusion) | data formatting | bytes 2097152 | tf_op jit(solution)/shard_map/transpose | solution.py:104
  146.5 6.3 %all-to-all-done.1 = bf16[128,2,2048]{2,1,0:T(2,128)(2,1)S(1)} async-done(((bf16[128,2,2048]{2,1,0:T(2,128)(2,1)}), bf16[128,2,2048]{2,1,0:T(2,128)(2,1)S(1)}, u32[]{:S(2)}, u32[]{:S(2)}) %all-to-all-start.1) | async-done | bytes 1048608 | tf_op jit(solution)/shard_map/all_to_all | solution.py:128
  153.3 0.9 gather_fusion
  154.2 8.2 %fusion.11 = bf16[128,2,2048]{2,0,1:T(8,128)(2,1)S(1)} fusion(bf16[2,2048,3456]{2,1,0:T(8,128)(2,1)} %bitcast.125, bf16[128,2048]{1,0:T(8,128)(2,1)S(1)} %gather_fusion, pred[128]{0:T(512)(128)(4,1)S(1)} %get-tuple-element.9), kind=kOutput, calls=%fused_computation.20 | convolution fusion | flops 2148270080 | bytes 18350208 | tf_op jit(solution)/shard_map/td,gdc->tgc/dot_general | solution.py:131
  162.5 0.7 copy.56
  163.1 0.6 fusion.24
  163.7 0.9 fusion.26
  164.7 1.5 fusion.41
  166.2 1.5 fusion.40
  167.7 3.5 %fusion.87 = (f32[32,128]{1,0:T(8,128)S(1)}, f32[32,128,128]{1,2,0:T(8,128)}) fusion(pred[128,128]{0,1:T(8,128)(4,1)S(1)} %iota_compare_fusion.4, bf16[128,32,128]{0,2,1:T(8,128)(2,1)} %fusion.40, bf16[128,32,128]{0,2,1:T(8,128)(2,1)S(1)} %bitcast.108), kind=kOutput, calls=%fused_computation.118 | convolution fusion | flops 136315008 | bytes 4227072 | tf_op jit(solution)/shard_map/jvp()/sub | solution.py:47
  171.2 2.6 %fusion.22 = (f32[32,128]{1,0:T(8,128)S(1)}, bf16[32,128,128]{1,2,0:T(8,128)(2,1)S(1)}) fusion(f32[32,128,128]{1,2,0:T(8,128)} %get-tuple-element.22, bf16[32,128,128]{1,2,0:T(8,128)(2,1)} %fusion.41, f32[32,128]{1,0:T(8,128)S(1)} %multiply_divide_fusion, f32[32,128]{1,0:T(8,128)S(1)} %get-tuple-element.21), kind=kLoop, calls=%fused_computation.28 | loop fusion | flops 3141632 | bytes 4243456 | tf_op jit(solution)/shard_map/transpose(jvp())/reduce_sum | solution.py:47
  174.1 0.8 fusion.42
  175.3 0.9 fusion.83
  176.1 0.5 fusion.90
  176.6 0.9 fusion.91
  177.8 0.8 add_convert_fusion
  178.7 0.9 fusion.28
  179.6 2.3 %convolution_convert_fusion = bf16[256,4096]{1,0:T(8,128)(2,1)} fusion(bf16[128,4096]{0,1:T(8,128)(2,1)S(1)} %bitcast.105, bf16[128,4096]{0,1:T(8,128)(2,1)S(1)} %bitcast.116, bf16[1,128,4096]{1,2,0:T(8,128)(2,1)S(1)} %copy.63, f32[128]{0:T(128)S(1)} %multiply_multiply_fusion, f32[4096]{0:T(1024)S(1)} %copy-done.7, f32[128]{0:T(128)S(1)} %fusion.75, ...), kind=kOutput, calls=%fused_computation.10 | convolution fusion | flops 274235392 | bytes 5260800 | tf_op jit(solution)/shard_map/dot_general | solution.py:142
  181.9 10.9 %fusion.14 = bf16[256,2048]{1,0:T(8,128)(2,1)S(1)} fusion(bf16[2,2048,3456]{2,1,0:T(8,128)(2,1)} %bitcast.126, bf16[32,2,8,2048]{3,2,1,0:T(8,128)(2,1)} %bitcast.118), kind=kOutput, calls=%fused_computation.21 | convolution fusion | flops 4295491584 | bytes 19922944 | tf_op jit(solution)/shard_map/tgc,gdc->td/dot_general | solution.py:145
  192.8 1.5 reshape.185
  194.4 5.5 %all-to-all-start.2 = ((bf16[128,2,2048]{2,1,0:T(2,128)(2,1)}), bf16[128,2,2048]{2,1,0:T(2,128)(2,1)S(1)}, u32[]{:S(2)}, u32[]{:S(2)}) async-start(bf16[128,2,2048]{2,1,0:T(2,128)(2,1)} %reshape.185), calls=%async_computation.2 | async-start | bytes 2097152 | tf_op jit(solution)/shard_map/all_to_all | solution.py:151
  199.9 0.5 broadcast.138
  200.4 0.8 reduce.4
  201.3 1.3 copy.72
  202.6 15.1 %all-to-all-done.2 = bf16[128,2,2048]{2,1,0:T(2,128)(2,1)S(1)} async-done(((bf16[128,2,2048]{2,1,0:T(2,128)(2,1)}), bf16[128,2,2048]{2,1,0:T(2,128)(2,1)S(1)}, u32[]{:S(2)}, u32[]{:S(2)}) %all-to-all-start.2) | async-done | bytes 1048608 | tf_op jit(solution)/shard_map/all_to_all | solution.py:151
  218.1 1.0 fusion.65
  (48 shorter events, 4.4 us)
Async XLA Ops:
  7.2 106.2 %all-gather.2.cloned.1.call-start = ((), (), s32[]{:S(2)}) async-start(), calls=%async_computation.3 | async-start | bytes 28532736 | tf_op jit(solution)/shard_map/all_gather | solution.py:89
  11.1 0.7 copy-start.6
  16.1 20.9 %all-to-all-start = ((s32[128,1,2]{2,1,0:T(1,128)}), s32[128,1,2]{2,1,0:T(1,128)S(1)}, u32[]{:S(2)}, u32[]{:S(2)}) async-start(s32[128,1,2]{2,1,0:T(1,128)} %bitcast.15), calls=%async_computation | async-start | bytes 131072 | tf_op jit(solution)/shard_map/all_to_all | solution.py:126
  123.4 1.7 copy-start.9
  125.2 2.6 %copy-start.8 = (bf16[4,2048]{1,0:T(4,128)(2,1)}, bf16[4,2048]{1,0:T(4,128)(2,1)S(1)}, u32[]{:S(2)}) copy-start(bf16[4,2048]{1,0:T(4,128)(2,1)S(1)} %multiply_convert_fusion) | copy-start | bytes 49156
  125.7 9.3 %copy-start.5 = (bf16[1,128,4096]{2,1,0:T(8,128)(2,1)S(1)}, bf16[1,128,4096]{2,1,0:T(8,128)(2,1)}, u32[]{:S(2)}) copy-start(bf16[1,128,4096]{2,1,0:T(8,128)(2,1)} %param.21) | copy-start | bytes 3145732
  127.8 8.0 %copy-start.10 = (s32[1,128,1]{1,2,0:T(1,128)S(1)}, s32[1,128,1]{1,2,0:T(1,128)}, u32[]{:S(2)}) copy-start(s32[1,128,1]{1,2,0:T(1,128)} %param.19) | copy-start | bytes 1540
  127.8 25.1 %all-to-all-start.1 = ((bf16[128,2,2048]{2,1,0:T(2,128)(2,1)}), bf16[128,2,2048]{2,1,0:T(2,128)(2,1)S(1)}, u32[]{:S(2)}, u32[]{:S(2)}) async-start(bf16[128,2,2048]{2,1,0:T(2,128)(2,1)} %copy.55), calls=%async_computation.1 | async-start | bytes 2097152 | tf_op jit(solution)/shard_map/all_to_all | solution.py:128
  162.5 1.2 copy-start.7
  164.6 1.5 copy-start
  171.2 2.6 %copy-start.2 = (bf16[32,128,128]{1,2,0:T(8,128)(2,1)S(1)}, bf16[32,128,128]{1,2,0:T(8,128)(2,1)}, u32[]{:S(2)}) copy-start(bf16[32,128,128]{1,2,0:T(8,128)(2,1)} %fusion.41) | copy-start | bytes 3145732
  171.2 2.9 %copy-start.3 = (f32[32,128,128]{1,2,0:T(8,128)S(1)}, f32[32,128,128]{1,2,0:T(8,128)}, u32[]{:S(2)}) copy-start(f32[32,128,128]{1,2,0:T(8,128)} %get-tuple-element.22) | copy-start | bytes 6291460
  174.1 1.2 copy-start.4
  176.6 1.2 copy-start.1
  194.4 23.3 %all-to-all-start.2 = ((bf16[128,2,2048]{2,1,0:T(2,128)(2,1)}), bf16[128,2,2048]{2,1,0:T(2,128)(2,1)S(1)}, u32[]{:S(2)}, u32[]{:S(2)}) async-start(bf16[128,2,2048]{2,1,0:T(2,128)(2,1)} %reshape.185), calls=%async_computation.2 | async-start | bytes 2097152 | tf_op jit(solution)/shard_map/all_to_all | solution.py:151
Sparse Core Ops, SparseCore 0:
  12.0 101.3 all-gather.1

commit v5 on v4

--- a/solution.py
+++ b/solution.py
@@ -1,6 +1,8 @@
 import jax
 import jax.numpy as jnp
 from jax import lax
+from jax.experimental import pallas as pl
+from jax.experimental.pallas import tpu as pltpu
 from jax.sharding import PartitionSpec as P
 
 DI = 2048
@@ -47,6 +49,37 @@
     weights = stored(jax.nn.softmax(scores, axis=-1)).astype(jnp.float32)
     mixed = jnp.einsum("hts,shd->thd", weights, heads).reshape(length_total, UHEADS * UHD)
     return (hidden.astype(jnp.float32) + mixed).astype(jnp.bfloat16)
+
+
+def _pack_halves(*refs):
+    sources, out, sems = refs[:-2], refs[-2], refs[-1]
+    side = lax.axis_index("grp")
+    copies, column = [], 0
+    for i, src in enumerate(sources):
+        if i == len(sources) - 1:
+            rows = src.shape[0] // 2
+            width = src.shape[1]
+            window = src.at[pl.ds(side * rows, rows), :]
+        else:
+            width = src.shape[1] // 2
+            window = src.at[:, pl.ds(side * width, width)]
+        copy = pltpu.make_async_copy(window, out.at[:, pl.ds(column, width)], sems.at[i])
+        copy.start()
+        copies.append(copy)
+        column += width
+    for copy in copies:
+        copy.wait()
+
+
+def pack_halves(sources):
+    total = sum(w.shape[1] // 2 for w in sources[:-1]) + sources[-1].shape[1]
+    return pl.pallas_call(
+        _pack_halves,
+        out_shape=jax.ShapeDtypeStruct((sources[0].shape[0], total), sources[0].dtype),
+        in_specs=[pl.BlockSpec(memory_space=pl.ANY)] * len(sources),
+        out_specs=pl.BlockSpec(memory_space=pl.ANY),
+        scratch_shapes=[pltpu.SemaphoreType.DMA((len(sources),))],
+    )(*sources)
 
 
 def serve_rows(requests, lookup_matrix):
@@ -79,15 +112,11 @@
     last_row = item_states[:, ILEN - 1, :]
     side = lax.axis_index("grp")
 
-    def half(w, rows=None):
-        w = w if rows is None else w.reshape(rows, -1)
-        return lax.dynamic_slice_in_dim(w, side * (w.shape[1] // 2), w.shape[1] // 2, axis=1)
-
-    pieces = [half(w_key), half(w_value), half(w_query), half(w_adapt), half(user_query, w_key.shape[0])]
-    widths = [p.shape[1] for p in pieces]
+    sources = [w_key, w_value, w_query, w_adapt, user_query]
+    widths = [w.shape[1] // 2 for w in sources[:-1]] + [user_query.shape[1]]
     ends = [sum(widths[: i + 1]) for i in range(len(widths))]
     gathered = lax.all_gather(
-        jnp.concatenate(pieces, axis=1), ("grp", "fsdp"), axis=0, tiled=True
+        pack_halves(sources), ("grp", "fsdp"), axis=0, tiled=True
     ).reshape(groups, DI, ends[-1])
     kv_sum = jnp.einsum(
         "td,gdc->tgc", flat, gathered[:, :, : ends[1]], preferred_element_type=jnp.float32
@@ -100,8 +129,8 @@
     adapter_halves = gathered[:, :, ends[2] : ends[3]]
     query_map = (
         gathered[:, :, ends[3] :]
-        .reshape(groups, DI, -1, user_query.shape[1])
-        .transpose(1, 2, 0, 3)
+        .reshape(groups, shards, -1, user_query.shape[1])
+        .transpose(1, 0, 2, 3)
         .reshape(-1, user_query.shape[1])
     )
     item_embed = item_pool(

time: 227 us -> 230 us (1.013)
  local copies, waits for them, and re-layouts: 29 us -> 16.1 us
  waiting for transfers between devices: 106 us -> 114 us
  Pallas kernels: 0 us -> 7.86 us
    transpose x2 -> x0, local copies, waits for them, and re-layouts: 10.8 us -> none  [per_device(): query_map = gathered[:, :, ends[3]:].reshape(groups, DI, -1, user_query.s...]
    all_to_all x1, waiting for transfers between devices: 6.32 us -> 14.7 us  [per_device(): lax.all_to_all(found, ('grp', 'fsdp'), split_axis=0, concat_axis=0, tiled...]
    pallas_call x0 -> x1, Pallas kernels: none -> 7.86 us  [pack_halves(): pl.pallas_call(_pack_halves, out_shape=jax.ShapeDtypeStruct((sources[0].s...]
    unnamed x28 -> x22, local copies, waits for them, and re-layouts: 6.88 us -> 3.04 us
  transfers between devices with their start and end apart: 4 -> 4, of which waited for: 4 -> 4; matrix products, arithmetic and copies ran while one was open for 8% -> 5% of each run, Pallas kernels for 0% -> 0%
where the time goes in v5:
time: 230 us; the launch traced here: 229 us
  waiting for transfers between devices  114 us (50%)
  matrix products  43.8 us (19%)
  starting transfers between devices  24.3 us (11%)
  local copies, waits for them, and re-layouts  16.1 us (7%)
  between operations  14.4 us (6%)
  other arithmetic  8.23 us (4%)
  Pallas kernels  7.86 us (3%)
    all_gather x1, waiting for transfers between devices, per_device(): lax.all_gather(pack_halves(sources), ('grp', 'fsdp'), axis=0, tiled=True)  76.3 us
    all_to_all x1, waiting for transfers between devices, per_device(): lax.all_to_all(outgoing.reshape(devices, cap_slots, DI), ('grp', 'fsdp'),...  15.1 us
    all_to_all x1, waiting for transfers between devices, per_device(): lax.all_to_all(found, ('grp', 'fsdp'), split_axis=0, concat_axis=0, tiled...  14.7 us
    all_to_all x1, starting transfers between devices, per_device(): lax.all_to_all(request, ('grp', 'fsdp'), split_axis=0, concat_axis=0, til...  11.5 us
    dot_general x1, matrix products, per_device(): jnp.einsum('tgc,gdc->td', slot_grads.reshape(slot_grads.shape[0], groups,...  10.9 us
    all_to_all x1, waiting for transfers between devices, per_device(): lax.all_to_all(request, ('grp', 'fsdp'), split_axis=0, concat_axis=0, til...  8.29 us
    dot_general x1, matrix products, per_device(): jnp.einsum('td,gdc->tgc', fetched, adapter_halves, preferred_element_type...  8.24 us
    pallas_call x1, Pallas kernels, pack_halves(): pl.pallas_call(_pack_halves, out_shape=jax.ShapeDtypeStruct((sources[0].s...  7.86 us
  transfers between devices with their start and end apart: 4, of which 4 were waited for; matrix products, arithmetic and copies ran while one was open for 5% of the time, Pallas kernels for 0%

profile of v5, /device:TPU:1, one launch (start us, length us, event | category | flops | bytes accessed | tf_op | source)
XLA Modules:
  0.0 229.0 jit_solution(6419174988448187458)
XLA Ops:
  7.2 7.9 %shard_map.130 = bf16[32,3456]{1,0:T(8,128)(2,1)} custom-call(bf16[32,256]{1,0:T(8,128)(2,1)} %refs_0_.1, bf16[32,256]{1,0:T(8,128)(2,1)} %refs_1_.1, bf16[32,2048]{1,0:T(8,128)(2,1)} %refs_2_.1, bf16[32,4096]{1,0:T(8,128)(2,1)} %refs_3_.1, bf16[64,128]{1,0:T(8,128)(2,1)} %refs_4_.1), custom_call_target="tpu_custom_call" | custom-call | tf_op jit(solution)/shard_map/pallas_call | solution.py:76
  15.1 0.7 fusion.68
  16.0 0.8 select_reduce_fusion
  16.8 0.7 fusion.72
  17.5 1.1 scatter_custom_fusion
  18.6 0.8 all_to_all.12
  19.4 11.5 %all-to-all-start = ((s32[128,1,2]{2,1,0:T(1,128)}), s32[128,1,2]{2,1,0:T(1,128)S(1)}, u32[]{:S(2)}, u32[]{:S(2)}) async-start(s32[128,1,2]{2,1,0:T(1,128)} %bitcast.15), calls=%async_computation | async-start | bytes 131072 | tf_op jit(solution)/shard_map/all_to_all | solution.py:155
  30.9 0.9 slice.24
  32.0 8.3 %all-to-all-done = s32[128,1,2]{2,1,0:T(1,128)S(1)} async-done(((s32[128,1,2]{2,1,0:T(1,128)}), s32[128,1,2]{2,1,0:T(1,128)S(1)}, u32[]{:S(2)}, u32[]{:S(2)}) %all-to-all-start) | async-done | bytes 1056 | tf_op jit(solution)/shard_map/all_to_all | solution.py:155
  40.3 76.3 %all-gather.2.cloned.1.call-done = bf16[4096,3456]{1,0:T(8,128)(2,1)} async-done(((bf16[32,3456]{1,0:T(8,128)(2,1)}), bf16[4096,3456]{1,0:T(8,128)(2,1)}) %all-gather.2.cloned.1.call-update) | async-done | bytes 28311568 | tf_op jit(solution)/shard_map/all_gather | solution.py:118
  116.6 4.6 %fusion.45 = bf16[2,1024,4]{1,2,0:T(4,128)(2,1)S(1)} fusion(bf16[2,2048,3456]{2,1,0:T(8,128)(2,1)} %bitcast.122, bf16[4,1,2048]{2,1,0:T(2,128)(2,1)S(1)} %slice.24), kind=kOutput, calls=%fused_computation.56 | convolution fusion | flops 33562624 | bytes 8421376 | tf_op jit(solution)/shard_map/id,gdc->igc/dot_general | solution.py:126
  121.3 5.3 %fusion.37 = bf16[1024,2,256]{0,2,1:T(8,128)(2,1)S(1)} fusion(bf16[1024,2048,1]{1,0,2:T(8,128)(2,1)} %bitcast.130, bf16[2,2048,3456]{2,1,0:T(8,128)(2,1)} %bitcast.123), kind=kOutput, calls=%fused_computation.49 | convolution fusion | flops 2148007936 | bytes 7340032 | tf_op jit(solution)/shard_map/td,gdc->tgc/dot_general | solution.py:121
  126.7 0.4 reshape.173
  127.0 0.4 reshape.172
  128.4 0.5 convolution_convert_fusion.1
  129.0 2.0 copy.55
  131.0 7.3 %all-to-all-start.1 = ((bf16[128,2,2048]{2,1,0:T(2,128)(2,1)}), bf16[128,2,2048]{2,1,0:T(2,128)(2,1)S(1)}, u32[]{:S(2)}, u32[]{:S(2)}) async-start(bf16[128,2,2048]{2,1,0:T(2,128)(2,1)} %copy.55), calls=%async_computation.1 | async-start | bytes 2097152 | tf_op jit(solution)/shard_map/all_to_all | solution.py:157
  138.3 0.7 copy.63
  139.0 1.3 slice.38
  140.3 1.1 copy.57
  141.4 14.7 %all-to-all-done.1 = bf16[128,2,2048]{2,1,0:T(2,128)(2,1)S(1)} async-done(((bf16[128,2,2048]{2,1,0:T(2,128)(2,1)}), bf16[128,2,2048]{2,1,0:T(2,128)(2,1)S(1)}, u32[]{:S(2)}, u32[]{:S(2)}) %all-to-all-start.1) | async-done | bytes 1048608 | tf_op jit(solution)/shard_map/all_to_all | solution.py:157
  156.1 0.4 reshape.175
  156.5 0.9 gather_fusion
  157.5 8.2 %fusion.11 = bf16[128,2,2048]{2,0,1:T(8,128)(2,1)S(1)} fusion(bf16[2,2048,3456]{2,1,0:T(8,128)(2,1)} %bitcast.125, bf16[128,2048]{1,0:T(8,128)(2,1)S(1)} %gather_fusion, pred[128]{0:T(512)(128)(4,1)S(1)} %get-tuple-element.9), kind=kOutput, calls=%fused_computation.20 | convolution fusion | flops 2148270080 | bytes 18350208 | tf_op jit(solution)/shard_map/td,gdc->tgc/dot_general | solution.py:160
  165.7 0.7 copy.56
  166.4 0.6 fusion.24
  167.0 0.7 fusion.26
  167.7 1.5 fusion.41
  169.2 1.5 fusion.40
  170.7 3.5 %fusion.87 = (f32[32,128]{1,0:T(8,128)S(1)}, f32[32,128,128]{1,2,0:T(8,128)}) fusion(pred[128,128]{0,1:T(8,128)(4,1)S(1)} %iota_compare_fusion.4, bf16[128,32,128]{0,2,1:T(8,128)(2,1)} %fusion.40, bf16[128,32,128]{0,2,1:T(8,128)(2,1)S(1)} %bitcast.107), kind=kOutput, calls=%fused_computation.112 | convolution fusion | flops 136315008 | bytes 4227072 | tf_op jit(solution)/shard_map/jvp()/sub | solution.py:49
  174.2 2.6 %fusion.22 = (f32[32,128]{1,0:T(8,128)S(1)}, bf16[32,128,128]{1,2,0:T(8,128)(2,1)S(1)}) fusion(f32[32,128,128]{1,2,0:T(8,128)} %get-tuple-element.22, bf16[32,128,128]{1,2,0:T(8,128)(2,1)} %fusion.41, f32[32,128]{1,0:T(8,128)S(1)} %multiply_divide_fusion, f32[32,128]{1,0:T(8,128)S(1)} %get-tuple-element.21), kind=kLoop, calls=%fused_computation.28 | loop fusion | flops 3141632 | bytes 4243456 | tf_op jit(solution)/shard_map/transpose(jvp())/reduce_sum | solution.py:49
  177.1 0.8 fusion.42
  177.9 0.4 copy-done.4
  178.3 0.9 fusion.83
  179.2 0.5 fusion.90
  179.6 0.8 fusion.91
  180.9 0.8 add_convert_fusion
  181.7 0.9 fusion.28
  182.6 2.3 %convolution_convert_fusion = bf16[256,4096]{1,0:T(8,128)(2,1)} fusion(bf16[128,4096]{0,1:T(8,128)(2,1)S(1)} %bitcast.104, bf16[128,4096]{0,1:T(8,128)(2,1)S(1)} %bitcast.115, bf16[1,128,4096]{1,2,0:T(8,128)(2,1)S(1)} %copy.63, f32[128]{0:T(128)S(1)} %multiply_multiply_fusion, f32[4096]{0:T(1024)S(1)} %copy-done.6, f32[128]{0:T(128)S(1)} %fusion.75, ...), kind=kOutput, calls=%fused_computation.10 | convolution fusion | flops 274235392 | bytes 5260800 | tf_op jit(solution)/shard_map/dot_general | solution.py:171
  184.9 10.9 %fusion.14 = bf16[256,2048]{1,0:T(8,128)(2,1)S(1)} fusion(bf16[2,2048,3456]{2,1,0:T(8,128)(2,1)} %bitcast.126, bf16[32,2,8,2048]{3,2,1,0:T(8,128)(2,1)} %bitcast.118), kind=kOutput, calls=%fused_computation.21 | convolution fusion | flops 4295491584 | bytes 19922944 | tf_op jit(solution)/shard_map/tgc,gdc->td/dot_general | solution.py:174
  195.9 1.5 reshape.181
  197.4 5.5 %all-to-all-start.2 = ((bf16[128,2,2048]{2,1,0:T(2,128)(2,1)}), bf16[128,2,2048]{2,1,0:T(2,128)(2,1)S(1)}, u32[]{:S(2)}, u32[]{:S(2)}) async-start(bf16[128,2,2048]{2,1,0:T(2,128)(2,1)} %reshape.181), calls=%async_computation.2 | async-start | bytes 2097152 | tf_op jit(solution)/shard_map/all_to_all | solution.py:180
  202.9 0.5 broadcast.138
  203.4 0.8 reduce.4
  204.4 1.3 copy.72
  205.7 15.1 %all-to-all-done.2 = bf16[128,2,2048]{2,1,0:T(2,128)(2,1)S(1)} async-done(((bf16[128,2,2048]{2,1,0:T(2,128)(2,1)}), bf16[128,2,2048]{2,1,0:T(2,128)(2,1)S(1)}, u32[]{:S(2)}, u32[]{:S(2)}) %all-to-all-start.2) | async-done | bytes 1048608 | tf_op jit(solution)/shard_map/all_to_all | solution.py:180
  220.7 0.4 reshape.182
  221.1 1.0 fusion.65
  (41 shorter events, 2.4 us)
Async XLA Ops:
  7.2 109.5 %all-gather.2.cloned.1.call-start = ((), (), s32[]{:S(2)}) async-start(), calls=%async_computation.3 | async-start | bytes 28532736 | tf_op jit(solution)/shard_map/all_gather | solution.py:118
  19.4 20.9 %all-to-all-start = ((s32[128,1,2]{2,1,0:T(1,128)}), s32[128,1,2]{2,1,0:T(1,128)S(1)}, u32[]{:S(2)}, u32[]{:S(2)}) async-start(s32[128,1,2]{2,1,0:T(1,128)} %bitcast.15), calls=%async_computation | async-start | bytes 131072 | tf_op jit(solution)/shard_map/all_to_all | solution.py:155
  126.7 1.7 copy-start.8
  128.4 2.6 %copy-start.7 = (bf16[4,2048]{1,0:T(4,128)(2,1)}, bf16[4,2048]{1,0:T(4,128)(2,1)S(1)}, u32[]{:S(2)}) copy-start(bf16[4,2048]{1,0:T(4,128)(2,1)S(1)} %multiply_convert_fusion) | copy-start | bytes 49156
  128.9 9.3 %copy-start.5 = (bf16[1,128,4096]{2,1,0:T(8,128)(2,1)S(1)}, bf16[1,128,4096]{2,1,0:T(8,128)(2,1)}, u32[]{:S(2)}) copy-start(bf16[1,128,4096]{2,1,0:T(8,128)(2,1)} %param.21) | copy-start | bytes 3145732
  131.0 8.0 %copy-start.9 = (s32[1,128,1]{1,2,0:T(1,128)S(1)}, s32[1,128,1]{1,2,0:T(1,128)}, u32[]{:S(2)}) copy-start(s32[1,128,1]{1,2,0:T(1,128)} %param.19) | copy-start | bytes 1540
  131.0 25.1 %all-to-all-start.1 = ((bf16[128,2,2048]{2,1,0:T(2,128)(2,1)}), bf16[128,2,2048]{2,1,0:T(2,128)(2,1)S(1)}, u32[]{:S(2)}, u32[]{:S(2)}) async-start(bf16[128,2,2048]{2,1,0:T(2,128)(2,1)} %copy.55), calls=%async_computation.1 | async-start | bytes 2097152 | tf_op jit(solution)/shard_map/all_to_all | solution.py:157
  165.7 1.2 copy-start.6
  167.7 1.5 copy-start
  174.2 2.6 %copy-start.2 = (bf16[32,128,128]{1,2,0:T(8,128)(2,1)S(1)}, bf16[32,128,128]{1,2,0:T(8,128)(2,1)}, u32[]{:S(2)}) copy-start(bf16[32,128,128]{1,2,0:T(8,128)(2,1)} %fusion.41) | copy-start | bytes 3145732
  174.2 2.9 %copy-start.3 = (f32[32,128,128]{1,2,0:T(8,128)S(1)}, f32[32,128,128]{1,2,0:T(8,128)}, u32[]{:S(2)}) copy-start(f32[32,128,128]{1,2,0:T(8,128)} %get-tuple-element.22) | copy-start | bytes 6291460
  177.1 1.2 copy-start.4
  179.6 1.2 copy-start.1
  197.4 23.3 %all-to-all-start.2 = ((bf16[128,2,2048]{2,1,0:T(2,128)(2,1)}), bf16[128,2,2048]{2,1,0:T(2,128)(2,1)S(1)}, u32[]{:S(2)}, u32[]{:S(2)}) async-start(bf16[128,2,2048]{2,1,0:T(2,128)(2,1)} %reshape.181), calls=%async_computation.2 | async-start | bytes 2097152 | tf_op jit(solution)/shard_map/all_to_all | solution.py:180
Sparse Core Ops, SparseCore 0:
  15.2 101.3 all-gather.1

commit v6 on v5

--- a/solution.py
+++ b/solution.py
@@ -52,23 +52,19 @@
 
 
 def _pack_halves(*refs):
-    sources, out, sems = refs[:-2], refs[-2], refs[-1]
-    side = lax.axis_index("grp")
-    copies, column = [], 0
+    sources, out = refs[:-1], refs[-1]
+    first = lax.axis_index("grp") == 0
+    column = 0
     for i, src in enumerate(sources):
         if i == len(sources) - 1:
             rows = src.shape[0] // 2
             width = src.shape[1]
-            window = src.at[pl.ds(side * rows, rows), :]
+            low, high = src[:rows, :], src[rows:, :]
         else:
             width = src.shape[1] // 2
-            window = src.at[:, pl.ds(side * width, width)]
-        copy = pltpu.make_async_copy(window, out.at[:, pl.ds(column, width)], sems.at[i])
-        copy.start()
-        copies.append(copy)
+            low, high = src[:, :width], src[:, width:]
+        out[:, column : column + width] = jnp.where(first, low, high)
         column += width
-    for copy in copies:
-        copy.wait()
 
 
 def pack_halves(sources):
@@ -76,9 +72,6 @@
     return pl.pallas_call(
         _pack_halves,
         out_shape=jax.ShapeDtypeStruct((sources[0].shape[0], total), sources[0].dtype),
-        in_specs=[pl.BlockSpec(memory_space=pl.ANY)] * len(sources),
-        out_specs=pl.BlockSpec(memory_space=pl.ANY),
-        scratch_shapes=[pltpu.SemaphoreType.DMA((len(sources),))],
     )(*sources)
 
 

time: 230 us -> 226 us (0.983)
  Pallas kernels: 7.86 us -> 1.74 us
  waiting for transfers between devices: 114 us -> 117 us
    pallas_call x1, Pallas kernels: 7.86 us -> 1.74 us  [pack_halves(): pl.pallas_call(_pack_halves, out_shape=jax.ShapeDtypeStruct((sources[0].s...]
    all_gather x1, waiting for transfers between devices: 76.3 us -> 78.9 us  [per_device(): lax.all_gather(pack_halves(sources), ('grp', 'fsdp'), axis=0, tiled=True)]
where the time goes in v6:
time: 226 us; the launch traced here: 225 us
  waiting for transfers between devices  117 us (52%)
  matrix products  43.8 us (19%)
  starting transfers between devices  24.3 us (11%)
  local copies, waits for them, and re-layouts  16.1 us (7%)
  between operations  14.4 us (6%)
  other arithmetic  8.23 us (4%)
    all_gather x1, waiting for transfers between devices, per_device(): lax.all_gather(pack_halves(sources), ('grp', 'fsdp'), axis=0, tiled=True)  78.9 us
    all_to_all x1, waiting for transfers between devices, per_device(): lax.all_to_all(outgoing.reshape(devices, cap_slots, DI), ('grp', 'fsdp'),...  15.1 us
    all_to_all x1, waiting for transfers between devices, per_device(): lax.all_to_all(found, ('grp', 'fsdp'), split_axis=0, concat_axis=0, tiled...  14.7 us
    all_to_all x1, starting transfers between devices, per_device(): lax.all_to_all(request, ('grp', 'fsdp'), split_axis=0, concat_axis=0, til...  11.5 us
    dot_general x1, matrix products, per_device(): jnp.einsum('tgc,gdc->td', slot_grads.reshape(slot_grads.shape[0], groups,...  10.9 us
    all_to_all x1, waiting for transfers between devices, per_device(): lax.all_to_all(request, ('grp', 'fsdp'), split_axis=0, concat_axis=0, til...  8.29 us
    dot_general x1, matrix products, per_device(): jnp.einsum('td,gdc->tgc', fetched, adapter_halves, preferred_element_type...  8.24 us
    all_to_all x1, starting transfers between devices, per_device(): lax.all_to_all(found, ('grp', 'fsdp'), split_axis=0, concat_axis=0, tiled...  7.26 us
  transfers between devices with their start and end apart: 4, of which 4 were waited for; matrix products, arithmetic and copies ran while one was open for 5% of the time, Pallas kernels for 0%

profile of v6, /device:TPU:1, one launch (start us, length us, event | category | flops | bytes accessed | tf_op | source)
XLA Modules:
  0.0 225.4 jit_solution(12543890637233776888)
XLA Ops:
  7.2 1.7 shard_map.130
  9.0 0.7 fusion.68
  9.9 0.8 select_reduce_fusion
  10.7 0.7 fusion.72
  11.4 1.1 scatter_custom_fusion
  12.5 0.8 all_to_all.12
  13.3 11.5 %all-to-all-start = ((s32[128,1,2]{2,1,0:T(1,128)}), s32[128,1,2]{2,1,0:T(1,128)S(1)}, u32[]{:S(2)}, u32[]{:S(2)}) async-start(s32[128,1,2]{2,1,0:T(1,128)} %bitcast.15), calls=%async_computation | async-start | bytes 131072 | tf_op jit(solution)/shard_map/all_to_all | solution.py:148
  24.8 1.0 slice.24
  25.8 8.3 %all-to-all-done = s32[128,1,2]{2,1,0:T(1,128)S(1)} async-done(((s32[128,1,2]{2,1,0:T(1,128)}), s32[128,1,2]{2,1,0:T(1,128)S(1)}, u32[]{:S(2)}, u32[]{:S(2)}) %all-to-all-start) | async-done | bytes 1056 | tf_op jit(solution)/shard_map/all_to_all | solution.py:148
  34.2 78.9 %all-gather.2.cloned.1.call-done = bf16[4096,3456]{1,0:T(8,128)(2,1)} async-done(((bf16[32,3456]{1,0:T(8,128)(2,1)}), bf16[4096,3456]{1,0:T(8,128)(2,1)}) %all-gather.2.cloned.1.call-update) | async-done | bytes 28311568 | tf_op jit(solution)/shard_map/all_gather | solution.py:111
  113.1 4.6 %fusion.45 = bf16[2,1024,4]{1,2,0:T(4,128)(2,1)S(1)} fusion(bf16[2,2048,3456]{2,1,0:T(8,128)(2,1)} %bitcast.122, bf16[4,1,2048]{2,1,0:T(2,128)(2,1)S(1)} %slice.24), kind=kOutput, calls=%fused_computation.56 | convolution fusion | flops 33562624 | bytes 8421376 | tf_op jit(solution)/shard_map/id,gdc->igc/dot_general | solution.py:119
  117.8 5.3 %fusion.37 = bf16[1024,2,256]{0,2,1:T(8,128)(2,1)S(1)} fusion(bf16[1024,2048,1]{1,0,2:T(8,128)(2,1)} %bitcast.130, bf16[2,2048,3456]{2,1,0:T(8,128)(2,1)} %bitcast.123), kind=kOutput, calls=%fused_computation.49 | convolution fusion | flops 2148007936 | bytes 7340032 | tf_op jit(solution)/shard_map/td,gdc->tgc/dot_general | solution.py:114
  123.2 0.4 reshape.173
  123.5 0.4 reshape.172
  124.9 0.5 convolution_convert_fusion.1
  125.4 2.0 copy.55
  127.5 7.3 %all-to-all-start.1 = ((bf16[128,2,2048]{2,1,0:T(2,128)(2,1)}), bf16[128,2,2048]{2,1,0:T(2,128)(2,1)S(1)}, u32[]{:S(2)}, u32[]{:S(2)}) async-start(bf16[128,2,2048]{2,1,0:T(2,128)(2,1)} %copy.55), calls=%async_computation.1 | async-start | bytes 2097152 | tf_op jit(solution)/shard_map/all_to_all | solution.py:150
  134.8 0.7 copy.63
  135.5 1.3 slice.38
  136.8 1.1 copy.57
  137.9 14.7 %all-to-all-done.1 = bf16[128,2,2048]{2,1,0:T(2,128)(2,1)S(1)} async-done(((bf16[128,2,2048]{2,1,0:T(2,128)(2,1)}), bf16[128,2,2048]{2,1,0:T(2,128)(2,1)S(1)}, u32[]{:S(2)}, u32[]{:S(2)}) %all-to-all-start.1) | async-done | bytes 1048608 | tf_op jit(solution)/shard_map/all_to_all | solution.py:150
  152.6 0.4 reshape.175
  153.0 0.9 gather_fusion
  154.0 8.2 %fusion.11 = bf16[128,2,2048]{2,0,1:T(8,128)(2,1)S(1)} fusion(bf16[2,2048,3456]{2,1,0:T(8,128)(2,1)} %bitcast.125, bf16[128,2048]{1,0:T(8,128)(2,1)S(1)} %gather_fusion, pred[128]{0:T(512)(128)(4,1)S(1)} %get-tuple-element.9), kind=kOutput, calls=%fused_computation.20 | convolution fusion | flops 2148270080 | bytes 18350208 | tf_op jit(solution)/shard_map/td,gdc->tgc/dot_general | solution.py:153
  162.2 0.7 copy.56
  162.9 0.6 fusion.24
  163.5 0.7 fusion.26
  164.2 1.5 fusion.41
  165.7 1.5 fusion.40
  167.2 3.5 %fusion.87 = (f32[32,128]{1,0:T(8,128)S(1)}, f32[32,128,128]{1,2,0:T(8,128)}) fusion(pred[128,128]{0,1:T(8,128)(4,1)S(1)} %iota_compare_fusion.4, bf16[128,32,128]{0,2,1:T(8,128)(2,1)} %fusion.40, bf16[128,32,128]{0,2,1:T(8,128)(2,1)S(1)} %bitcast.107), kind=kOutput, calls=%fused_computation.112 | convolution fusion | flops 136315008 | bytes 4227072 | tf_op jit(solution)/shard_map/jvp()/sub | solution.py:49
  170.7 2.6 %fusion.22 = (f32[32,128]{1,0:T(8,128)S(1)}, bf16[32,128,128]{1,2,0:T(8,128)(2,1)S(1)}) fusion(f32[32,128,128]{1,2,0:T(8,128)} %get-tuple-element.22, bf16[32,128,128]{1,2,0:T(8,128)(2,1)} %fusion.41, f32[32,128]{1,0:T(8,128)S(1)} %multiply_divide_fusion, f32[32,128]{1,0:T(8,128)S(1)} %get-tuple-element.21), kind=kLoop, calls=%fused_computation.28 | loop fusion | flops 3141632 | bytes 4243456 | tf_op jit(solution)/shard_map/transpose(jvp())/reduce_sum | solution.py:49
  173.6 0.8 fusion.42
  174.4 0.4 copy-done.4
  174.8 0.9 fusion.83
  175.7 0.5 fusion.90
  176.1 0.8 fusion.91
  177.3 0.8 add_convert_fusion
  178.2 0.9 fusion.28
  179.1 2.3 %convolution_convert_fusion = bf16[256,4096]{1,0:T(8,128)(2,1)} fusion(bf16[128,4096]{0,1:T(8,128)(2,1)S(1)} %bitcast.104, bf16[128,4096]{0,1:T(8,128)(2,1)S(1)} %bitcast.115, bf16[1,128,4096]{1,2,0:T(8,128)(2,1)S(1)} %copy.63, f32[128]{0:T(128)S(1)} %multiply_multiply_fusion, f32[4096]{0:T(1024)S(1)} %copy-done.6, f32[128]{0:T(128)S(1)} %fusion.75, ...), kind=kOutput, calls=%fused_computation.10 | convolution fusion | flops 274235392 | bytes 5260800 | tf_op jit(solution)/shard_map/dot_general | solution.py:164
  181.4 10.9 %fusion.14 = bf16[256,2048]{1,0:T(8,128)(2,1)S(1)} fusion(bf16[2,2048,3456]{2,1,0:T(8,128)(2,1)} %bitcast.126, bf16[32,2,8,2048]{3,2,1,0:T(8,128)(2,1)} %bitcast.118), kind=kOutput, calls=%fused_computation.21 | convolution fusion | flops 4295491584 | bytes 19922944 | tf_op jit(solution)/shard_map/tgc,gdc->td/dot_general | solution.py:167
  192.4 1.5 reshape.181
  193.9 5.5 %all-to-all-start.2 = ((bf16[128,2,2048]{2,1,0:T(2,128)(2,1)}), bf16[128,2,2048]{2,1,0:T(2,128)(2,1)S(1)}, u32[]{:S(2)}, u32[]{:S(2)}) async-start(bf16[128,2,2048]{2,1,0:T(2,128)(2,1)} %reshape.181), calls=%async_computation.2 | async-start | bytes 2097152 | tf_op jit(solution)/shard_map/all_to_all | solution.py:173
  199.4 0.5 broadcast.138
  199.9 0.8 reduce.4
  200.8 1.3 copy.72
  202.2 15.1 %all-to-all-done.2 = bf16[128,2,2048]{2,1,0:T(2,128)(2,1)S(1)} async-done(((bf16[128,2,2048]{2,1,0:T(2,128)(2,1)}), bf16[128,2,2048]{2,1,0:T(2,128)(2,1)S(1)}, u32[]{:S(2)}, u32[]{:S(2)}) %all-to-all-start.2) | async-done | bytes 1048608 | tf_op jit(solution)/shard_map/all_to_all | solution.py:173
  217.2 0.4 reshape.182
  217.6 1.0 fusion.65
  (41 shorter events, 2.4 us)
Async XLA Ops:
  7.2 105.9 %all-gather.2.cloned.1.call-start = ((), (), s32[]{:S(2)}) async-start(), calls=%async_computation.3 | async-start | bytes 28532736 | tf_op jit(solution)/shard_map/all_gather | solution.py:111
  13.3 20.9 %all-to-all-start = ((s32[128,1,2]{2,1,0:T(1,128)}), s32[128,1,2]{2,1,0:T(1,128)S(1)}, u32[]{:S(2)}, u32[]{:S(2)}) async-start(s32[128,1,2]{2,1,0:T(1,128)} %bitcast.15), calls=%async_computation | async-start | bytes 131072 | tf_op jit(solution)/shard_map/all_to_all | solution.py:148
  123.1 1.7 copy-start.8
  124.9 2.6 %copy-start.7 = (bf16[4,2048]{1,0:T(4,128)(2,1)}, bf16[4,2048]{1,0:T(4,128)(2,1)S(1)}, u32[]{:S(2)}) copy-start(bf16[4,2048]{1,0:T(4,128)(2,1)S(1)} %multiply_convert_fusion) | copy-start | bytes 49156
  125.4 9.3 %copy-start.5 = (bf16[1,128,4096]{2,1,0:T(8,128)(2,1)S(1)}, bf16[1,128,4096]{2,1,0:T(8,128)(2,1)}, u32[]{:S(2)}) copy-start(bf16[1,128,4096]{2,1,0:T(8,128)(2,1)} %param.21) | copy-start | bytes 3145732
  127.5 8.0 %copy-start.9 = (s32[1,128,1]{1,2,0:T(1,128)S(1)}, s32[1,128,1]{1,2,0:T(1,128)}, u32[]{:S(2)}) copy-start(s32[1,128,1]{1,2,0:T(1,128)} %param.19) | copy-start | bytes 1540
  127.5 25.1 %all-to-all-start.1 = ((bf16[128,2,2048]{2,1,0:T(2,128)(2,1)}), bf16[128,2,2048]{2,1,0:T(2,128)(2,1)S(1)}, u32[]{:S(2)}, u32[]{:S(2)}) async-start(bf16[128,2,2048]{2,1,0:T(2,128)(2,1)} %copy.55), calls=%async_computation.1 | async-start | bytes 2097152 | tf_op jit(solution)/shard_map/all_to_all | solution.py:150
  162.2 1.2 copy-start.6
  164.2 1.5 copy-start
  170.7 2.6 %copy-start.2 = (bf16[32,128,128]{1,2,0:T(8,128)(2,1)S(1)}, bf16[32,128,128]{1,2,0:T(8,128)(2,1)}, u32[]{:S(2)}) copy-start(bf16[32,128,128]{1,2,0:T(8,128)(2,1)} %fusion.41) | copy-start | bytes 3145732
  170.7 2.9 %copy-start.3 = (f32[32,128,128]{1,2,0:T(8,128)S(1)}, f32[32,128,128]{1,2,0:T(8,128)}, u32[]{:S(2)}) copy-start(f32[32,128,128]{1,2,0:T(8,128)} %get-tuple-element.22) | copy-start | bytes 6291460
  173.6 1.2 copy-start.4
  176.1 1.2 copy-start.1
  193.9 23.3 %all-to-all-start.2 = ((bf16[128,2,2048]{2,1,0:T(2,128)(2,1)}), bf16[128,2,2048]{2,1,0:T(2,128)(2,1)S(1)}, u32[]{:S(2)}, u32[]{:S(2)}) async-start(bf16[128,2,2048]{2,1,0:T(2,128)(2,1)} %reshape.181), calls=%async_computation.2 | async-start | bytes 2097152 | tf_op jit(solution)/shard_map/all_to_all | solution.py:173
Sparse Core Ops, SparseCore 0:
  11.6 101.4 all-gather.1

commit v7 on v6

--- a/solution.py
+++ b/solution.py
@@ -146,7 +146,11 @@
     request = request.reshape(devices, cap_slots)
     width = item_embed.shape[1]
     incoming = lax.all_to_all(request, ("grp", "fsdp"), split_axis=0, concat_axis=0, tiled=True)
-    found = serve_rows(incoming, item_embed)
+    found = jnp.take(
+        jnp.concatenate([item_embed, jnp.zeros((1, item_embed.shape[1]), item_embed.dtype)], axis=0),
+        jnp.clip(incoming, 0, count),
+        axis=0,
+    )
     returned = lax.all_to_all(found, ("grp", "fsdp"), split_axis=0, concat_axis=0, tiled=True)
     fetched = jnp.take(returned.reshape(devices * cap_slots, width), position, axis=0)
     hidden = stored(

time: 226 us -> 228 us (level)
  no operation moved by 1% of the time
where the time goes in v7:
time: 228 us; the launch traced here: 227 us
  waiting for transfers between devices  117 us (51%)
  matrix products  43.3 us (19%)
  starting transfers between devices  24.3 us (11%)
  local copies, waits for them, and re-layouts  16.2 us (7%)
  between operations  14.4 us (6%)
  other arithmetic  10.4 us (5%)
    all_gather x1, waiting for transfers between devices, per_device(): lax.all_gather(pack_halves(sources), ('grp', 'fsdp'), axis=0, tiled=True)  77.4 us
    all_to_all x1, waiting for transfers between devices, per_device(): lax.all_to_all(outgoing.reshape(devices, cap_slots, DI), ('grp', 'fsdp'),...  16.4 us
    all_to_all x1, waiting for transfers between devices, per_device(): lax.all_to_all(found, ('grp', 'fsdp'), split_axis=0, concat_axis=0, tiled...  14.7 us
    all_to_all x1, starting transfers between devices, per_device(): lax.all_to_all(request, ('grp', 'fsdp'), split_axis=0, concat_axis=0, til...  11.5 us
    dot_general x1, matrix products, per_device(): jnp.einsum('tgc,gdc->td', slot_grads.reshape(slot_grads.shape[0], groups,...  10.9 us
    all_to_all x1, waiting for transfers between devices, per_device(): lax.all_to_all(request, ('grp', 'fsdp'), split_axis=0, concat_axis=0, til...  8.29 us
    dot_general x1, matrix products, per_device(): jnp.einsum('td,gdc->tgc', fetched, adapter_halves, preferred_element_type...  8.24 us
    all_to_all x1, starting transfers between devices, per_device(): lax.all_to_all(found, ('grp', 'fsdp'), split_axis=0, concat_axis=0, tiled...  7.26 us
  transfers between devices with their start and end apart: 4, of which 4 were waited for; matrix products, arithmetic and copies ran while one was open for 5% of the time, Pallas kernels for 0%

profile of v7, /device:TPU:1, one launch (start us, length us, event | category | flops | bytes accessed | tf_op | source)
XLA Modules:
  0.0 227.1 jit_solution(14693640439558282058)
XLA Ops:
  7.2 1.7 shard_map.130
  9.0 0.7 fusion.68
  9.9 0.8 select_reduce_fusion
  10.7 0.7 fusion.70
  11.4 1.1 scatter_custom_fusion
  12.5 0.8 all_to_all.12
  13.3 11.5 %all-to-all-start = ((s32[128,1,2]{2,1,0:T(1,128)}), s32[128,1,2]{2,1,0:T(1,128)S(1)}, u32[]{:S(2)}, u32[]{:S(2)}) async-start(s32[128,1,2]{2,1,0:T(1,128)} %bitcast.15), calls=%async_computation | async-start | bytes 131072 | tf_op jit(solution)/shard_map/all_to_all | solution.py:148
  24.8 1.0 slice.24
  25.8 8.3 %all-to-all-done = s32[128,1,2]{2,1,0:T(1,128)S(1)} async-done(((s32[128,1,2]{2,1,0:T(1,128)}), s32[128,1,2]{2,1,0:T(1,128)S(1)}, u32[]{:S(2)}, u32[]{:S(2)}) %all-to-all-start) | async-done | bytes 1056 | tf_op jit(solution)/shard_map/all_to_all | solution.py:148
  34.1 0.5 broadcast.194
  34.6 0.9 fusion.84
  35.7 77.4 %all-gather.2.cloned.1.call-done = bf16[4096,3456]{1,0:T(8,128)(2,1)} async-done(((bf16[32,3456]{1,0:T(8,128)(2,1)}), bf16[4096,3456]{1,0:T(8,128)(2,1)}) %all-gather.2.cloned.1.call-update) | async-done | bytes 28311568 | tf_op jit(solution)/shard_map/all_gather | solution.py:111
  113.1 4.6 %fusion.45 = bf16[2,1024,4]{1,2,0:T(4,128)(2,1)S(1)} fusion(bf16[2,2048,3456]{2,1,0:T(8,128)(2,1)} %bitcast.123, bf16[4,1,2048]{2,1,0:T(2,128)(2,1)S(1)} %slice.24), kind=kOutput, calls=%fused_computation.57 | convolution fusion | flops 33562624 | bytes 8421376 | tf_op jit(solution)/shard_map/id,gdc->igc/dot_general | solution.py:119
  117.8 5.3 %fusion.37 = bf16[1024,2,256]{0,2,1:T(8,128)(2,1)S(1)} fusion(bf16[1024,2048,1]{1,0,2:T(8,128)(2,1)} %bitcast.131, bf16[2,2048,3456]{2,1,0:T(8,128)(2,1)} %bitcast.124), kind=kOutput, calls=%fused_computation.50 | convolution fusion | flops 2148007936 | bytes 7340032 | tf_op jit(solution)/shard_map/td,gdc->tgc/dot_general | solution.py:114
  123.1 0.4 reshape.202
  124.9 1.4 gather_fusion
  126.3 0.7 reshape.214
  127.0 2.0 broadcast_select_fusion
  129.1 7.3 %all-to-all-start.1 = ((bf16[128,2,2048]{2,1,0:T(2,128)(2,1)}), bf16[128,2,2048]{2,1,0:T(2,128)(2,1)S(1)}, u32[]{:S(2)}, u32[]{:S(2)}) async-start(bf16[128,2,2048]{2,1,0:T(2,128)(2,1)} %broadcast_select_fusion), calls=%async_computation.1 | async-start | bytes 2097152 | tf_op jit(solution)/shard_map/all_to_all | solution.py:154
  136.4 0.7 copy.59
  137.1 1.3 slice.40
  138.4 1.1 copy.53
  139.5 14.7 %all-to-all-done.1 = bf16[128,2,2048]{2,1,0:T(2,128)(2,1)S(1)} async-done(((bf16[128,2,2048]{2,1,0:T(2,128)(2,1)}), bf16[128,2,2048]{2,1,0:T(2,128)(2,1)S(1)}, u32[]{:S(2)}, u32[]{:S(2)}) %all-to-all-start.1) | async-done | bytes 1048608 | tf_op jit(solution)/shard_map/all_to_all | solution.py:154
  154.2 0.4 reshape.204
  154.6 0.9 gather_fusion.1
  155.6 8.2 %fusion.11 = bf16[128,2,2048]{2,0,1:T(8,128)(2,1)S(1)} fusion(bf16[2,2048,3456]{2,1,0:T(8,128)(2,1)} %bitcast.126, bf16[128,2048]{1,0:T(8,128)(2,1)S(1)} %gather_fusion.1, pred[128]{0:T(512)(128)(4,1)S(1)} %get-tuple-element.9), kind=kOutput, calls=%fused_computation.21 | convolution fusion | flops 2148270080 | bytes 18350208 | tf_op jit(solution)/shard_map/td,gdc->tgc/dot_general | solution.py:157
  163.8 0.7 copy.52
  164.5 0.6 fusion.24
  165.1 0.7 fusion.26
  165.8 1.5 fusion.41
  167.3 1.5 fusion.40
  168.8 3.5 %fusion.86 = (f32[32,128]{1,0:T(8,128)S(1)}, f32[32,128,128]{1,2,0:T(8,128)}) fusion(pred[128,128]{0,1:T(8,128)(4,1)S(1)} %iota_compare_fusion.4, bf16[128,32,128]{0,2,1:T(8,128)(2,1)} %fusion.40, bf16[128,32,128]{0,2,1:T(8,128)(2,1)S(1)} %bitcast.107), kind=kOutput, calls=%fused_computation.116 | convolution fusion | flops 136315008 | bytes 4227072 | tf_op jit(solution)/shard_map/jvp()/sub | solution.py:49
  172.3 2.6 %fusion.22 = (f32[32,128]{1,0:T(8,128)S(1)}, bf16[32,128,128]{1,2,0:T(8,128)(2,1)S(1)}) fusion(f32[32,128,128]{1,2,0:T(8,128)} %get-tuple-element.24, bf16[32,128,128]{1,2,0:T(8,128)(2,1)} %fusion.41, f32[32,128]{1,0:T(8,128)S(1)} %multiply_divide_fusion, f32[32,128]{1,0:T(8,128)S(1)} %get-tuple-element.23), kind=kLoop, calls=%fused_computation.28 | loop fusion | flops 3141632 | bytes 4243456 | tf_op jit(solution)/shard_map/transpose(jvp())/reduce_sum | solution.py:49
  175.2 0.8 fusion.42
  176.0 0.4 copy-done.4
  176.4 0.8 fusion.81
  177.3 0.5 fusion.89
  177.7 0.8 fusion.90
  179.0 0.8 add_convert_fusion
  179.8 0.9 fusion.28
  180.7 2.3 %convolution_convert_fusion = bf16[256,4096]{1,0:T(8,128)(2,1)} fusion(bf16[128,4096]{0,1:T(8,128)(2,1)S(1)} %bitcast.104, bf16[128,4096]{0,1:T(8,128)(2,1)S(1)} %bitcast.115, bf16[1,128,4096]{1,2,0:T(8,128)(2,1)S(1)} %copy.59, f32[128]{0:T(128)S(1)} %multiply_multiply_fusion, f32[4096]{0:T(1024)S(1)} %copy-done.6, f32[128]{0:T(128)S(1)} %fusion.73, ...), kind=kOutput, calls=%fused_computation.11 | convolution fusion | flops 274235392 | bytes 5260800 | tf_op jit(solution)/shard_map/dot_general | solution.py:168
  183.0 10.9 %fusion.14 = bf16[256,2048]{1,0:T(8,128)(2,1)S(1)} fusion(bf16[2,2048,3456]{2,1,0:T(8,128)(2,1)} %bitcast.127, bf16[32,2,8,2048]{3,2,1,0:T(8,128)(2,1)} %bitcast.118), kind=kOutput, calls=%fused_computation.22 | convolution fusion | flops 4295491584 | bytes 19922944 | tf_op jit(solution)/shard_map/tgc,gdc->td/dot_general | solution.py:171
  194.0 1.5 reshape.210
  195.5 5.5 %all-to-all-start.2 = ((bf16[128,2,2048]{2,1,0:T(2,128)(2,1)}), bf16[128,2,2048]{2,1,0:T(2,128)(2,1)S(1)}, u32[]{:S(2)}, u32[]{:S(2)}) async-start(bf16[128,2,2048]{2,1,0:T(2,128)(2,1)} %reshape.210), calls=%async_computation.2 | async-start | bytes 2097152 | tf_op jit(solution)/shard_map/all_to_all | solution.py:177
  201.1 1.3 copy.68
  202.4 16.4 %all-to-all-done.2 = bf16[128,2,2048]{2,1,0:T(2,128)(2,1)S(1)} async-done(((bf16[128,2,2048]{2,1,0:T(2,128)(2,1)}), bf16[128,2,2048]{2,1,0:T(2,128)(2,1)S(1)}, u32[]{:S(2)}, u32[]{:S(2)}) %all-to-all-start.2) | async-done | bytes 1048608 | tf_op jit(solution)/shard_map/all_to_all | solution.py:177
  218.8 0.4 reshape.211
  219.2 1.0 fusion.65
  (46 shorter events, 2.9 us)
Async XLA Ops:
  7.2 105.9 %all-gather.2.cloned.1.call-start = ((), (), s32[]{:S(2)}) async-start(), calls=%async_computation.3 | async-start | bytes 28532736 | tf_op jit(solution)/shard_map/all_gather | solution.py:111
  13.3 20.9 %all-to-all-start = ((s32[128,1,2]{2,1,0:T(1,128)}), s32[128,1,2]{2,1,0:T(1,128)S(1)}, u32[]{:S(2)}, u32[]{:S(2)}) async-start(s32[128,1,2]{2,1,0:T(1,128)} %bitcast.15), calls=%async_computation | async-start | bytes 131072 | tf_op jit(solution)/shard_map/all_to_all | solution.py:148
  123.1 1.7 copy-start.8
  124.9 1.4 copy-start.7
  127.0 9.3 %copy-start.5 = (bf16[1,128,4096]{2,1,0:T(8,128)(2,1)S(1)}, bf16[1,128,4096]{2,1,0:T(8,128)(2,1)}, u32[]{:S(2)}) copy-start(bf16[1,128,4096]{2,1,0:T(8,128)(2,1)} %param.21) | copy-start | bytes 3145732
  129.1 8.0 %copy-start.9 = (s32[1,128,1]{1,2,0:T(1,128)S(1)}, s32[1,128,1]{1,2,0:T(1,128)}, u32[]{:S(2)}) copy-start(s32[1,128,1]{1,2,0:T(1,128)} %param.19) | copy-start | bytes 1540
  129.1 25.1 %all-to-all-start.1 = ((bf16[128,2,2048]{2,1,0:T(2,128)(2,1)}), bf16[128,2,2048]{2,1,0:T(2,128)(2,1)S(1)}, u32[]{:S(2)}, u32[]{:S(2)}) async-start(bf16[128,2,2048]{2,1,0:T(2,128)(2,1)} %broadcast_select_fusion), calls=%async_computation.1 | async-start | bytes 2097152 | tf_op jit(solution)/shard_map/all_to_all | solution.py:154
  163.8 1.2 copy-start.6
  165.8 1.5 copy-start
  172.3 2.6 %copy-start.2 = (bf16[32,128,128]{1,2,0:T(8,128)(2,1)S(1)}, bf16[32,128,128]{1,2,0:T(8,128)(2,1)}, u32[]{:S(2)}) copy-start(bf16[32,128,128]{1,2,0:T(8,128)(2,1)} %fusion.41) | copy-start | bytes 3145732
  172.3 2.9 %copy-start.3 = (f32[32,128,128]{1,2,0:T(8,128)S(1)}, f32[32,128,128]{1,2,0:T(8,128)}, u32[]{:S(2)}) copy-start(f32[32,128,128]{1,2,0:T(8,128)} %get-tuple-element.24) | copy-start | bytes 6291460
  175.2 1.2 copy-start.4
  177.7 1.2 copy-start.1
  195.5 23.3 %all-to-all-start.2 = ((bf16[128,2,2048]{2,1,0:T(2,128)(2,1)}), bf16[128,2,2048]{2,1,0:T(2,128)(2,1)S(1)}, u32[]{:S(2)}, u32[]{:S(2)}) async-start(bf16[128,2,2048]{2,1,0:T(2,128)(2,1)} %reshape.210), calls=%async_computation.2 | async-start | bytes 2097152 | tf_op jit(solution)/shard_map/all_to_all | solution.py:177
Sparse Core Ops, SparseCore 0:
  11.6 101.4 all-gather.1

commit v8 on v7

--- a/solution.py
+++ b/solution.py
@@ -150,6 +150,7 @@
         jnp.concatenate([item_embed, jnp.zeros((1, item_embed.shape[1]), item_embed.dtype)], axis=0),
         jnp.clip(incoming, 0, count),
         axis=0,
+        mode="clip",
     )
     returned = lax.all_to_all(found, ("grp", "fsdp"), split_axis=0, concat_axis=0, tiled=True)
     fetched = jnp.take(returned.reshape(devices * cap_slots, width), position, axis=0)

time: 228 us -> 226 us (level)
  no operation moved by 1% of the time
where the time goes in v8:
time: 226 us
  waiting for transfers between devices  117 us (52%)
  matrix products  43.3 us (19%)
  starting transfers between devices  24.3 us (11%)
  local copies, waits for them, and re-layouts  17 us (8%)
  between operations  14.4 us (6%)
  other arithmetic  8.47 us (4%)
    all_gather x1, waiting for transfers between devices, per_device(): lax.all_gather(pack_halves(sources), ('grp', 'fsdp'), axis=0, tiled=True)  77.3 us
    all_to_all x1, waiting for transfers between devices, per_device(): lax.all_to_all(outgoing.reshape(devices, cap_slots, DI), ('grp', 'fsdp'),...  16.4 us
    all_to_all x1, waiting for transfers between devices, per_device(): lax.all_to_all(found, ('grp', 'fsdp'), split_axis=0, concat_axis=0, tiled...  14.7 us
    all_to_all x1, starting transfers between devices, per_device(): lax.all_to_all(request, ('grp', 'fsdp'), split_axis=0, concat_axis=0, til...  11.5 us
    dot_general x1, matrix products, per_device(): jnp.einsum('tgc,gdc->td', slot_grads.reshape(slot_grads.shape[0], groups,...  10.9 us
    all_to_all x1, waiting for transfers between devices, per_device(): lax.all_to_all(request, ('grp', 'fsdp'), split_axis=0, concat_axis=0, til...  8.29 us
    dot_general x1, matrix products, per_device(): jnp.einsum('td,gdc->tgc', fetched, adapter_halves, preferred_element_type...  8.24 us
    all_to_all x1, starting transfers between devices, per_device(): lax.all_to_all(found, ('grp', 'fsdp'), split_axis=0, concat_axis=0, tiled...  7.26 us
  transfers between devices with their start and end apart: 4, of which 4 were waited for; matrix products, arithmetic and copies ran while one was open for 5% of the time, Pallas kernels for 0%

profile of v8, /device:TPU:1, one launch (start us, length us, event | category | flops | bytes accessed | tf_op | source)
XLA Modules:
  0.0 225.8 jit_solution(6188680818958642916)
XLA Ops:
  7.2 1.7 shard_map.130
  9.0 0.7 fusion.68
  9.9 0.8 select_reduce_fusion
  10.7 0.7 fusion.70
  11.4 1.1 scatter_custom_fusion
  12.5 0.8 all_to_all.12
  13.3 11.5 %all-to-all-start = ((s32[128,1,2]{2,1,0:T(1,128)}), s32[128,1,2]{2,1,0:T(1,128)S(1)}, u32[]{:S(2)}, u32[]{:S(2)}) async-start(s32[128,1,2]{2,1,0:T(1,128)} %bitcast.15), calls=%async_computation | async-start | bytes 131072 | tf_op jit(solution)/shard_map/all_to_all | solution.py:148
  24.8 1.0 slice.24
  25.8 8.3 %all-to-all-done = s32[128,1,2]{2,1,0:T(1,128)S(1)} async-done(((s32[128,1,2]{2,1,0:T(1,128)}), s32[128,1,2]{2,1,0:T(1,128)S(1)}, u32[]{:S(2)}, u32[]{:S(2)}) %all-to-all-start) | async-done | bytes 1056 | tf_op jit(solution)/shard_map/all_to_all | solution.py:148
  34.1 0.5 broadcast.165
  34.6 1.0 fusion.83
  35.8 77.3 %all-gather.2.cloned.1.call-done = bf16[4096,3456]{1,0:T(8,128)(2,1)} async-done(((bf16[32,3456]{1,0:T(8,128)(2,1)}), bf16[4096,3456]{1,0:T(8,128)(2,1)}) %all-gather.2.cloned.1.call-update) | async-done | bytes 28311568 | tf_op jit(solution)/shard_map/all_gather | solution.py:111
  113.1 4.6 %fusion.45 = bf16[2,1024,4]{1,2,0:T(4,128)(2,1)S(1)} fusion(bf16[2,2048,3456]{2,1,0:T(8,128)(2,1)} %bitcast.117, bf16[4,1,2048]{2,1,0:T(2,128)(2,1)S(1)} %slice.24), kind=kOutput, calls=%fused_computation.56 | convolution fusion | flops 33562624 | bytes 8421376 | tf_op jit(solution)/shard_map/id,gdc->igc/dot_general | solution.py:119
  117.8 5.3 %fusion.37 = bf16[1024,2,256]{0,2,1:T(8,128)(2,1)S(1)} fusion(bf16[1024,2048,1]{1,0,2:T(8,128)(2,1)} %bitcast.125, bf16[2,2048,3456]{2,1,0:T(8,128)(2,1)} %bitcast.118), kind=kOutput, calls=%fused_computation.49 | convolution fusion | flops 2148007936 | bytes 7340032 | tf_op jit(solution)/shard_map/td,gdc->tgc/dot_general | solution.py:114
  123.1 0.4 reshape.184
  123.5 0.4 reshape.183
  124.9 1.4 gather_fusion
  126.3 1.5 reshape.196
  127.8 7.3 %all-to-all-start.1 = ((bf16[128,2,2048]{2,1,0:T(2,128)(2,1)}), bf16[128,2,2048]{2,1,0:T(2,128)(2,1)S(1)}, u32[]{:S(2)}, u32[]{:S(2)}) async-start(bf16[128,2,2048]{2,1,0:T(2,128)(2,1)} %reshape.196), calls=%async_computation.1 | async-start | bytes 2097152 | tf_op jit(solution)/shard_map/all_to_all | solution.py:155
  135.1 0.7 copy.59
  135.8 1.3 slice.40
  137.1 1.1 copy.53
  138.3 14.7 %all-to-all-done.1 = bf16[128,2,2048]{2,1,0:T(2,128)(2,1)S(1)} async-done(((bf16[128,2,2048]{2,1,0:T(2,128)(2,1)}), bf16[128,2,2048]{2,1,0:T(2,128)(2,1)S(1)}, u32[]{:S(2)}, u32[]{:S(2)}) %all-to-all-start.1) | async-done | bytes 1048608 | tf_op jit(solution)/shard_map/all_to_all | solution.py:155
  152.9 0.4 reshape.186
  153.3 0.9 gather_fusion.1
  154.3 8.2 %fusion.11 = bf16[128,2,2048]{2,0,1:T(8,128)(2,1)S(1)} fusion(bf16[2,2048,3456]{2,1,0:T(8,128)(2,1)} %bitcast.120, bf16[128,2048]{1,0:T(8,128)(2,1)S(1)} %gather_fusion.1, pred[128]{0:T(512)(128)(4,1)S(1)} %get-tuple-element.11), kind=kOutput, calls=%fused_computation.21 | convolution fusion | flops 2148270080 | bytes 18350208 | tf_op jit(solution)/shard_map/td,gdc->tgc/dot_general | solution.py:158
  162.5 0.7 copy.52
  163.2 0.6 fusion.24
  163.8 0.7 fusion.26
  164.5 1.5 fusion.41
  166.0 1.5 fusion.40
  167.5 3.5 %fusion.86 = (f32[32,128]{1,0:T(8,128)S(1)}, f32[32,128,128]{1,2,0:T(8,128)}) fusion(pred[128,128]{0,1:T(8,128)(4,1)S(1)} %iota_compare_fusion.4, bf16[128,32,128]{0,2,1:T(8,128)(2,1)} %fusion.40, bf16[128,32,128]{0,2,1:T(8,128)(2,1)S(1)} %bitcast.103), kind=kOutput, calls=%fused_computation.112 | convolution fusion | flops 136315008 | bytes 4227072 | tf_op jit(solution)/shard_map/jvp()/sub | solution.py:49
  171.0 2.6 %fusion.22 = (f32[32,128]{1,0:T(8,128)S(1)}, bf16[32,128,128]{1,2,0:T(8,128)(2,1)S(1)}) fusion(f32[32,128,128]{1,2,0:T(8,128)} %get-tuple-element.24, bf16[32,128,128]{1,2,0:T(8,128)(2,1)} %fusion.41, f32[32,128]{1,0:T(8,128)S(1)} %multiply_divide_fusion, f32[32,128]{1,0:T(8,128)S(1)} %get-tuple-element.23), kind=kLoop, calls=%fused_computation.28 | loop fusion | flops 3141632 | bytes 4243456 | tf_op jit(solution)/shard_map/transpose(jvp())/reduce_sum | solution.py:49
  173.9 0.8 fusion.42
  174.7 0.4 copy-done.4
  175.1 0.9 fusion.81
  176.0 0.5 fusion.89
  176.5 0.9 fusion.90
  177.7 0.8 add_convert_fusion
  178.5 0.9 fusion.28
  179.5 2.3 %convolution_convert_fusion = bf16[256,4096]{1,0:T(8,128)(2,1)} fusion(bf16[128,4096]{0,1:T(8,128)(2,1)S(1)} %bitcast.100, bf16[128,4096]{0,1:T(8,128)(2,1)S(1)} %bitcast.111, bf16[1,128,4096]{1,2,0:T(8,128)(2,1)S(1)} %copy.59, f32[128]{0:T(128)S(1)} %multiply_multiply_fusion, f32[4096]{0:T(1024)S(1)} %copy-done.6, f32[128]{0:T(128)S(1)} %fusion.73, ...), kind=kOutput, calls=%fused_computation.11 | convolution fusion | flops 274235392 | bytes 5260800 | tf_op jit(solution)/shard_map/dot_general | solution.py:169
  181.8 10.9 %fusion.14 = bf16[256,2048]{1,0:T(8,128)(2,1)S(1)} fusion(bf16[2,2048,3456]{2,1,0:T(8,128)(2,1)} %bitcast.121, bf16[32,2,8,2048]{3,2,1,0:T(8,128)(2,1)} %bitcast.114), kind=kOutput, calls=%fused_computation.22 | convolution fusion | flops 4295491584 | bytes 19922944 | tf_op jit(solution)/shard_map/tgc,gdc->td/dot_general | solution.py:172
  192.7 1.5 reshape.192
  194.2 5.5 %all-to-all-start.2 = ((bf16[128,2,2048]{2,1,0:T(2,128)(2,1)}), bf16[128,2,2048]{2,1,0:T(2,128)(2,1)S(1)}, u32[]{:S(2)}, u32[]{:S(2)}) async-start(bf16[128,2,2048]{2,1,0:T(2,128)(2,1)} %reshape.192), calls=%async_computation.2 | async-start | bytes 2097152 | tf_op jit(solution)/shard_map/all_to_all | solution.py:178
  199.9 1.3 copy.68
  201.2 16.4 %all-to-all-done.2 = bf16[128,2,2048]{2,1,0:T(2,128)(2,1)S(1)} async-done(((bf16[128,2,2048]{2,1,0:T(2,128)(2,1)}), bf16[128,2,2048]{2,1,0:T(2,128)(2,1)S(1)}, u32[]{:S(2)}, u32[]{:S(2)}) %all-to-all-start.2) | async-done | bytes 1048608 | tf_op jit(solution)/shard_map/all_to_all | solution.py:178
  217.5 0.4 reshape.193
  218.0 1.0 fusion.65
  (43 shorter events, 2.5 us)
Async XLA Ops:
  7.2 105.9 %all-gather.2.cloned.1.call-start = ((), (), s32[]{:S(2)}) async-start(), calls=%async_computation.3 | async-start | bytes 28532736 | tf_op jit(solution)/shard_map/all_gather | solution.py:111
  13.3 20.9 %all-to-all-start = ((s32[128,1,2]{2,1,0:T(1,128)}), s32[128,1,2]{2,1,0:T(1,128)S(1)}, u32[]{:S(2)}, u32[]{:S(2)}) async-start(s32[128,1,2]{2,1,0:T(1,128)} %bitcast.15), calls=%async_computation | async-start | bytes 131072 | tf_op jit(solution)/shard_map/all_to_all | solution.py:148
  123.1 1.7 copy-start.8
  124.9 1.4 copy-start.7
  126.3 8.8 %copy-start.5 = (bf16[1,128,4096]{2,1,0:T(8,128)(2,1)S(1)}, bf16[1,128,4096]{2,1,0:T(8,128)(2,1)}, u32[]{:S(2)}) copy-start(bf16[1,128,4096]{2,1,0:T(8,128)(2,1)} %param.21) | copy-start | bytes 3145732
  127.8 8.0 %copy-start.9 = (s32[1,128,1]{1,2,0:T(1,128)S(1)}, s32[1,128,1]{1,2,0:T(1,128)}, u32[]{:S(2)}) copy-start(s32[1,128,1]{1,2,0:T(1,128)} %param.19) | copy-start | bytes 1540
  127.8 25.1 %all-to-all-start.1 = ((bf16[128,2,2048]{2,1,0:T(2,128)(2,1)}), bf16[128,2,2048]{2,1,0:T(2,128)(2,1)S(1)}, u32[]{:S(2)}, u32[]{:S(2)}) async-start(bf16[128,2,2048]{2,1,0:T(2,128)(2,1)} %reshape.196), calls=%async_computation.1 | async-start | bytes 2097152 | tf_op jit(solution)/shard_map/all_to_all | solution.py:155
  162.5 1.2 copy-start.6
  164.5 1.5 copy-start
  171.0 2.6 %copy-start.2 = (bf16[32,128,128]{1,2,0:T(8,128)(2,1)S(1)}, bf16[32,128,128]{1,2,0:T(8,128)(2,1)}, u32[]{:S(2)}) copy-start(bf16[32,128,128]{1,2,0:T(8,128)(2,1)} %fusion.41) | copy-start | bytes 3145732
  171.0 2.9 %copy-start.3 = (f32[32,128,128]{1,2,0:T(8,128)S(1)}, f32[32,128,128]{1,2,0:T(8,128)}, u32[]{:S(2)}) copy-start(f32[32,128,128]{1,2,0:T(8,128)} %get-tuple-element.24) | copy-start | bytes 6291460
  173.9 1.2 copy-start.4
  176.4 1.2 copy-start.1
  194.2 23.3 %all-to-all-start.2 = ((bf16[128,2,2048]{2,1,0:T(2,128)(2,1)}), bf16[128,2,2048]{2,1,0:T(2,128)(2,1)S(1)}, u32[]{:S(2)}, u32[]{:S(2)}) async-start(bf16[128,2,2048]{2,1,0:T(2,128)(2,1)} %reshape.192), calls=%async_computation.2 | async-start | bytes 2097152 | tf_op jit(solution)/shard_map/all_to_all | solution.py:178
Sparse Core Ops, SparseCore 0:
  11.6 101.4 all-gather.1

commit v9 on v6

--- a/solution.py
+++ b/solution.py
@@ -73,6 +73,20 @@
         _pack_halves,
         out_shape=jax.ShapeDtypeStruct((sources[0].shape[0], total), sources[0].dtype),
     )(*sources)
+
+
+def ring_gather(block, strides, shards):
+    for stride in strides:
+        base = [f for f in range(shards) if (f // stride) % 4 == 0]
+        up = [(f + k * stride, f + ((k + 1) % 4) * stride) for f in base for k in range(4)]
+        down = [(b, a) for a, b in up]
+        from_below = lax.ppermute(block, "fsdp", up)
+        from_above = lax.ppermute(block, "fsdp", down)
+        from_two_up = lax.ppermute(from_above, "fsdp", down)
+        relative = jnp.stack([block, from_above, from_two_up, from_below])
+        place = (lax.axis_index("fsdp") // stride) % 4
+        block = jnp.roll(relative, place, axis=0)
+    return block
 
 
 def serve_rows(requests, lookup_matrix):
@@ -105,23 +119,31 @@
     last_row = item_states[:, ILEN - 1, :]
     side = lax.axis_index("grp")
 
-    sources = [w_key, w_value, w_query, w_adapt, user_query]
+    sources = [w_key, w_value, w_adapt, user_query]
     widths = [w.shape[1] // 2 for w in sources[:-1]] + [user_query.shape[1]]
     ends = [sum(widths[: i + 1]) for i in range(len(widths))]
     gathered = lax.all_gather(
         pack_halves(sources), ("grp", "fsdp"), axis=0, tiled=True
     ).reshape(groups, DI, ends[-1])
+    query_half = w_query.shape[1] // groups
+    own_query = lax.dynamic_slice_in_dim(w_query, side * query_half, query_half, axis=1)
+    own_query = ring_gather(own_query, (1, 4, 16), shards).reshape(DI, query_half)
+    other_query = lax.ppermute(own_query, "grp", [(0, 1), (1, 0)])
+    query_own = jnp.dot(last_row, own_query, preferred_element_type=jnp.float32)
+    query_other = jnp.dot(last_row, other_query, preferred_element_type=jnp.float32)
+    query_sum = jnp.where(
+        side == 0,
+        jnp.concatenate([query_own, query_other], axis=1),
+        jnp.concatenate([query_other, query_own], axis=1),
+    )
     kv_sum = jnp.einsum(
         "td,gdc->tgc", flat, gathered[:, :, : ends[1]], preferred_element_type=jnp.float32
     )
     key_sum = kv_sum[:, :, : widths[0]].reshape(flat.shape[0], -1)
     summed_value = kv_sum[:, :, widths[0] :].reshape(flat.shape[0], -1)
-    query_sum = jnp.einsum(
-        "id,gdc->igc", last_row, gathered[:, :, ends[1] : ends[2]], preferred_element_type=jnp.float32
-    ).reshape(count, -1)
-    adapter_halves = gathered[:, :, ends[2] : ends[3]]
+    adapter_halves = gathered[:, :, ends[1] : ends[2]]
     query_map = (
-        gathered[:, :, ends[3] :]
+        gathered[:, :, ends[2] :]
         .reshape(groups, shards, -1, user_query.shape[1])
         .transpose(1, 0, 2, 3)
         .reshape(-1, user_query.shape[1])

time: 226 us -> 268 us (1.19)
  local copies, waits for them, and re-layouts: 16.1 us -> 40.4 us
  starting transfers between devices: 24.3 us -> 42.5 us
  other arithmetic: 8.23 us -> 4.33 us
  waiting for transfers between devices: 117 us -> 120 us
    ppermute x0 -> x10, waiting for transfers between devices: none -> 82.1 us  [the longest x3 46.9 us: ring_gather(): from_two_up = lax.ppermute(from_above, 'fsdp', down)]
    all_gather x1, waiting for transfers between devices: 78.9 us -> 0.02 us  [per_device(): lax.all_gather(pack_halves(sources), ('grp', 'fsdp'), axis=0, tiled=True)]
    ppermute x0 -> x10, starting transfers between devices: none -> 24.6 us  [the longest x3 10 us: ring_gather(): from_above = lax.ppermute(block, 'fsdp', down)]
    unnamed x22 -> x42, local copies, waits for them, and re-layouts: 3.04 us -> 19.3 us
    dynamic_slice x0 -> x1, local copies, waits for them, and re-layouts: none -> 5.05 us  [ring_gather(): block = jnp.roll(relative, place, axis=0)]
    all_to_all x1, starting transfers between devices: 11.5 us -> 7.67 us  [per_device(): lax.all_to_all(request, ('grp', 'fsdp'), split_axis=0, concat_axis=0, til...]
    concatenate x0 -> x3, local copies, waits for them, and re-layouts: none -> 2.95 us  [ring_gather(): block = jnp.roll(relative, place, axis=0)]
    dot_general x1 -> x2, matrix products: 4.57 us -> 5.71 us  [the longest x1 2.86 us: per_device(): query_own = jnp.dot(last_row, own_query, preferred_element_type=jnp.float32)]
  transfers between devices with their start and end apart: 4 -> 14, of which waited for: 4 -> 10; matrix products, arithmetic and copies ran while one was open for 5% -> 14% of each run, Pallas kernels for 0% -> 0%
where the time goes in v9:
time: 268 us; the launch traced here: 267 us
  waiting for transfers between devices  120 us (45%)
  matrix products  43.8 us (16%)
  starting transfers between devices  42.5 us (16%)
  local copies, waits for them, and re-layouts  40.4 us (15%)
  between operations  14.5 us (5%)
  other arithmetic  4.33 us (2%)
    ppermute x3, waiting for transfers between devices, ring_gather(): from_two_up = lax.ppermute(from_above, 'fsdp', down)  46.9 us
    ppermute x3, waiting for transfers between devices, ring_gather(): from_above = lax.ppermute(block, 'fsdp', down)  32.1 us
    unnamed x42, local copies, waits for them, and re-layouts  19.3 us
    all_to_all x1, waiting for transfers between devices, per_device(): lax.all_to_all(outgoing.reshape(devices, cap_slots, DI), ('grp', 'fsdp'),...  15.1 us
    all_to_all x1, waiting for transfers between devices, per_device(): lax.all_to_all(found, ('grp', 'fsdp'), split_axis=0, concat_axis=0, tiled...  14.6 us
    dot_general x1, matrix products, per_device(): jnp.einsum('tgc,gdc->td', slot_grads.reshape(slot_grads.shape[0], groups,...  10.9 us
    ppermute x3, starting transfers between devices, ring_gather(): from_above = lax.ppermute(block, 'fsdp', down)  10 us
    ppermute x3, starting transfers between devices, ring_gather(): from_two_up = lax.ppermute(from_above, 'fsdp', down)  9.09 us
  transfers between devices with their start and end apart: 14, of which 10 were waited for; matrix products, arithmetic and copies ran while one was open for 14% of the time, Pallas kernels for 0%

profile of v9, /device:TPU:1, one launch (start us, length us, event | category | flops | bytes accessed | tf_op | source)
XLA Modules:
  0.0 267.2 jit_solution(16356430104472783576)
XLA Ops:
  7.2 1.7 shard_map.130
  8.9 1.5 bitcast_dynamic-update-slice_fusion.22
  10.4 4.6 %collective-permute-start = (bf16[32,1024]{1,0:T(8,128)(2,1)S(1)}, bf16[32,1024]{1,0:T(8,128)(2,1)S(1)}, u32[]{:S(2)}, u32[]{:S(2)}) collective-permute-start(bf16[32,1024]{1,0:T(8,128)(2,1)S(1)} %get-tuple-element.16), channel_id=1, source_target_pairs={{1,0},{2,1},{3,2},{0,3},{5,4},{6,5},{7,6},{4,7},{9,8},{10,9},{11,1... | collective-permute-start | bytes 196616 | tf_op jit(solution)/shard_map/ppermute | solution.py:84
  15.0 1.3 collective-permute-done
  16.3 3.0 %collective-permute-start.1 = (bf16[32,1024]{1,0:T(8,128)(2,1)S(1)}, bf16[32,1024]{1,0:T(8,128)(2,1)S(1)}, u32[]{:S(2)}, u32[]{:S(2)}) collective-permute-start(bf16[32,1024]{1,0:T(8,128)(2,1)S(1)} %collective-permute-done), channel_id=1, source_target_pairs={{1,0},{2,1},{3,2},{0,3},{5,4},{6,5},{7,6},{4,7},{9,8},{10,9},{11,1... | collective-permute-start | bytes 196616 | tf_op jit(solution)/shard_map/ppermute | solution.py:85
  24.4 1.0 bitcast_dynamic-update-slice_fusion.14
  25.5 2.8 %collective-permute-start.3 = (bf16[4,32,1024]{2,1,0:T(8,128)(2,1)S(1)}, bf16[4,32,1024]{2,1,0:T(8,128)(2,1)S(1)}, u32[]{:S(2)}, u32[]{:S(2)}) collective-permute-start(bf16[4,32,1024]{2,1,0:T(8,128)(2,1)S(1)} %get-tuple-element.14), channel_id=1, source_target_pairs={{4,0},{8,4},{12,8},{0,12},{5,1},{9,5},{13,9},{1,13},{6,2},{10,6},{... | collective-permute-start | bytes 786440 | tf_op jit(solution)/shard_map/ppermute | solution.py:84
  28.3 4.1 %collective-permute-done.3 = bf16[4,32,1024]{2,1,0:T(8,128)(2,1)S(1)} collective-permute-done((bf16[4,32,1024]{2,1,0:T(8,128)(2,1)S(1)}, bf16[4,32,1024]{2,1,0:T(8,128)(2,1)S(1)}, u32[]{:S(2)}, u32[]{:S(2)}) %collective-permute-start.3) | collective-permute-done | bytes 262176 | tf_op jit(solution)/shard_map/ppermute | solution.py:84
  32.4 3.4 %collective-permute-start.4 = (bf16[4,32,1024]{2,1,0:T(8,128)(2,1)S(1)}, bf16[4,32,1024]{2,1,0:T(8,128)(2,1)S(1)}, u32[]{:S(2)}, u32[]{:S(2)}) collective-permute-start(bf16[4,32,1024]{2,1,0:T(8,128)(2,1)S(1)} %collective-permute-done.3), channel_id=1, source_target_pairs={{4,0},{8,4},{12,8},{0,12},{5,1},{9,5},{13,9},{1,13},{6,2},{10,6},{... | collective-permute-start | bytes 786440 | tf_op jit(solution)/shard_map/ppermute | solution.py:85
  35.8 3.3 %collective-permute-done.4 = bf16[4,32,1024]{2,1,0:T(8,128)(2,1)S(1)} collective-permute-done((bf16[4,32,1024]{2,1,0:T(8,128)(2,1)S(1)}, bf16[4,32,1024]{2,1,0:T(8,128)(2,1)S(1)}, u32[]{:S(2)}, u32[]{:S(2)}) %collective-permute-start.4) | collective-permute-done | bytes 262176 | tf_op jit(solution)/shard_map/ppermute | solution.py:85
  39.1 3.1 %collective-permute-done.5 = bf16[4,32,1024]{2,1,0:T(8,128)(2,1)S(1)} collective-permute-done((bf16[4,32,1024]{2,1,0:T(8,128)(2,1)S(1)}, bf16[4,32,1024]{2,1,0:T(8,128)(2,1)S(1)}, u32[]{:S(2)}, u32[]{:S(2)}) %collective-permute-start.5) | collective-permute-done | bytes 262176 | tf_op jit(solution)/shard_map/ppermute | solution.py:83
  42.4 1.3 bitcast_dynamic-update-slice_fusion.6
  43.6 2.6 collective-permute-start.6
  46.2 26.7 %collective-permute-done.6 = bf16[4,4,32,1024]{3,2,1,0:T(8,128)(2,1)S(1)} collective-permute-done((bf16[4,4,32,1024]{3,2,1,0:T(8,128)(2,1)S(1)}, bf16[4,4,32,1024]{3,2,1,0:T(8,128)(2,1)S(1)}, u32[]{:S(2)}, u32[]{:S(2)}) %collective-permute-start.6) | collective-permute-done | bytes 1048608 | tf_op jit(solution)/shard_map/ppermute | solution.py:84
  72.9 2.7 %collective-permute-start.7 = (bf16[4,4,32,1024]{3,2,1,0:T(8,128)(2,1)S(1)}, bf16[4,4,32,1024]{3,2,1,0:T(8,128)(2,1)S(1)}, u32[]{:S(2)}, u32[]{:S(2)}) collective-permute-start(bf16[4,4,32,1024]{3,2,1,0:T(8,128)(2,1)S(1)} %collective-permute-done.6), channel_id=1, source_target_pairs={{16,0},{32,16},{48,32},{0,48},{17,1},{33,17},{49,33},{1,49},{18,2}... | collective-permute-start | bytes 3145736 | tf_op jit(solution)/shard_map/ppermute | solution.py:85
  75.6 1.1 bitcast_dynamic-update-slice_fusion.4
  76.7 42.9 %collective-permute-done.7 = bf16[4,4,32,1024]{3,2,1,0:T(8,128)(2,1)S(1)} collective-permute-done((bf16[4,4,32,1024]{3,2,1,0:T(8,128)(2,1)S(1)}, bf16[4,4,32,1024]{3,2,1,0:T(8,128)(2,1)S(1)}, u32[]{:S(2)}, u32[]{:S(2)}) %collective-permute-start.7) | collective-permute-done | bytes 1048608 | tf_op jit(solution)/shard_map/ppermute | solution.py:85
  119.6 1.1 bitcast_dynamic-update-slice_fusion.2
  120.7 2.3 bitcast_dynamic-update-slice_fusion
  123.0 1.1 bitcast_dynamic-update-slice_fusion.7
  124.1 1.1 bitcast_dynamic-update-slice_fusion.5
  125.2 1.1 bitcast_dynamic-update-slice_fusion.3
  126.3 2.3 bitcast_dynamic-update-slice_fusion.1
  128.6 5.0 %constant_dynamic-slice_fusion = bf16[4,4,4,32,1024]{4,3,2,1,0:T(8,128)(2,1)} fusion(bf16[8,4,4,32,1024]{4,3,2,1,0:T(8,128)(2,1)} %bitcast_dynamic-update-slice_fusion.1, s32[]{:T(128)S(6)} %select_n.107), kind=kLoop, calls=%fused_computation.120 | loop fusion | bytes 8388612 | tf_op jit(solution)/shard_map/jit(_roll_dynamic)/dynamic_slice | solution.py:88
  133.6 5.5 %collective-permute-start.9 = (bf16[2048,1024]{1,0:T(8,128)(2,1)}, bf16[2048,1024]{1,0:T(8,128)(2,1)}, u32[]{:S(2)}, u32[]{:S(2)}) collective-permute-start(bf16[2048,1024]{1,0:T(8,128)(2,1)} %bitcast.13), channel_id=1, source_target_pairs={{0,64},{64,0},{1,65},{65,1},{2,66},{66,2},{3,67},{67,3},{4,68},{68... | collective-permute-start | bytes 12582920 | tf_op jit(solution)/shard_map/ppermute | solution.py:131
  139.6 1.1 scatter_custom_fusion
  141.5 7.7 %all-to-all-start = ((s32[128,1,2]{2,1,0:T(1,128)}), s32[128,1,2]{2,1,0:T(1,128)S(1)}, u32[]{:S(2)}, u32[]{:S(2)}) async-start(s32[128,1,2]{2,1,0:T(1,128)} %bitcast.27), calls=%async_computation | async-start | bytes 131072 | tf_op jit(solution)/shard_map/all_to_all | solution.py:170
  149.2 0.9 slice.21
  150.2 8.2 %all-to-all-done = s32[128,1,2]{2,1,0:T(1,128)S(1)} async-done(((s32[128,1,2]{2,1,0:T(1,128)}), s32[128,1,2]{2,1,0:T(1,128)S(1)}, u32[]{:S(2)}, u32[]{:S(2)}) %all-to-all-start) | async-done | bytes 1056 | tf_op jit(solution)/shard_map/all_to_all | solution.py:170
  158.5 2.9 %convolution_bitcast_fusion.1 = bf16[4,1024]{1,0:T(4,128)(2,1)S(1)} fusion(bf16[2048,1024]{1,0:T(8,128)(2,1)} %bitcast.13, bf16[4,1,2048]{2,0,1:T(4,128)(2,1)S(1)} %copy.85), kind=kOutput, calls=%fused_computation.55 | convolution fusion | flops 16777216 | bytes 4218880 | tf_op jit(solution)/shard_map/dot_general | solution.py:132
  161.4 2.8 %convolution_bitcast_fusion = bf16[4,1024]{1,0:T(4,128)(2,1)S(1)} fusion(bf16[2048,1024]{1,0:T(8,128)(2,1)} %collective-permute-done.9, bf16[4,1,2048]{2,0,1:T(4,128)(2,1)S(1)} %copy.85), kind=kOutput, calls=%fused_computation.54 | convolution fusion | flops 16777216 | bytes 4218880 | tf_op jit(solution)/shard_map/dot_general | solution.py:133
  164.4 5.2 %fusion.35 = bf16[1024,2,256]{0,2,1:T(8,128)(2,1)S(1)} fusion(bf16[1024,2048,1]{1,0,2:T(8,128)(2,1)} %bitcast.168, bf16[2,2048,2432]{2,1,0:T(8,128)(2,1)} %bitcast.162), kind=kOutput, calls=%fused_computation.47 | convolution fusion | flops 2148007936 | bytes 7340032 | tf_op jit(solution)/shard_map/td,gdc->tgc/dot_general | solution.py:139
  172.0 2.0 copy.55
  174.0 4.7 %all-to-all-start.1 = ((bf16[128,2,2048]{2,1,0:T(2,128)(2,1)}), bf16[128,2,2048]{2,1,0:T(2,128)(2,1)S(1)}, u32[]{:S(2)}, u32[]{:S(2)}) async-start(bf16[128,2,2048]{2,1,0:T(2,128)(2,1)} %copy.55), calls=%async_computation.1 | async-start | bytes 2097152 | tf_op jit(solution)/shard_map/all_to_all | solution.py:172
  179.4 1.3 slice.33
  180.7 1.1 copy.57
  181.9 14.6 %all-to-all-done.1 = bf16[128,2,2048]{2,1,0:T(2,128)(2,1)S(1)} async-done(((bf16[128,2,2048]{2,1,0:T(2,128)(2,1)}), bf16[128,2,2048]{2,1,0:T(2,128)(2,1)S(1)}, u32[]{:S(2)}, u32[]{:S(2)}) %all-to-all-start.1) | async-done | bytes 1048608 | tf_op jit(solution)/shard_map/all_to_all | solution.py:172
  197.9 8.2 %fusion.9 = bf16[128,2,2048]{2,0,1:T(8,128)(2,1)S(1)} fusion(bf16[2,2048,2432]{2,1,0:T(8,128)(2,1)} %bitcast.164, bf16[128,2048]{1,0:T(8,128)(2,1)S(1)} %gather_fusion, pred[128]{0:T(512)(128)(4,1)S(1)} %get-tuple-element.9), kind=kOutput, calls=%fused_computation.18 | convolution fusion | flops 2148270080 | bytes 18350208 | tf_op jit(solution)/shard_map/td,gdc->tgc/dot_general | solution.py:175
  208.1 1.5 fusion.38
  209.6 3.4 %fusion.83 = (f32[32,128]{1,0:T(8,128)S(1)}, f32[32,128,128]{1,2,0:T(8,128)}) fusion(pred[128,128]{0,1:T(8,128)(4,1)S(1)} %iota_compare_fusion.4, bf16[128,32,128]{0,2,1:T(8,128)(2,1)} %fusion.38, bf16[128,32,128]{0,2,1:T(8,128)(2,1)S(1)} %bitcast.146), kind=kOutput, calls=%fused_computation.140 | convolution fusion | flops 136315008 | bytes 4227072 | tf_op jit(solution)/shard_map/jvp()/sub | solution.py:49
  213.6 1.1 copy-done.2
  220.9 2.3 convolution_convert_fusion
  223.2 10.9 %fusion.12 = bf16[256,2048]{1,0:T(8,128)(2,1)S(1)} fusion(bf16[2,2048,2432]{2,1,0:T(8,128)(2,1)} %bitcast.165, bf16[32,2,8,2048]{3,2,1,0:T(8,128)(2,1)} %bitcast.158), kind=kOutput, calls=%fused_computation.19 | convolution fusion | flops 4295491584 | bytes 19922944 | tf_op jit(solution)/shard_map/tgc,gdc->td/dot_general | solution.py:189
  234.1 1.5 reshape.183
  235.6 5.5 %all-to-all-start.2 = ((bf16[128,2,2048]{2,1,0:T(2,128)(2,1)}), bf16[128,2,2048]{2,1,0:T(2,128)(2,1)S(1)}, u32[]{:S(2)}, u32[]{:S(2)}) async-start(bf16[128,2,2048]{2,1,0:T(2,128)(2,1)} %reshape.183), calls=%async_computation.2 | async-start | bytes 2097152 | tf_op jit(solution)/shard_map/all_to_all | solution.py:195
  242.6 1.3 copy.72
  243.9 15.1 %all-to-all-done.2 = bf16[128,2,2048]{2,1,0:T(2,128)(2,1)S(1)} async-done(((bf16[128,2,2048]{2,1,0:T(2,128)(2,1)}), bf16[128,2,2048]{2,1,0:T(2,128)(2,1)S(1)}, u32[]{:S(2)}, u32[]{:S(2)}) %all-to-all-start.2) | async-done | bytes 1048608 | tf_op jit(solution)/shard_map/all_to_all | solution.py:195
  259.4 1.0 fusion.60
  (86 shorter events, 21.7 us)
Async XLA Ops:
  7.2 157.2 %all-gather.2.cloned.1.call-start = ((), (), s32[]{:S(2)}) async-start(), calls=%async_computation.3 | async-start | bytes 20078592 | tf_op jit(solution)/shard_map/all_gather | solution.py:125
  10.4 5.9 %collective-permute-start = (bf16[32,1024]{1,0:T(8,128)(2,1)S(1)}, bf16[32,1024]{1,0:T(8,128)(2,1)S(1)}, u32[]{:S(2)}, u32[]{:S(2)}) collective-permute-start(bf16[32,1024]{1,0:T(8,128)(2,1)S(1)} %get-tuple-element.16), channel_id=1, source_target_pairs={{1,0},{2,1},{3,2},{0,3},{5,4},{6,5},{7,6},{4,7},{9,8},{10,9},{11,1... | collective-permute-start | bytes 196616 | tf_op jit(solution)/shard_map/ppermute | solution.py:84
  15.0 6.3 %collective-permute-start.2 = (bf16[32,1024]{1,0:T(8,128)(2,1)S(1)}, bf16[32,1024]{1,0:T(8,128)(2,1)S(1)}, u32[]{:S(2)}, u32[]{:S(2)}) collective-permute-start(bf16[32,1024]{1,0:T(8,128)(2,1)S(1)} %get-tuple-element.16), channel_id=1, source_target_pairs={{0,1},{1,2},{2,3},{3,0},{4,5},{5,6},{6,7},{7,4},{8,9},{9,10},{10,1... | collective-permute-start | bytes 196616 | tf_op jit(solution)/shard_map/ppermute | solution.py:83
  16.3 4.3 %collective-permute-start.1 = (bf16[32,1024]{1,0:T(8,128)(2,1)S(1)}, bf16[32,1024]{1,0:T(8,128)(2,1)S(1)}, u32[]{:S(2)}, u32[]{:S(2)}) collective-permute-start(bf16[32,1024]{1,0:T(8,128)(2,1)S(1)} %collective-permute-done), channel_id=1, source_target_pairs={{1,0},{2,1},{3,2},{0,3},{5,4},{6,5},{7,6},{4,7},{9,8},{10,9},{11,1... | collective-permute-start | bytes 196616 | tf_op jit(solution)/shard_map/ppermute | solution.py:85
  25.5 6.9 %collective-permute-start.3 = (bf16[4,32,1024]{2,1,0:T(8,128)(2,1)S(1)}, bf16[4,32,1024]{2,1,0:T(8,128)(2,1)S(1)}, u32[]{:S(2)}, u32[]{:S(2)}) collective-permute-start(bf16[4,32,1024]{2,1,0:T(8,128)(2,1)S(1)} %get-tuple-element.14), channel_id=1, source_target_pairs={{4,0},{8,4},{12,8},{0,12},{5,1},{9,5},{13,9},{1,13},{6,2},{10,6},{... | collective-permute-start | bytes 786440 | tf_op jit(solution)/shard_map/ppermute | solution.py:84
  32.4 6.7 %collective-permute-start.4 = (bf16[4,32,1024]{2,1,0:T(8,128)(2,1)S(1)}, bf16[4,32,1024]{2,1,0:T(8,128)(2,1)S(1)}, u32[]{:S(2)}, u32[]{:S(2)}) collective-permute-start(bf16[4,32,1024]{2,1,0:T(8,128)(2,1)S(1)} %collective-permute-done.3), channel_id=1, source_target_pairs={{4,0},{8,4},{12,8},{0,12},{5,1},{9,5},{13,9},{1,13},{6,2},{10,6},{... | collective-permute-start | bytes 786440 | tf_op jit(solution)/shard_map/ppermute | solution.py:85
  35.8 6.4 %collective-permute-start.5 = (bf16[4,32,1024]{2,1,0:T(8,128)(2,1)S(1)}, bf16[4,32,1024]{2,1,0:T(8,128)(2,1)S(1)}, u32[]{:S(2)}, u32[]{:S(2)}) collective-permute-start(bf16[4,32,1024]{2,1,0:T(8,128)(2,1)S(1)} %get-tuple-element.14), channel_id=1, source_target_pairs={{0,4},{4,8},{8,12},{12,0},{1,5},{5,9},{9,13},{13,1},{2,6},{6,10},{... | collective-permute-start | bytes 786440 | tf_op jit(solution)/shard_map/ppermute | solution.py:83
  43.6 29.3 %collective-permute-start.6 = (bf16[4,4,32,1024]{3,2,1,0:T(8,128)(2,1)S(1)}, bf16[4,4,32,1024]{3,2,1,0:T(8,128)(2,1)S(1)}, u32[]{:S(2)}, u32[]{:S(2)}) collective-permute-start(bf16[4,4,32,1024]{3,2,1,0:T(8,128)(2,1)S(1)} %get-tuple-element.12), channel_id=1, source_target_pairs={{16,0},{32,16},{48,32},{0,48},{17,1},{33,17},{49,33},{1,49},{18,2}... | collective-permute-start | bytes 3145736 | tf_op jit(solution)/shard_map/ppermute | solution.py:84
  72.9 46.6 %collective-permute-start.7 = (bf16[4,4,32,1024]{3,2,1,0:T(8,128)(2,1)S(1)}, bf16[4,4,32,1024]{3,2,1,0:T(8,128)(2,1)S(1)}, u32[]{:S(2)}, u32[]{:S(2)}) collective-permute-start(bf16[4,4,32,1024]{3,2,1,0:T(8,128)(2,1)S(1)} %collective-permute-done.6), channel_id=1, source_target_pairs={{16,0},{32,16},{48,32},{0,48},{17,1},{33,17},{49,33},{1,49},{18,2}... | collective-permute-start | bytes 3145736 | tf_op jit(solution)/shard_map/ppermute | solution.py:85
  75.6 45.0 %collective-permute-start.8 = (bf16[4,4,32,1024]{3,2,1,0:T(8,128)(2,1)S(1)}, bf16[4,4,32,1024]{3,2,1,0:T(8,128)(2,1)}, u32[]{:S(2)}, u32[]{:S(2)}) collective-permute-start(bf16[4,4,32,1024]{3,2,1,0:T(8,128)(2,1)S(1)} %get-tuple-element.12), channel_id=1, source_target_pairs={{0,16},{16,32},{32,48},{48,0},{1,17},{17,33},{33,49},{49,1},{2,18}... | collective-permute-start | bytes 3145736 | tf_op jit(solution)/shard_map/ppermute | solution.py:83
  128.6 10.6 %copy-start.8 = (s32[1,128,1]{1,2,0:T(1,128)S(1)}, s32[1,128,1]{1,2,0:T(1,128)}, u32[]{:S(2)}) copy-start(s32[1,128,1]{1,2,0:T(1,128)} %param.19) | copy-start | bytes 1540
  133.6 27.8 %collective-permute-start.9 = (bf16[2048,1024]{1,0:T(8,128)(2,1)}, bf16[2048,1024]{1,0:T(8,128)(2,1)}, u32[]{:S(2)}, u32[]{:S(2)}) collective-permute-start(bf16[2048,1024]{1,0:T(8,128)(2,1)} %bitcast.13), channel_id=1, source_target_pairs={{0,64},{64,0},{1,65},{65,1},{2,66},{66,2},{3,67},{67,3},{4,68},{68... | collective-permute-start | bytes 12582920 | tf_op jit(solution)/shard_map/ppermute | solution.py:131
  141.5 17.0 %all-to-all-start = ((s32[128,1,2]{2,1,0:T(1,128)}), s32[128,1,2]{2,1,0:T(1,128)S(1)}, u32[]{:S(2)}, u32[]{:S(2)}) async-start(s32[128,1,2]{2,1,0:T(1,128)} %bitcast.27), calls=%async_computation | async-start | bytes 131072 | tf_op jit(solution)/shard_map/all_to_all | solution.py:170
  169.7 1.7 copy-start.7
  171.5 2.6 copy-start.6
  172.0 6.7 %copy-start.4 = (bf16[1,128,4096]{2,1,0:T(8,128)(2,1)S(1)}, bf16[1,128,4096]{2,1,0:T(8,128)(2,1)}, u32[]{:S(2)}) copy-start(bf16[1,128,4096]{2,1,0:T(8,128)(2,1)} %param.21) | copy-start | bytes 3145732
  174.0 22.5 %all-to-all-start.1 = ((bf16[128,2,2048]{2,1,0:T(2,128)(2,1)}), bf16[128,2,2048]{2,1,0:T(2,128)(2,1)S(1)}, u32[]{:S(2)}, u32[]{:S(2)}) async-start(bf16[128,2,2048]{2,1,0:T(2,128)(2,1)} %copy.55), calls=%async_computation.1 | async-start | bytes 2097152 | tf_op jit(solution)/shard_map/all_to_all | solution.py:172
  206.2 1.3 copy-start.5
  206.8 1.3 copy-start
  213.1 1.6 copy-start.2
  215.4 1.2 copy-start.3
  217.9 1.2 copy-start.1
  235.6 23.3 %all-to-all-start.2 = ((bf16[128,2,2048]{2,1,0:T(2,128)(2,1)}), bf16[128,2,2048]{2,1,0:T(2,128)(2,1)S(1)}, u32[]{:S(2)}, u32[]{:S(2)}) async-start(bf16[128,2,2048]{2,1,0:T(2,128)(2,1)} %reshape.183), calls=%async_computation.2 | async-start | bytes 2097152 | tf_op jit(solution)/shard_map/all_to_all | solution.py:195
Sparse Core Ops, SparseCore 0:
  11.1 113.4 all-gather.1

commit v10 on v6

--- a/solution.py
+++ b/solution.py
@@ -158,18 +158,18 @@
         lambda values: user_layer(values, user_gain, query_map), hidden
     )
     (grad_hidden,) = pull(cotangent[0])
-    slot_of = (
-        position[None, :] == jnp.arange(devices * cap_slots, dtype=jnp.int32)[:, None]
-    ).astype(grad_hidden.dtype)
-    slot_grads = jnp.dot(slot_of, grad_hidden, preferred_element_type=jnp.float32).astype(
-        grad_hidden.dtype
-    )
-    outgoing = jnp.einsum(
+    grad_rows = jnp.einsum(
         "tgc,gdc->td",
-        slot_grads.reshape(slot_grads.shape[0], groups, -1),
+        grad_hidden.reshape(grad_hidden.shape[0], groups, -1),
         adapter_halves,
         preferred_element_type=jnp.float32,
     ).astype(jnp.bfloat16)
+    slot_of = (
+        position[None, :] == jnp.arange(devices * cap_slots, dtype=jnp.int32)[:, None]
+    ).astype(grad_rows.dtype)
+    outgoing = jnp.dot(slot_of, grad_rows, preferred_element_type=jnp.float32).astype(
+        grad_rows.dtype
+    )
     arrived = lax.all_to_all(
         outgoing.reshape(devices, cap_slots, DI),
         ("grp", "fsdp"),

time: 226 us -> 227 us (level)
  no operation moved by 1% of the time
where the time goes in v10:
time: 227 us; the launch traced here: 226 us
  waiting for transfers between devices  117 us (52%)
  matrix products  42.8 us (19%)
  starting transfers between devices  24.3 us (11%)
  local copies, waits for them, and re-layouts  16.1 us (7%)
  between operations  14.4 us (6%)
  other arithmetic  9.95 us (4%)
    all_gather x1, waiting for transfers between devices, per_device(): lax.all_gather(pack_halves(sources), ('grp', 'fsdp'), axis=0, tiled=True)  78.9 us
    all_to_all x1, waiting for transfers between devices, per_device(): lax.all_to_all(outgoing.reshape(devices, cap_slots, DI), ('grp', 'fsdp'),...  15.1 us
    all_to_all x1, waiting for transfers between devices, per_device(): lax.all_to_all(found, ('grp', 'fsdp'), split_axis=0, concat_axis=0, tiled...  14.7 us
    dot_general x1, matrix products, per_device(): jnp.einsum('tgc,gdc->td', grad_hidden.reshape(grad_hidden.shape[0], group...  11.8 us
    all_to_all x1, starting transfers between devices, per_device(): lax.all_to_all(request, ('grp', 'fsdp'), split_axis=0, concat_axis=0, til...  11.5 us
    all_to_all x1, waiting for transfers between devices, per_device(): lax.all_to_all(request, ('grp', 'fsdp'), split_axis=0, concat_axis=0, til...  8.29 us
    dot_general x1, matrix products, per_device(): jnp.einsum('td,gdc->tgc', fetched, adapter_halves, preferred_element_type...  8.24 us
    all_to_all x1, starting transfers between devices, per_device(): lax.all_to_all(found, ('grp', 'fsdp'), split_axis=0, concat_axis=0, tiled...  7.26 us
  transfers between devices with their start and end apart: 4, of which 4 were waited for; matrix products, arithmetic and copies ran while one was open for 5% of the time, Pallas kernels for 0%

profile of v10, /device:TPU:1, one launch (start us, length us, event | category | flops | bytes accessed | tf_op | source)
XLA Modules:
  0.0 226.2 jit_solution(8200844994504663367)
XLA Ops:
  7.2 1.7 shard_map.130
  9.0 0.7 fusion.61
  9.9 0.8 select_reduce_fusion
  10.7 0.7 fusion.65
  11.4 1.1 scatter_custom_fusion
  12.5 0.8 all_to_all.12
  13.3 11.5 %all-to-all-start = ((s32[128,1,2]{2,1,0:T(1,128)}), s32[128,1,2]{2,1,0:T(1,128)S(1)}, u32[]{:S(2)}, u32[]{:S(2)}) async-start(s32[128,1,2]{2,1,0:T(1,128)} %bitcast.15), calls=%async_computation | async-start | bytes 131072 | tf_op jit(solution)/shard_map/all_to_all | solution.py:148
  24.8 1.0 slice.24
  25.8 8.3 %all-to-all-done = s32[128,1,2]{2,1,0:T(1,128)S(1)} async-done(((s32[128,1,2]{2,1,0:T(1,128)}), s32[128,1,2]{2,1,0:T(1,128)S(1)}, u32[]{:S(2)}, u32[]{:S(2)}) %all-to-all-start) | async-done | bytes 1056 | tf_op jit(solution)/shard_map/all_to_all | solution.py:148
  34.2 78.9 %all-gather.2.cloned.1.call-done = bf16[4096,3456]{1,0:T(8,128)(2,1)} async-done(((bf16[32,3456]{1,0:T(8,128)(2,1)}), bf16[4096,3456]{1,0:T(8,128)(2,1)}) %all-gather.2.cloned.1.call-update) | async-done | bytes 28311568 | tf_op jit(solution)/shard_map/all_gather | solution.py:111
  113.1 4.6 %fusion.43 = bf16[2,1024,4]{1,2,0:T(4,128)(2,1)S(1)} fusion(bf16[2,2048,3456]{2,1,0:T(8,128)(2,1)} %bitcast.118, bf16[4,1,2048]{2,1,0:T(2,128)(2,1)S(1)} %slice.24), kind=kOutput, calls=%fused_computation.54 | convolution fusion | flops 33562624 | bytes 8421376 | tf_op jit(solution)/shard_map/id,gdc->igc/dot_general | solution.py:119
  117.8 5.3 %fusion.35 = bf16[1024,2,256]{0,2,1:T(8,128)(2,1)S(1)} fusion(bf16[1024,2048,1]{1,0,2:T(8,128)(2,1)} %bitcast.126, bf16[2,2048,3456]{2,1,0:T(8,128)(2,1)} %bitcast.119), kind=kOutput, calls=%fused_computation.47 | convolution fusion | flops 2148007936 | bytes 7340032 | tf_op jit(solution)/shard_map/td,gdc->tgc/dot_general | solution.py:114
  123.5 0.4 reshape.172
  124.9 0.5 convolution_convert_fusion.1
  125.4 2.0 copy.53
  127.5 7.3 %all-to-all-start.1 = ((bf16[128,2,2048]{2,1,0:T(2,128)(2,1)}), bf16[128,2,2048]{2,1,0:T(2,128)(2,1)S(1)}, u32[]{:S(2)}, u32[]{:S(2)}) async-start(bf16[128,2,2048]{2,1,0:T(2,128)(2,1)} %copy.53), calls=%async_computation.1 | async-start | bytes 2097152 | tf_op jit(solution)/shard_map/all_to_all | solution.py:150
  134.8 0.7 copy.61
  135.5 1.3 slice.38
  136.8 1.1 copy.55
  137.9 14.7 %all-to-all-done.1 = bf16[128,2,2048]{2,1,0:T(2,128)(2,1)S(1)} async-done(((bf16[128,2,2048]{2,1,0:T(2,128)(2,1)}), bf16[128,2,2048]{2,1,0:T(2,128)(2,1)S(1)}, u32[]{:S(2)}, u32[]{:S(2)}) %all-to-all-start.1) | async-done | bytes 1048608 | tf_op jit(solution)/shard_map/all_to_all | solution.py:150
  152.6 0.4 reshape.175
  153.0 0.9 gather_fusion
  154.0 8.2 %fusion.8 = bf16[128,2,2048]{2,0,1:T(8,128)(2,1)S(1)} fusion(bf16[2,2048,3456]{2,1,0:T(8,128)(2,1)} %bitcast.121, bf16[128,2048]{1,0:T(8,128)(2,1)S(1)} %gather_fusion, pred[128]{0:T(512)(128)(4,1)S(1)} %get-tuple-element.9), kind=kOutput, calls=%fused_computation.18 | convolution fusion | flops 2148270080 | bytes 18350208 | tf_op jit(solution)/shard_map/td,gdc->tgc/dot_general | solution.py:153
  162.2 0.7 copy.54
  162.9 0.6 fusion.24
  163.5 0.7 fusion.26
  164.2 1.5 fusion.39
  165.7 1.5 fusion.38
  167.2 3.5 %fusion.80 = (f32[32,128]{1,0:T(8,128)S(1)}, f32[32,128,128]{1,2,0:T(8,128)}) fusion(pred[128,128]{0,1:T(8,128)(4,1)S(1)} %iota_compare_fusion.4, bf16[128,32,128]{0,2,1:T(8,128)(2,1)} %fusion.38, bf16[128,32,128]{0,2,1:T(8,128)(2,1)S(1)} %bitcast.103), kind=kOutput, calls=%fused_computation.106 | convolution fusion | flops 136315008 | bytes 4227072 | tf_op jit(solution)/shard_map/jvp()/sub | solution.py:49
  170.7 2.6 %fusion.22 = (f32[32,128]{1,0:T(8,128)S(1)}, bf16[32,128,128]{1,2,0:T(8,128)(2,1)S(1)}) fusion(f32[32,128,128]{1,2,0:T(8,128)} %get-tuple-element.22, bf16[32,128,128]{1,2,0:T(8,128)(2,1)} %fusion.39, f32[32,128]{1,0:T(8,128)S(1)} %multiply_divide_fusion, f32[32,128]{1,0:T(8,128)S(1)} %get-tuple-element.21), kind=kLoop, calls=%fused_computation.28 | loop fusion | flops 3141632 | bytes 4243456 | tf_op jit(solution)/shard_map/transpose(jvp())/reduce_sum | solution.py:49
  173.6 0.8 fusion.40
  174.4 0.4 copy-done.4
  174.8 0.9 fusion.76
  175.7 0.5 fusion.83
  176.1 0.8 fusion.84
  177.3 0.8 add_convert_fusion
  178.2 0.9 fusion.28
  179.1 1.7 fusion.46
  180.8 11.8 %fusion.14 = bf16[128,2048]{1,0:T(8,128)(2,1)S(1)} fusion(bf16[128,2,2048]{0,2,1:T(8,128)(2,1)} %bitcast.116, bf16[2,2048,3456]{2,1,0:T(8,128)(2,1)} %bitcast.122), kind=kOutput, calls=%fused_computation.22 | convolution fusion | flops 2147745792 | bytes 18350080 | tf_op jit(solution)/shard_map/tgc,gdc->td/dot_general | solution.py:161
  192.7 0.4 convolution_convert_fusion
  193.1 1.5 reshape.181
  194.6 5.5 %all-to-all-start.2 = ((bf16[128,2,2048]{2,1,0:T(2,128)(2,1)}), bf16[128,2,2048]{2,1,0:T(2,128)(2,1)S(1)}, u32[]{:S(2)}, u32[]{:S(2)}) async-start(bf16[128,2,2048]{2,1,0:T(2,128)(2,1)} %reshape.181), calls=%async_computation.2 | async-start | bytes 2097152 | tf_op jit(solution)/shard_map/all_to_all | solution.py:173
  200.1 0.5 broadcast.138
  200.6 0.8 reduce.4
  201.6 1.3 copy.70
  202.9 15.1 %all-to-all-done.2 = bf16[128,2,2048]{2,1,0:T(2,128)(2,1)S(1)} async-done(((bf16[128,2,2048]{2,1,0:T(2,128)(2,1)}), bf16[128,2,2048]{2,1,0:T(2,128)(2,1)S(1)}, u32[]{:S(2)}, u32[]{:S(2)}) %all-to-all-start.2) | async-done | bytes 1048608 | tf_op jit(solution)/shard_map/all_to_all | solution.py:173
  218.0 0.4 reshape.182
  218.4 1.0 fusion.58
  (42 shorter events, 2.8 us)
Async XLA Ops:
  7.2 105.9 %all-gather.2.cloned.1.call-start = ((), (), s32[]{:S(2)}) async-start(), calls=%async_computation.3 | async-start | bytes 28532736 | tf_op jit(solution)/shard_map/all_gather | solution.py:111
  13.3 20.9 %all-to-all-start = ((s32[128,1,2]{2,1,0:T(1,128)}), s32[128,1,2]{2,1,0:T(1,128)S(1)}, u32[]{:S(2)}, u32[]{:S(2)}) async-start(s32[128,1,2]{2,1,0:T(1,128)} %bitcast.15), calls=%async_computation | async-start | bytes 131072 | tf_op jit(solution)/shard_map/all_to_all | solution.py:148
  123.1 1.7 copy-start.8
  124.9 2.6 %copy-start.7 = (bf16[4,2048]{1,0:T(4,128)(2,1)}, bf16[4,2048]{1,0:T(4,128)(2,1)S(1)}, u32[]{:S(2)}) copy-start(bf16[4,2048]{1,0:T(4,128)(2,1)S(1)} %multiply_convert_fusion) | copy-start | bytes 49156
  125.4 9.3 %copy-start.5 = (bf16[1,128,4096]{2,1,0:T(8,128)(2,1)S(1)}, bf16[1,128,4096]{2,1,0:T(8,128)(2,1)}, u32[]{:S(2)}) copy-start(bf16[1,128,4096]{2,1,0:T(8,128)(2,1)} %param.21) | copy-start | bytes 3145732
  127.5 8.0 %copy-start.9 = (s32[1,128,1]{1,2,0:T(1,128)S(1)}, s32[1,128,1]{1,2,0:T(1,128)}, u32[]{:S(2)}) copy-start(s32[1,128,1]{1,2,0:T(1,128)} %param.19) | copy-start | bytes 1540
  127.5 25.1 %all-to-all-start.1 = ((bf16[128,2,2048]{2,1,0:T(2,128)(2,1)}), bf16[128,2,2048]{2,1,0:T(2,128)(2,1)S(1)}, u32[]{:S(2)}, u32[]{:S(2)}) async-start(bf16[128,2,2048]{2,1,0:T(2,128)(2,1)} %copy.53), calls=%async_computation.1 | async-start | bytes 2097152 | tf_op jit(solution)/shard_map/all_to_all | solution.py:150
  162.2 1.2 copy-start.6
  164.2 1.5 copy-start
  170.7 2.6 %copy-start.2 = (bf16[32,128,128]{1,2,0:T(8,128)(2,1)S(1)}, bf16[32,128,128]{1,2,0:T(8,128)(2,1)}, u32[]{:S(2)}) copy-start(bf16[32,128,128]{1,2,0:T(8,128)(2,1)} %fusion.39) | copy-start | bytes 3145732
  170.7 2.9 %copy-start.3 = (f32[32,128,128]{1,2,0:T(8,128)S(1)}, f32[32,128,128]{1,2,0:T(8,128)}, u32[]{:S(2)}) copy-start(f32[32,128,128]{1,2,0:T(8,128)} %get-tuple-element.22) | copy-start | bytes 6291460
  173.6 1.2 copy-start.4
  176.1 1.2 copy-start.1
  194.6 23.3 %all-to-all-start.2 = ((bf16[128,2,2048]{2,1,0:T(2,128)(2,1)}), bf16[128,2,2048]{2,1,0:T(2,128)(2,1)S(1)}, u32[]{:S(2)}, u32[]{:S(2)}) async-start(bf16[128,2,2048]{2,1,0:T(2,128)(2,1)} %reshape.181), calls=%async_computation.2 | async-start | bytes 2097152 | tf_op jit(solution)/shard_map/all_to_all | solution.py:173
Sparse Core Ops, SparseCore 0:
  11.6 101.4 all-gather.1

commit v11 on v10

--- a/solution.py
+++ b/solution.py
@@ -146,9 +146,11 @@
     request = request.reshape(devices, cap_slots)
     width = item_embed.shape[1]
     incoming = lax.all_to_all(request, ("grp", "fsdp"), split_axis=0, concat_axis=0, tiled=True)
-    found = serve_rows(incoming, item_embed)
-    returned = lax.all_to_all(found, ("grp", "fsdp"), split_axis=0, concat_axis=0, tiled=True)
-    fetched = jnp.take(returned.reshape(devices * cap_slots, width), position, axis=0)
+    found = jnp.swapaxes(serve_rows(incoming, item_embed), 0, 1)
+    returned = lax.all_to_all(found, ("grp", "fsdp"), split_axis=1, concat_axis=1, tiled=True)
+    fetched = jnp.take(
+        returned.reshape(devices * cap_slots, width), rank_in * devices + owner_users, axis=0
+    )
     hidden = stored(
         jnp.einsum("td,gdc->tgc", fetched, adapter_halves, preferred_element_type=jnp.float32).reshape(
             fetched.shape[0], -1
@@ -165,21 +167,22 @@
         preferred_element_type=jnp.float32,
     ).astype(jnp.bfloat16)
     slot_of = (
-        position[None, :] == jnp.arange(devices * cap_slots, dtype=jnp.int32)[:, None]
+        (rank_in * devices + owner_users)[None, :]
+        == jnp.arange(devices * cap_slots, dtype=jnp.int32)[:, None]
     ).astype(grad_rows.dtype)
     outgoing = jnp.dot(slot_of, grad_rows, preferred_element_type=jnp.float32).astype(
         grad_rows.dtype
     )
     arrived = lax.all_to_all(
-        outgoing.reshape(devices, cap_slots, DI),
+        outgoing.reshape(cap_slots, devices, DI),
         ("grp", "fsdp"),
-        split_axis=0,
-        concat_axis=0,
+        split_axis=1,
+        concat_axis=1,
         tiled=True,
     ).astype(jnp.float32)
     terms = arrived.reshape(devices * cap_slots, DI)
     slot_hot = (
-        incoming.reshape(-1)[:, None] == jnp.arange(count, dtype=jnp.int32)[None, :]
+        incoming.T.reshape(-1)[:, None] == jnp.arange(count, dtype=jnp.int32)[None, :]
     ).astype(jnp.float32)
     item_grad = jnp.dot(slot_hot.T, terms, precision=lax.Precision.HIGHEST)
     return (item_embed, user_attention_output[None], item_grad)

time: 227 us -> 227 us (level)
  transfers between devices with their start and end apart: 4 -> 4, of which waited for: 4 -> 4; matrix products, arithmetic and copies ran while one was open for 5% -> 4% of each run, Pallas kernels for 0% -> 0%
where the time goes in v11:
time: 227 us
  waiting for transfers between devices  118 us (52%)
  matrix products  42.8 us (19%)
  starting transfers between devices  24.3 us (11%)
  local copies, waits for them, and re-layouts  16 us (7%)
  between operations  14.4 us (6%)
  other arithmetic  9.15 us (4%)
    all_gather x1, waiting for transfers between devices, per_device(): lax.all_gather(pack_halves(sources), ('grp', 'fsdp'), axis=0, tiled=True)  78.9 us
    all_to_all x1, waiting for transfers between devices, per_device(): lax.all_to_all(outgoing.reshape(cap_slots, devices, DI), ('grp', 'fsdp'),...  16.4 us
    all_to_all x1, waiting for transfers between devices, per_device(): lax.all_to_all(found, ('grp', 'fsdp'), split_axis=1, concat_axis=1, tiled...  14.7 us
    dot_general x1, matrix products, per_device(): jnp.einsum('tgc,gdc->td', grad_hidden.reshape(grad_hidden.shape[0], group...  11.8 us
    all_to_all x1, starting transfers between devices, per_device(): lax.all_to_all(request, ('grp', 'fsdp'), split_axis=0, concat_axis=0, til...  11.5 us
    all_to_all x1, waiting for transfers between devices, per_device(): lax.all_to_all(request, ('grp', 'fsdp'), split_axis=0, concat_axis=0, til...  8.29 us
    dot_general x1, matrix products, per_device(): jnp.einsum('td,gdc->tgc', fetched, adapter_halves, preferred_element_type...  8.24 us
    all_to_all x1, starting transfers between devices, per_device(): lax.all_to_all(found, ('grp', 'fsdp'), split_axis=1, concat_axis=1, tiled...  7.26 us
  transfers between devices with their start and end apart: 4, of which 4 were waited for; matrix products, arithmetic and copies ran while one was open for 4% of the time, Pallas kernels for 0%

profile of v11, /device:TPU:1, one launch (start us, length us, event | category | flops | bytes accessed | tf_op | source)
XLA Modules:
  0.0 226.6 jit_solution(3794687089667145)
XLA Ops:
  7.2 1.7 shard_map.130
  9.0 0.7 fusion.62
  9.9 0.8 select_reduce_fusion
  10.7 0.7 fusion.67
  11.4 1.1 scatter_custom_fusion
  12.5 0.8 all_to_all.12
  13.3 11.5 %all-to-all-start = ((s32[128,1,2]{2,1,0:T(1,128)}), s32[128,1,2]{2,1,0:T(1,128)S(1)}, u32[]{:S(2)}, u32[]{:S(2)}) async-start(s32[128,1,2]{2,1,0:T(1,128)} %bitcast.15), calls=%async_computation | async-start | bytes 131072 | tf_op jit(solution)/shard_map/all_to_all | solution.py:148
  24.8 1.0 slice.24
  25.8 8.3 %all-to-all-done = s32[128,1,2]{2,1,0:T(1,128)S(1)} async-done(((s32[128,1,2]{2,1,0:T(1,128)}), s32[128,1,2]{2,1,0:T(1,128)S(1)}, u32[]{:S(2)}, u32[]{:S(2)}) %all-to-all-start) | async-done | bytes 1056 | tf_op jit(solution)/shard_map/all_to_all | solution.py:148
  34.2 78.9 %all-gather.2.cloned.1.call-done = bf16[4096,3456]{1,0:T(8,128)(2,1)} async-done(((bf16[32,3456]{1,0:T(8,128)(2,1)}), bf16[4096,3456]{1,0:T(8,128)(2,1)}) %all-gather.2.cloned.1.call-update) | async-done | bytes 28311568 | tf_op jit(solution)/shard_map/all_gather | solution.py:111
  113.1 4.6 %fusion.44 = bf16[2,1024,4]{1,2,0:T(4,128)(2,1)S(1)} fusion(bf16[2,2048,3456]{2,1,0:T(8,128)(2,1)} %bitcast.140, bf16[4,1,2048]{2,1,0:T(2,128)(2,1)S(1)} %slice.24), kind=kOutput, calls=%fused_computation.55 | convolution fusion | flops 33562624 | bytes 8421376 | tf_op jit(solution)/shard_map/id,gdc->igc/dot_general | solution.py:119
  117.8 5.3 %fusion.36 = bf16[1024,2,256]{0,2,1:T(8,128)(2,1)S(1)} fusion(bf16[1024,2048,1]{1,0,2:T(8,128)(2,1)} %bitcast.149, bf16[2,2048,3456]{2,1,0:T(8,128)(2,1)} %bitcast.141), kind=kOutput, calls=%fused_computation.48 | convolution fusion | flops 2148007936 | bytes 7340032 | tf_op jit(solution)/shard_map/td,gdc->tgc/dot_general | solution.py:114
  123.2 0.4 reshape.196
  123.5 0.4 reshape.195
  124.9 0.5 fusion.11
  125.4 2.0 copy.102
  127.5 7.3 %all-to-all-start.1 = ((bf16[2,128,2048]{2,0,1:T(2,128)(2,1)}), bf16[2,128,2048]{2,0,1:T(2,128)(2,1)S(1)}, u32[]{:S(2)}, u32[]{:S(2)}) async-start(bf16[2,128,2048]{2,0,1:T(2,128)(2,1)} %copy.102), calls=%async_computation.1 | async-start | bytes 2097152 | tf_op jit(solution)/shard_map/all_to_all | solution.py:150
  134.8 0.7 copy.112
  135.5 1.3 slice.38
  136.8 1.1 copy.105
  137.9 14.7 %all-to-all-done.1 = bf16[2,128,2048]{2,0,1:T(2,128)(2,1)S(1)} async-done(((bf16[2,128,2048]{2,0,1:T(2,128)(2,1)}), bf16[2,128,2048]{2,0,1:T(2,128)(2,1)S(1)}, u32[]{:S(2)}, u32[]{:S(2)}) %all-to-all-start.1) | async-done | bytes 1048608 | tf_op jit(solution)/shard_map/all_to_all | solution.py:150
  152.6 0.3 copy.103
  152.9 0.9 gather_fusion
  153.9 8.2 %fusion.8 = bf16[128,2,2048]{2,0,1:T(8,128)(2,1)S(1)} fusion(bf16[2,2048,3456]{2,1,0:T(8,128)(2,1)} %bitcast.143, bf16[128,2048]{1,0:T(8,128)(2,1)S(1)} %gather_fusion, pred[128]{0:T(512)(128)(4,1)S(1)} %get-tuple-element.15), kind=kOutput, calls=%fused_computation.18 | convolution fusion | flops 2148270080 | bytes 18350208 | tf_op jit(solution)/shard_map/td,gdc->tgc/dot_general | solution.py:155
  162.1 0.7 copy.104
  162.8 0.6 fusion.25
  163.4 0.7 fusion.27
  164.1 1.5 fusion.40
  165.6 1.5 fusion.39
  167.1 3.5 %fusion.83 = (f32[32,128]{1,0:T(8,128)S(1)}, f32[32,128,128]{1,2,0:T(8,128)}) fusion(pred[128,128]{0,1:T(8,128)(4,1)S(1)} %iota_compare_fusion.4, bf16[128,32,128]{0,2,1:T(8,128)(2,1)} %fusion.39, bf16[128,32,128]{0,2,1:T(8,128)(2,1)S(1)} %bitcast.122), kind=kOutput, calls=%fused_computation.112 | convolution fusion | flops 136315008 | bytes 4227072 | tf_op jit(solution)/shard_map/jvp()/sub | solution.py:49
  170.6 2.6 %fusion.23 = (f32[32,128]{1,0:T(8,128)S(1)}, bf16[32,128,128]{1,2,0:T(8,128)(2,1)S(1)}) fusion(f32[32,128,128]{1,2,0:T(8,128)} %get-tuple-element.30, bf16[32,128,128]{1,2,0:T(8,128)(2,1)} %fusion.40, f32[32,128]{1,0:T(8,128)S(1)} %multiply_divide_fusion, f32[32,128]{1,0:T(8,128)S(1)} %get-tuple-element.29), kind=kLoop, calls=%fused_computation.29 | loop fusion | flops 3141632 | bytes 4243456 | tf_op jit(solution)/shard_map/transpose(jvp())/reduce_sum | solution.py:49
  173.5 0.8 fusion.41
  174.3 0.4 copy-done.4
  174.7 0.9 fusion.79
  175.6 0.5 fusion.86
  176.1 0.9 fusion.87
  176.9 0.4 copy-done.1
  177.3 0.8 add_convert_fusion
  178.1 0.9 fusion.29
  179.0 1.7 fusion.47
  180.8 11.8 %fusion.15 = bf16[128,2048]{1,0:T(8,128)(2,1)S(1)} fusion(bf16[128,2,2048]{0,2,1:T(8,128)(2,1)} %bitcast.137, bf16[2,2048,3456]{2,1,0:T(8,128)(2,1)} %bitcast.144), kind=kOutput, calls=%fused_computation.23 | convolution fusion | flops 2147745792 | bytes 18350080 | tf_op jit(solution)/shard_map/tgc,gdc->td/dot_general | solution.py:163
  192.6 0.4 convolution_convert_fusion
  193.0 2.1 copy.121
  195.1 5.5 %all-to-all-start.2 = ((bf16[2,128,2048]{2,0,1:T(2,128)(2,1)}), bf16[2,128,2048]{2,0,1:T(2,128)(2,1)S(1)}, u32[]{:S(2)}, u32[]{:S(2)}) async-start(bf16[2,128,2048]{2,0,1:T(2,128)(2,1)} %copy.121), calls=%async_computation.2 | async-start | bytes 2097152 | tf_op jit(solution)/shard_map/all_to_all | solution.py:176
  200.7 1.3 copy.123
  202.0 16.4 %all-to-all-done.2 = bf16[2,128,2048]{2,0,1:T(2,128)(2,1)S(1)} async-done(((bf16[2,128,2048]{2,0,1:T(2,128)(2,1)}), bf16[2,128,2048]{2,0,1:T(2,128)(2,1)S(1)}, u32[]{:S(2)}, u32[]{:S(2)}) %all-to-all-start.2) | async-done | bytes 1048608 | tf_op jit(solution)/shard_map/all_to_all | solution.py:176
  218.4 0.3 copy.122
  218.8 1.0 fusion.59
  (40 shorter events, 2.0 us)
Async XLA Ops:
  7.2 105.9 %all-gather.2.cloned.1.call-start = ((), (), s32[]{:S(2)}) async-start(), calls=%async_computation.3 | async-start | bytes 28532736 | tf_op jit(solution)/shard_map/all_gather | solution.py:111
  13.3 20.9 %all-to-all-start = ((s32[128,1,2]{2,1,0:T(1,128)}), s32[128,1,2]{2,1,0:T(1,128)S(1)}, u32[]{:S(2)}, u32[]{:S(2)}) async-start(s32[128,1,2]{2,1,0:T(1,128)} %bitcast.15), calls=%async_computation | async-start | bytes 131072 | tf_op jit(solution)/shard_map/all_to_all | solution.py:148
  123.1 1.7 copy-start.9
  124.9 2.6 %copy-start.7 = (bf16[4,2048]{1,0:T(4,128)(2,1)}, bf16[4,2048]{1,0:T(4,128)(2,1)S(1)}, u32[]{:S(2)}) copy-start(bf16[4,2048]{1,0:T(4,128)(2,1)S(1)} %multiply_convert_fusion) | copy-start | bytes 49156
  125.4 9.3 %copy-start.5 = (bf16[1,128,4096]{2,1,0:T(8,128)(2,1)S(1)}, bf16[1,128,4096]{2,1,0:T(8,128)(2,1)}, u32[]{:S(2)}) copy-start(bf16[1,128,4096]{2,1,0:T(8,128)(2,1)} %param.21) | copy-start | bytes 3145732
  127.5 8.0 %copy-start.8 = (s32[1,128,1]{1,2,0:T(1,128)S(1)}, s32[1,128,1]{1,2,0:T(1,128)}, u32[]{:S(2)}) copy-start(s32[1,128,1]{1,2,0:T(1,128)} %param.19) | copy-start | bytes 1540
  127.5 25.1 %all-to-all-start.1 = ((bf16[2,128,2048]{2,0,1:T(2,128)(2,1)}), bf16[2,128,2048]{2,0,1:T(2,128)(2,1)S(1)}, u32[]{:S(2)}, u32[]{:S(2)}) async-start(bf16[2,128,2048]{2,0,1:T(2,128)(2,1)} %copy.102), calls=%async_computation.1 | async-start | bytes 2097152 | tf_op jit(solution)/shard_map/all_to_all | solution.py:150
  162.1 1.2 copy-start.6
  164.1 1.5 copy-start
  170.6 2.6 %copy-start.2 = (bf16[32,128,128]{1,2,0:T(8,128)(2,1)S(1)}, bf16[32,128,128]{1,2,0:T(8,128)(2,1)}, u32[]{:S(2)}) copy-start(bf16[32,128,128]{1,2,0:T(8,128)(2,1)} %fusion.40) | copy-start | bytes 3145732
  170.6 2.9 %copy-start.3 = (f32[32,128,128]{1,2,0:T(8,128)S(1)}, f32[32,128,128]{1,2,0:T(8,128)}, u32[]{:S(2)}) copy-start(f32[32,128,128]{1,2,0:T(8,128)} %get-tuple-element.30) | copy-start | bytes 6291460
  173.5 1.2 copy-start.4
  176.0 1.2 copy-start.1
  195.1 23.3 %all-to-all-start.2 = ((bf16[2,128,2048]{2,0,1:T(2,128)(2,1)}), bf16[2,128,2048]{2,0,1:T(2,128)(2,1)S(1)}, u32[]{:S(2)}, u32[]{:S(2)}) async-start(bf16[2,128,2048]{2,0,1:T(2,128)(2,1)} %copy.121), calls=%async_computation.2 | async-start | bytes 2097152 | tf_op jit(solution)/shard_map/all_to_all | solution.py:176
Sparse Core Ops, SparseCore 0:
  11.6 101.4 all-gather.1

commit v12 on v10

--- a/solution.py
+++ b/solution.py
@@ -146,7 +146,12 @@
     request = request.reshape(devices, cap_slots)
     width = item_embed.shape[1]
     incoming = lax.all_to_all(request, ("grp", "fsdp"), split_axis=0, concat_axis=0, tiled=True)
-    found = serve_rows(incoming, item_embed)
+    found = jnp.take(
+        jnp.concatenate([item_embed, jnp.zeros((1, item_embed.shape[1]), item_embed.dtype)], axis=0),
+        jnp.clip(incoming, 0, count),
+        axis=0,
+        mode="clip",
+    )
     returned = lax.all_to_all(found, ("grp", "fsdp"), split_axis=0, concat_axis=0, tiled=True)
     fetched = jnp.take(returned.reshape(devices * cap_slots, width), position, axis=0)
     hidden = stored(

time: 227 us -> 227 us (level)
    gather x0 -> x2, local copies, waits for them, and re-layouts: none -> 2.86 us  [per_device(): jnp.take(jnp.concatenate([item_embed, jnp.zeros((1, item_embed.shape[1]),...]
where the time goes in v12:
time: 227 us
  waiting for transfers between devices  117 us (52%)
  matrix products  42.3 us (19%)
  starting transfers between devices  24.3 us (11%)
  local copies, waits for them, and re-layouts  17 us (7%)
  between operations  14.4 us (6%)
  other arithmetic  10.2 us (4%)
    all_gather x1, waiting for transfers between devices, per_device(): lax.all_gather(pack_halves(sources), ('grp', 'fsdp'), axis=0, tiled=True)  77.3 us
    all_to_all x1, waiting for transfers between devices, per_device(): lax.all_to_all(outgoing.reshape(devices, cap_slots, DI), ('grp', 'fsdp'),...  16.4 us
    all_to_all x1, waiting for transfers between devices, per_device(): lax.all_to_all(found, ('grp', 'fsdp'), split_axis=0, concat_axis=0, tiled...  14.7 us
    dot_general x1, matrix products, per_device(): jnp.einsum('tgc,gdc->td', grad_hidden.reshape(grad_hidden.shape[0], group...  11.8 us
    all_to_all x1, starting transfers between devices, per_device(): lax.all_to_all(request, ('grp', 'fsdp'), split_axis=0, concat_axis=0, til...  11.5 us
    all_to_all x1, waiting for transfers between devices, per_device(): lax.all_to_all(request, ('grp', 'fsdp'), split_axis=0, concat_axis=0, til...  8.29 us
    dot_general x1, matrix products, per_device(): jnp.einsum('td,gdc->tgc', fetched, adapter_halves, preferred_element_type...  8.24 us
    all_to_all x1, starting transfers between devices, per_device(): lax.all_to_all(found, ('grp', 'fsdp'), split_axis=0, concat_axis=0, tiled...  7.26 us
  transfers between devices with their start and end apart: 4, of which 4 were waited for; matrix products, arithmetic and copies ran while one was open for 5% of the time, Pallas kernels for 0%

profile of v12, /device:TPU:1, one launch (start us, length us, event | category | flops | bytes accessed | tf_op | source)
XLA Modules:
  0.0 226.5 jit_solution(16478546288046833601)
XLA Ops:
  7.2 1.7 shard_map.130
  9.0 0.7 fusion.61
  9.9 0.8 select_reduce_fusion
  10.7 0.7 fusion.63
  11.4 1.1 scatter_custom_fusion
  12.5 0.8 all_to_all.12
  13.3 11.5 %all-to-all-start = ((s32[128,1,2]{2,1,0:T(1,128)}), s32[128,1,2]{2,1,0:T(1,128)S(1)}, u32[]{:S(2)}, u32[]{:S(2)}) async-start(s32[128,1,2]{2,1,0:T(1,128)} %bitcast.15), calls=%async_computation | async-start | bytes 131072 | tf_op jit(solution)/shard_map/all_to_all | solution.py:148
  24.8 1.0 slice.24
  25.8 8.3 %all-to-all-done = s32[128,1,2]{2,1,0:T(1,128)S(1)} async-done(((s32[128,1,2]{2,1,0:T(1,128)}), s32[128,1,2]{2,1,0:T(1,128)S(1)}, u32[]{:S(2)}, u32[]{:S(2)}) %all-to-all-start) | async-done | bytes 1056 | tf_op jit(solution)/shard_map/all_to_all | solution.py:148
  34.1 0.5 broadcast.165
  34.6 1.0 fusion.76
  35.8 77.3 %all-gather.2.cloned.1.call-done = bf16[4096,3456]{1,0:T(8,128)(2,1)} async-done(((bf16[32,3456]{1,0:T(8,128)(2,1)}), bf16[4096,3456]{1,0:T(8,128)(2,1)}) %all-gather.2.cloned.1.call-update) | async-done | bytes 28311568 | tf_op jit(solution)/shard_map/all_gather | solution.py:111
  113.1 4.6 %fusion.43 = bf16[2,1024,4]{1,2,0:T(4,128)(2,1)S(1)} fusion(bf16[2,2048,3456]{2,1,0:T(8,128)(2,1)} %bitcast.113, bf16[4,1,2048]{2,1,0:T(2,128)(2,1)S(1)} %slice.24), kind=kOutput, calls=%fused_computation.54 | convolution fusion | flops 33562624 | bytes 8421376 | tf_op jit(solution)/shard_map/id,gdc->igc/dot_general | solution.py:119
  117.8 5.3 %fusion.35 = bf16[1024,2,256]{0,2,1:T(8,128)(2,1)S(1)} fusion(bf16[1024,2048,1]{1,0,2:T(8,128)(2,1)} %bitcast.121, bf16[2,2048,3456]{2,1,0:T(8,128)(2,1)} %bitcast.114), kind=kOutput, calls=%fused_computation.47 | convolution fusion | flops 2148007936 | bytes 7340032 | tf_op jit(solution)/shard_map/td,gdc->tgc/dot_general | solution.py:114
  123.1 0.4 reshape.184
  124.9 1.4 gather_fusion
  126.3 1.5 reshape.196
  127.8 7.3 %all-to-all-start.1 = ((bf16[128,2,2048]{2,1,0:T(2,128)(2,1)}), bf16[128,2,2048]{2,1,0:T(2,128)(2,1)S(1)}, u32[]{:S(2)}, u32[]{:S(2)}) async-start(bf16[128,2,2048]{2,1,0:T(2,128)(2,1)} %reshape.196), calls=%async_computation.1 | async-start | bytes 2097152 | tf_op jit(solution)/shard_map/all_to_all | solution.py:155
  135.1 0.7 copy.57
  135.8 1.3 slice.40
  137.1 1.1 copy.51
  138.3 14.7 %all-to-all-done.1 = bf16[128,2,2048]{2,1,0:T(2,128)(2,1)S(1)} async-done(((bf16[128,2,2048]{2,1,0:T(2,128)(2,1)}), bf16[128,2,2048]{2,1,0:T(2,128)(2,1)S(1)}, u32[]{:S(2)}, u32[]{:S(2)}) %all-to-all-start.1) | async-done | bytes 1048608 | tf_op jit(solution)/shard_map/all_to_all | solution.py:155
  152.9 0.4 reshape.186
  153.3 0.9 gather_fusion.1
  154.3 8.2 %fusion.8 = bf16[128,2,2048]{2,0,1:T(8,128)(2,1)S(1)} fusion(bf16[2,2048,3456]{2,1,0:T(8,128)(2,1)} %bitcast.116, bf16[128,2048]{1,0:T(8,128)(2,1)S(1)} %gather_fusion.1, pred[128]{0:T(512)(128)(4,1)S(1)} %get-tuple-element.11), kind=kOutput, calls=%fused_computation.19 | convolution fusion | flops 2148270080 | bytes 18350208 | tf_op jit(solution)/shard_map/td,gdc->tgc/dot_general | solution.py:158
  162.5 0.7 copy.50
  163.2 0.6 fusion.24
  163.8 0.7 fusion.26
  164.5 1.5 fusion.39
  166.0 1.5 fusion.38
  167.5 3.5 %fusion.79 = (f32[32,128]{1,0:T(8,128)S(1)}, f32[32,128,128]{1,2,0:T(8,128)}) fusion(pred[128,128]{0,1:T(8,128)(4,1)S(1)} %iota_compare_fusion.4, bf16[128,32,128]{0,2,1:T(8,128)(2,1)} %fusion.38, bf16[128,32,128]{0,2,1:T(8,128)(2,1)S(1)} %bitcast.99), kind=kOutput, calls=%fused_computation.106 | convolution fusion | flops 136315008 | bytes 4227072 | tf_op jit(solution)/shard_map/jvp()/sub | solution.py:49
  171.0 2.6 %fusion.22 = (f32[32,128]{1,0:T(8,128)S(1)}, bf16[32,128,128]{1,2,0:T(8,128)(2,1)S(1)}) fusion(f32[32,128,128]{1,2,0:T(8,128)} %get-tuple-element.24, bf16[32,128,128]{1,2,0:T(8,128)(2,1)} %fusion.39, f32[32,128]{1,0:T(8,128)S(1)} %multiply_divide_fusion, f32[32,128]{1,0:T(8,128)S(1)} %get-tuple-element.23), kind=kLoop, calls=%fused_computation.28 | loop fusion | flops 3141632 | bytes 4243456 | tf_op jit(solution)/shard_map/transpose(jvp())/reduce_sum | solution.py:49
  173.9 0.8 fusion.40
  174.7 0.4 copy-done.4
  175.1 0.9 fusion.74
  176.0 0.5 fusion.82
  176.5 0.9 fusion.83
  177.7 0.8 add_convert_fusion
  178.5 0.9 fusion.28
  179.5 1.7 fusion.46
  181.2 11.8 %fusion.14 = bf16[128,2048]{1,0:T(8,128)(2,1)S(1)} fusion(bf16[128,2,2048]{0,2,1:T(8,128)(2,1)} %bitcast.112, bf16[2,2048,3456]{2,1,0:T(8,128)(2,1)} %bitcast.117), kind=kOutput, calls=%fused_computation.22 | convolution fusion | flops 2147745792 | bytes 18350080 | tf_op jit(solution)/shard_map/tgc,gdc->td/dot_general | solution.py:166
  193.0 0.4 convolution_convert_fusion
  193.4 1.5 reshape.192
  195.0 5.5 %all-to-all-start.2 = ((bf16[128,2,2048]{2,1,0:T(2,128)(2,1)}), bf16[128,2,2048]{2,1,0:T(2,128)(2,1)S(1)}, u32[]{:S(2)}, u32[]{:S(2)}) async-start(bf16[128,2,2048]{2,1,0:T(2,128)(2,1)} %reshape.192), calls=%async_computation.2 | async-start | bytes 2097152 | tf_op jit(solution)/shard_map/all_to_all | solution.py:178
  200.6 1.3 copy.66
  201.9 16.4 %all-to-all-done.2 = bf16[128,2,2048]{2,1,0:T(2,128)(2,1)S(1)} async-done(((bf16[128,2,2048]{2,1,0:T(2,128)(2,1)}), bf16[128,2,2048]{2,1,0:T(2,128)(2,1)S(1)}, u32[]{:S(2)}, u32[]{:S(2)}) %all-to-all-start.2) | async-done | bytes 1048608 | tf_op jit(solution)/shard_map/all_to_all | solution.py:178
  218.3 0.4 reshape.193
  218.7 1.0 fusion.58
  (44 shorter events, 2.9 us)
Async XLA Ops:
  7.2 105.9 %all-gather.2.cloned.1.call-start = ((), (), s32[]{:S(2)}) async-start(), calls=%async_computation.3 | async-start | bytes 28532736 | tf_op jit(solution)/shard_map/all_gather | solution.py:111
  13.3 20.9 %all-to-all-start = ((s32[128,1,2]{2,1,0:T(1,128)}), s32[128,1,2]{2,1,0:T(1,128)S(1)}, u32[]{:S(2)}, u32[]{:S(2)}) async-start(s32[128,1,2]{2,1,0:T(1,128)} %bitcast.15), calls=%async_computation | async-start | bytes 131072 | tf_op jit(solution)/shard_map/all_to_all | solution.py:148
  123.1 1.7 copy-start.8
  124.9 1.4 copy-start.7
  126.3 8.8 %copy-start.5 = (bf16[1,128,4096]{2,1,0:T(8,128)(2,1)S(1)}, bf16[1,128,4096]{2,1,0:T(8,128)(2,1)}, u32[]{:S(2)}) copy-start(bf16[1,128,4096]{2,1,0:T(8,128)(2,1)} %param.21) | copy-start | bytes 3145732
  127.8 8.0 %copy-start.9 = (s32[1,128,1]{1,2,0:T(1,128)S(1)}, s32[1,128,1]{1,2,0:T(1,128)}, u32[]{:S(2)}) copy-start(s32[1,128,1]{1,2,0:T(1,128)} %param.19) | copy-start | bytes 1540
  127.8 25.1 %all-to-all-start.1 = ((bf16[128,2,2048]{2,1,0:T(2,128)(2,1)}), bf16[128,2,2048]{2,1,0:T(2,128)(2,1)S(1)}, u32[]{:S(2)}, u32[]{:S(2)}) async-start(bf16[128,2,2048]{2,1,0:T(2,128)(2,1)} %reshape.196), calls=%async_computation.1 | async-start | bytes 2097152 | tf_op jit(solution)/shard_map/all_to_all | solution.py:155
  162.5 1.2 copy-start.6
  164.5 1.5 copy-start
  171.0 2.6 %copy-start.2 = (bf16[32,128,128]{1,2,0:T(8,128)(2,1)S(1)}, bf16[32,128,128]{1,2,0:T(8,128)(2,1)}, u32[]{:S(2)}) copy-start(bf16[32,128,128]{1,2,0:T(8,128)(2,1)} %fusion.39) | copy-start | bytes 3145732
  171.0 2.9 %copy-start.3 = (f32[32,128,128]{1,2,0:T(8,128)S(1)}, f32[32,128,128]{1,2,0:T(8,128)}, u32[]{:S(2)}) copy-start(f32[32,128,128]{1,2,0:T(8,128)} %get-tuple-element.24) | copy-start | bytes 6291460
  173.9 1.2 copy-start.4
  176.4 1.2 copy-start.1
  195.0 23.3 %all-to-all-start.2 = ((bf16[128,2,2048]{2,1,0:T(2,128)(2,1)}), bf16[128,2,2048]{2,1,0:T(2,128)(2,1)S(1)}, u32[]{:S(2)}, u32[]{:S(2)}) async-start(bf16[128,2,2048]{2,1,0:T(2,128)(2,1)} %reshape.192), calls=%async_computation.2 | async-start | bytes 2097152 | tf_op jit(solution)/shard_map/all_to_all | solution.py:178
Sparse Core Ops, SparseCore 0:
  11.6 101.4 all-gather.1

commit v13 on v10

--- a/solution.py
+++ b/solution.py
@@ -150,8 +150,9 @@
     returned = lax.all_to_all(found, ("grp", "fsdp"), split_axis=0, concat_axis=0, tiled=True)
     fetched = jnp.take(returned.reshape(devices * cap_slots, width), position, axis=0)
     hidden = stored(
-        jnp.einsum("td,gdc->tgc", fetched, adapter_halves, preferred_element_type=jnp.float32).reshape(
-            fetched.shape[0], -1
+        jnp.concatenate(
+            [jnp.dot(fetched, adapter_halves[g], preferred_element_type=jnp.float32) for g in range(groups)],
+            axis=1,
         )
     )
     user_attention_output, pull = jax.vjp(

time: 227 us -> 231 us (1.018)
    reshape x0 -> x2, local copies, waits for them, and re-layouts: none -> 4.22 us  [user_layer(): jnp.einsum('hts,shd->thd', weights, heads)]
    dot_general x1, matrix products: 11.8 us -> 9.49 us  [per_device(): jnp.einsum('tgc,gdc->td', grad_hidden.reshape(grad_hidden.shape[0], group...]
    dot_general x1 -> x2, matrix products: 8.24 us -> 9.46 us  [per_device(): jnp.dot(fetched, adapter_halves[g], preferred_element_type=jnp.float32)]
  transfers between devices with their start and end apart: 4 -> 4, of which waited for: 4 -> 4; matrix products, arithmetic and copies ran while one was open for 5% -> 4% of each run, Pallas kernels for 0% -> 0%
where the time goes in v13:
time: 231 us; the launch traced here: 230 us
  waiting for transfers between devices  119 us (52%)
  matrix products  43.4 us (19%)
  starting transfers between devices  24.3 us (11%)
  local copies, waits for them, and re-layouts  17.4 us (8%)
  between operations  14.4 us (6%)
  other arithmetic  10.6 us (5%)
    all_gather x1, waiting for transfers between devices, per_device(): lax.all_gather(pack_halves(sources), ('grp', 'fsdp'), axis=0, tiled=True)  78.9 us
    all_to_all x1, waiting for transfers between devices, per_device(): lax.all_to_all(outgoing.reshape(devices, cap_slots, DI), ('grp', 'fsdp'),...  16.4 us
    all_to_all x1, waiting for transfers between devices, per_device(): lax.all_to_all(found, ('grp', 'fsdp'), split_axis=0, concat_axis=0, tiled...  15 us
    all_to_all x1, starting transfers between devices, per_device(): lax.all_to_all(request, ('grp', 'fsdp'), split_axis=0, concat_axis=0, til...  11.5 us
    dot_general x1, matrix products, per_device(): jnp.einsum('tgc,gdc->td', grad_hidden.reshape(grad_hidden.shape[0], group...  9.49 us
    dot_general x2, matrix products, per_device(): jnp.dot(fetched, adapter_halves[g], preferred_element_type=jnp.float32)  9.46 us
    all_to_all x1, waiting for transfers between devices, per_device(): lax.all_to_all(request, ('grp', 'fsdp'), split_axis=0, concat_axis=0, til...  8.29 us
    all_to_all x1, starting transfers between devices, per_device(): lax.all_to_all(found, ('grp', 'fsdp'), split_axis=0, concat_axis=0, tiled...  7.27 us
  transfers between devices with their start and end apart: 4, of which 4 were waited for; matrix products, arithmetic and copies ran while one was open for 4% of the time, Pallas kernels for 0%

profile of v13, /device:TPU:1, one launch (start us, length us, event | category | flops | bytes accessed | tf_op | source)
XLA Modules:
  0.0 230.5 jit_solution(17737175516297476482)
XLA Ops:
  7.2 1.7 shard_map.130
  9.0 0.7 fusion.71
  9.9 0.8 select_reduce_fusion
  10.7 0.7 fusion.75
  11.4 1.1 scatter_custom_fusion
  12.5 0.8 all_to_all.12
  13.3 11.5 %all-to-all-start = ((s32[128,1,2]{2,1,0:T(1,128)}), s32[128,1,2]{2,1,0:T(1,128)S(1)}, u32[]{:S(2)}, u32[]{:S(2)}) async-start(s32[128,1,2]{2,1,0:T(1,128)} %bitcast.15), calls=%async_computation | async-start | bytes 131072 | tf_op jit(solution)/shard_map/all_to_all | solution.py:148
  24.8 1.0 slice.32
  25.8 8.3 %all-to-all-done = s32[128,1,2]{2,1,0:T(1,128)S(1)} async-done(((s32[128,1,2]{2,1,0:T(1,128)}), s32[128,1,2]{2,1,0:T(1,128)S(1)}, u32[]{:S(2)}, u32[]{:S(2)}) %all-to-all-start) | async-done | bytes 1056 | tf_op jit(solution)/shard_map/all_to_all | solution.py:148
  34.2 78.9 %all-gather.2.cloned.1.call-done = bf16[4096,3456]{1,0:T(8,128)(2,1)} async-done(((bf16[32,3456]{1,0:T(8,128)(2,1)}), bf16[4096,3456]{1,0:T(8,128)(2,1)}) %all-gather.2.cloned.1.call-update) | async-done | bytes 28311568 | tf_op jit(solution)/shard_map/all_gather | solution.py:111
  113.1 4.6 %fusion.42 = bf16[2,1024,4]{1,2,0:T(4,128)(2,1)S(1)} fusion(bf16[2,2048,3456]{2,1,0:T(8,128)(2,1)} %bitcast.145, bf16[4,1,2048]{2,1,0:T(2,128)(2,1)S(1)} %slice.32), kind=kOutput, calls=%fused_computation.57 | convolution fusion | flops 33562624 | bytes 8421376 | tf_op jit(solution)/shard_map/id,gdc->igc/dot_general | solution.py:119
  117.8 5.3 %fusion.34 = bf16[1024,2,256]{0,2,1:T(8,128)(2,1)S(1)} fusion(bf16[1024,2048,1]{1,0,2:T(8,128)(2,1)} %bitcast.154, bf16[2,2048,3456]{2,1,0:T(8,128)(2,1)} %bitcast.146), kind=kOutput, calls=%fused_computation.50 | convolution fusion | flops 2148007936 | bytes 7340032 | tf_op jit(solution)/shard_map/td,gdc->tgc/dot_general | solution.py:114
  123.2 0.4 reshape.170
  123.5 0.3 fusion.94
  124.0 0.4 reshape.171
  124.9 0.5 convolution_convert_fusion.1
  125.4 2.0 copy.53
  127.5 7.3 %all-to-all-start.1 = ((bf16[128,2,2048]{2,1,0:T(2,128)(2,1)}), bf16[128,2,2048]{2,1,0:T(2,128)(2,1)S(1)}, u32[]{:S(2)}, u32[]{:S(2)}) async-start(bf16[128,2,2048]{2,1,0:T(2,128)(2,1)} %copy.53), calls=%async_computation.1 | async-start | bytes 2097152 | tf_op jit(solution)/shard_map/all_to_all | solution.py:150
  134.8 1.3 copy.80
  136.1 1.3 slice.49
  137.6 15.0 %all-to-all-done.1 = bf16[128,2,2048]{2,1,0:T(2,128)(2,1)S(1)} async-done(((bf16[128,2,2048]{2,1,0:T(2,128)(2,1)}), bf16[128,2,2048]{2,1,0:T(2,128)(2,1)S(1)}, u32[]{:S(2)}, u32[]{:S(2)}) %all-to-all-start.1) | async-done | bytes 1048608 | tf_op jit(solution)/shard_map/all_to_all | solution.py:150
  152.6 0.4 reshape.173
  153.0 0.9 gather_fusion
  153.9 4.8 %fusion.12 = bf16[128,2048]{1,0:T(8,128)(2,1)S(1)} fusion(bf16[2,2048,3456]{2,1,0:T(8,128)(2,1)} %bitcast.148, bf16[128,2048]{1,0:T(8,128)(2,1)S(1)} %gather_fusion, pred[128]{0:T(512)(128)(4,1)S(1)} %get-tuple-element.3), kind=kOutput, calls=%fused_computation.24 | convolution fusion | flops 1074266112 | bytes 9437312 | tf_op jit(solution)/shard_map/dot_general | solution.py:154
  158.7 4.7 %fusion.11 = bf16[128,2048]{1,0:T(8,128)(2,1)S(1)} fusion(bf16[2,2048,3456]{2,1,0:T(8,128)(2,1)} %bitcast.149, bf16[128,2048]{1,0:T(8,128)(2,1)S(1)} %gather_fusion, pred[128]{0:T(512)(128)(4,1)S(1)} %get-tuple-element.3), kind=kOutput, calls=%fused_computation.23 | convolution fusion | flops 1074266112 | bytes 9437312 | tf_op jit(solution)/shard_map/dot_general | solution.py:154
  164.5 1.9 fusion.37
  166.3 1.4 fusion.38
  167.8 3.5 %fusion.95 = (f32[32,128]{1,0:T(8,128)S(1)}, f32[32,128,128]{1,2,0:T(8,128)}) fusion(pred[128,128]{0,1:T(8,128)(4,1)S(1)} %iota_compare_fusion.4, bf16[128,32,128]{0,2,1:T(8,128)(2,1)} %fusion.37, bf16[128,4096]{1,0:T(8,128)(2,1)S(1)} %fusion.25), kind=kOutput, calls=%fused_computation.122 | convolution fusion | flops 136315008 | bytes 4227072 | tf_op jit(solution)/shard_map/jvp()/sub | solution.py:49
  171.3 2.6 %fusion.21 = (f32[32,128]{1,0:T(8,128)S(1)}, bf16[32,128,128]{1,2,0:T(8,128)(2,1)S(1)}) fusion(f32[32,128,128]{1,2,0:T(8,128)} %get-tuple-element.16, bf16[32,128,128]{1,2,0:T(8,128)(2,1)} %fusion.38, f32[32,128]{1,0:T(8,128)S(1)} %multiply_divide_fusion, f32[32,128]{1,0:T(8,128)S(1)} %get-tuple-element.15), kind=kLoop, calls=%fused_computation.31 | loop fusion | flops 3141632 | bytes 4243456 | tf_op jit(solution)/shard_map/transpose(jvp())/reduce_sum | solution.py:49
  174.4 0.9 fusion.91
  175.3 0.8 fusion.39
  176.1 0.4 copy-done.1
  176.5 0.8 fusion.100
  177.3 2.0 fusion.54
  179.3 0.9 add_convert_fusion
  180.2 0.5 copy.81
  180.7 2.9 %copy.79 = f32[128,4096]{1,0:T(8,128)} copy(f32[128,4096]{0,1:T(8,128)} %bitcast.138) | data formatting | bytes 4194304 | tf_op jit(solution)/shard_map/jvp()/reshape | solution.py:50
  183.6 3.1 %fusion.27 = (f32[128]{0:T(128)S(1)}, bf16[1,128,4096]{2,1,0:T(8,128)(2,1)}) fusion(bf16[128,4096]{1,0:T(8,128)(2,1)S(1)} %pad_maximum_fusion, bf16[128,4096]{1,0:T(8,128)(2,1)S(1)} %copy.81, f32[4096]{0:T(1024)S(1)} %copy-done.7, f32[128,4096]{1,0:T(8,128)} %copy.79), kind=kLoop, calls=%fused_computation.37 | loop fusion | flops 3669888 | bytes 5259776 | tf_op jit(solution)/shard_map/transpose(jvp())/reduce_sum | solution.py:23
  186.7 0.7 fusion.46
  187.5 9.5 %fusion.13 = bf16[128,2048]{1,0:T(8,128)(2,1)S(1)} fusion(bf16[2,2048,3456]{2,1,0:T(8,128)(2,1)} %bitcast.150, bf16[16,2,8,2048]{3,2,1,0:T(8,128)(2,1)S(1)} %bitcast.143), kind=kOutput, calls=%fused_computation.25 | convolution fusion | flops 2147745792 | bytes 18350080 | tf_op jit(solution)/shard_map/tgc,gdc->td/dot_general | solution.py:162
  197.0 0.4 convolution_convert_fusion
  197.4 1.5 reshape.179
  198.9 5.5 %all-to-all-start.2 = ((bf16[128,2,2048]{2,1,0:T(2,128)(2,1)}), bf16[128,2,2048]{2,1,0:T(2,128)(2,1)S(1)}, u32[]{:S(2)}, u32[]{:S(2)}) async-start(bf16[128,2,2048]{2,1,0:T(2,128)(2,1)} %reshape.179), calls=%async_computation.2 | async-start | bytes 2097152 | tf_op jit(solution)/shard_map/all_to_all | solution.py:174
  204.4 0.5 broadcast.138
  204.9 0.8 reduce.4
  205.9 16.4 %all-to-all-done.2 = bf16[128,2,2048]{2,1,0:T(2,128)(2,1)S(1)} async-done(((bf16[128,2,2048]{2,1,0:T(2,128)(2,1)}), bf16[128,2,2048]{2,1,0:T(2,128)(2,1)S(1)}, u32[]{:S(2)}, u32[]{:S(2)}) %all-to-all-start.2) | async-done | bytes 1048608 | tf_op jit(solution)/shard_map/all_to_all | solution.py:174
  222.2 0.4 reshape.180
  222.7 1.0 fusion.68
  (46 shorter events, 3.1 us)
Async XLA Ops:
  7.2 105.9 %all-gather.2.cloned.1.call-start = ((), (), s32[]{:S(2)}) async-start(), calls=%async_computation.3 | async-start | bytes 28532736 | tf_op jit(solution)/shard_map/all_gather | solution.py:111
  13.3 20.9 %all-to-all-start = ((s32[128,1,2]{2,1,0:T(1,128)}), s32[128,1,2]{2,1,0:T(1,128)S(1)}, u32[]{:S(2)}, u32[]{:S(2)}) async-start(s32[128,1,2]{2,1,0:T(1,128)} %bitcast.15), calls=%async_computation | async-start | bytes 131072 | tf_op jit(solution)/shard_map/all_to_all | solution.py:148
  123.1 1.7 copy-start.9
  124.9 2.6 %copy-start.8 = (bf16[4,2048]{1,0:T(4,128)(2,1)}, bf16[4,2048]{1,0:T(4,128)(2,1)S(1)}, u32[]{:S(2)}) copy-start(bf16[4,2048]{1,0:T(4,128)(2,1)S(1)} %multiply_convert_fusion) | copy-start | bytes 49156
  125.4 9.3 %copy-start.2 = (bf16[1,128,4096]{2,1,0:T(8,128)(2,1)S(1)}, bf16[1,128,4096]{2,1,0:T(8,128)(2,1)}, u32[]{:S(2)}) copy-start(bf16[1,128,4096]{2,1,0:T(8,128)(2,1)} %param.21) | copy-start | bytes 3145732
  127.5 8.6 %copy-start.10 = (s32[1,128,1]{1,2,0:T(1,128)S(1)}, s32[1,128,1]{1,2,0:T(1,128)}, u32[]{:S(2)}) copy-start(s32[1,128,1]{1,2,0:T(1,128)} %param.19) | copy-start | bytes 1540
  127.5 25.1 %all-to-all-start.1 = ((bf16[128,2,2048]{2,1,0:T(2,128)(2,1)}), bf16[128,2,2048]{2,1,0:T(2,128)(2,1)S(1)}, u32[]{:S(2)}, u32[]{:S(2)}) async-start(bf16[128,2,2048]{2,1,0:T(2,128)(2,1)} %copy.53), calls=%async_computation.1 | async-start | bytes 2097152 | tf_op jit(solution)/shard_map/all_to_all | solution.py:150
  163.4 0.7 copy-start.7
  164.5 1.9 copy-start
  171.2 2.6 %copy-start.4 = (bf16[32,128,128]{1,2,0:T(8,128)(2,1)S(1)}, bf16[32,128,128]{1,2,0:T(8,128)(2,1)}, u32[]{:S(2)}) copy-start(bf16[32,128,128]{1,2,0:T(8,128)(2,1)} %fusion.38) | copy-start | bytes 3145732
  171.3 2.9 %copy-start.5 = (f32[32,128,128]{1,2,0:T(8,128)S(1)}, f32[32,128,128]{1,2,0:T(8,128)}, u32[]{:S(2)}) copy-start(f32[32,128,128]{1,2,0:T(8,128)} %get-tuple-element.16) | copy-start | bytes 6291460
  171.3 3.1 %copy-start.6 = (bf16[128,32,128]{0,2,1:T(8,128)(2,1)S(1)}, bf16[128,32,128]{0,2,1:T(8,128)(2,1)}, u32[]{:S(2)}) copy-start(bf16[128,32,128]{0,2,1:T(8,128)(2,1)} %fusion.37) | copy-start | bytes 3145732
  175.2 1.2 copy-start.1
  183.6 3.1 %copy-start.3 = (bf16[1,128,4096]{2,1,0:T(8,128)(2,1)S(1)}, bf16[1,128,4096]{2,1,0:T(8,128)(2,1)}, u32[]{:S(2)}) copy-start(bf16[1,128,4096]{2,1,0:T(8,128)(2,1)} %param.21) | copy-start | bytes 3145732
  198.9 23.3 %all-to-all-start.2 = ((bf16[128,2,2048]{2,1,0:T(2,128)(2,1)}), bf16[128,2,2048]{2,1,0:T(2,128)(2,1)S(1)}, u32[]{:S(2)}, u32[]{:S(2)}) async-start(bf16[128,2,2048]{2,1,0:T(2,128)(2,1)} %reshape.179), calls=%async_computation.2 | async-start | bytes 2097152 | tf_op jit(solution)/shard_map/all_to_all | solution.py:174
Sparse Core Ops, SparseCore 0:
  11.6 101.4 all-gather.1
